TPU v7x, 32 devices: a whole 2x2x4 slice. The times are simulated.
32 devices in a mesh: blk: 8 (over z, core), vb: 4 (over y, x).
Axes of the slice: x: 2, y: 2, z: 4, core: 2. Of those that a mesh axis runs over, the one named last changes fastest.
Arguments:
- amplitudes: float32 [32, 1024, 1024], P('blk', 'vb'), may hold values from -6 to 6
- integrals: float32 [2048, 1024], P('blk'), may hold values from -0.5 to 0.5
- row_orbitals: int32 [2048], P('blk'), may hold values from 0 to 1023
- pair_orbitals: int32 [32, 2], P('blk'), may hold values from 0 to 255
- occupied_energy: float32 [256], replicated, may hold values from -2 to -0.5
- virtual_energy: float32 [1024], replicated, may hold values from 0.5 to 3
Outputs:
- density: float32 [32, 1024, 1024], P('blk', 'vb')
All inputs are finite; a program needn't handle non-finite values.
Results may differ from a plain program's by a relative error of at most 0.0003.
Values sent between devices are 32-bit elements; how exact they have to be, the bound alone decides.
No kernel may reach another device: no remote copies, remote signals or barrier semaphores. Data moves between devices by JAX's collectives and lax.ppermute only.
A program may use at most 64 MiB of HBM per device.

v0:
```python
import jax
import jax.numpy as jnp
from jax import lax
from jax.sharding import PartitionSpec as P

HOPS = 5


def passed_along(block, axis, distance):
    devices = range(lax.axis_size(axis))
    route = [((i - distance) % len(devices), i) for i in devices]
    return lax.ppermute(block, axis, route)


def step_down(carried):
    return passed_along(carried, "blk", 1)


def local(amplitudes, integrals, row_orbitals, pair_orbitals, occupied_energy, virtual_energy):
    width = virtual_energy.shape[0]
    nocc = occupied_energy.shape[0]
    quarter = width // lax.axis_size("vb")
    qstart = lax.axis_index("vb") * quarter
    virt_iota = jnp.arange(width, dtype=jnp.int32)
    occ_iota = jnp.arange(nocc, dtype=jnp.int32)
    row_energy = jnp.sum(
        jnp.where(row_orbitals[:, None] == virt_iota[None, :], virtual_energy[None, :], 0.0), axis=1
    )
    pair_match = pair_orbitals[:, :, None] == occ_iota[None, None, :]
    pair_energy = jnp.sum(jnp.where(pair_match, occupied_energy[None, None, :], 0.0), axis=(1, 2))
    own_virtual = lax.dynamic_slice_in_dim(virtual_energy, qstart, quarter, 0)
    own = (integrals, row_energy)
    window = [own]
    current = passed_along((own[0], own[1]), "blk", -(HOPS - HOPS // 2))
    window = [current]
    for turn in range(HOPS):
        current = step_down(current)
        window.append(current)
    factors = lax.all_to_all(amplitudes, "vb", split_axis=2, concat_axis=1, tiled=True)

    def pair_columns(inputs):
        factor, energy = inputs
        total = jnp.zeros((width, quarter), jnp.float32)
        for block, energies in window:
            denom = energies[:, None] + own_virtual[None, :] - energy
            weighted = jnp.dot(
                block, factor, precision=lax.Precision.HIGHEST, preferred_element_type=jnp.float32
            )
            total = total + jnp.dot(
                block.T,
                weighted / denom,
                precision=lax.Precision.HIGHEST,
                preferred_element_type=jnp.float32,
            )
        return total

    totals = lax.map(pair_columns, (factors, pair_energy))
    return lax.all_to_all(totals, "vb", split_axis=1, concat_axis=2, tiled=True)


def solution(mesh):
    return jax.shard_map(
        local,
        mesh=mesh,
        in_specs=(P("blk", "vb", None), P("blk", None), P("blk"), P("blk", None), P(), P()),
        out_specs=P("blk", "vb", None),
        check_vma=False,
    )
```

profile of v0, /device:TPU:0, one launch (start us, length us, event | category | flops | bytes accessed | tf_op | source)
XLA Modules:
  0.0 425.2 jit_solution(7205439664500854542)
XLA Ops:
  0.0 3.5 collective-permute-start
  3.5 22.9 %collective-permute-done = f32[256,1024]{1,0:T(8,128)S(1)} collective-permute-done((f32[256,1024]{1,0:T(8,128)}, f32[256,1024]{1,0:T(8,128)S(1)}, u32[]{:S(2)}, u32[]{:S(2)}) %collective-permute-start) | collective-permute-done | bytes 1048608 | tf_op jit(solution)/shard_map/ppermute | solution.py:12
  26.4 12.8 %collective-permute-start.2 = (f32[256,1024]{1,0:T(8,128)S(1)}, f32[256,1024]{1,0:T(8,128)S(1)}, u32[]{:S(2)}, u32[]{:S(2)}) collective-permute-start(f32[256,1024]{1,0:T(8,128)S(1)} %collective-permute-done), channel_id=1, source_target_pairs={{28,0},{0,4},{4,8},{8,12},{12,16},{16,20},{20,24},{24,28},{29,1},{... | collective-permute-start | bytes 3145736 | tf_op jit(solution)/shard_map/ppermute | solution.py:12
  39.2 15.6 %collective-permute-done.2 = f32[256,1024]{1,0:T(8,128)S(1)} collective-permute-done((f32[256,1024]{1,0:T(8,128)S(1)}, f32[256,1024]{1,0:T(8,128)S(1)}, u32[]{:S(2)}, u32[]{:S(2)}) %collective-permute-start.2) | collective-permute-done | bytes 1048608 | tf_op jit(solution)/shard_map/ppermute | solution.py:12
  54.8 5.3 %copy.15 = f32[4,256,1024]{1,0,2:T(4,128)} copy(f32[4,256,1024]{2,1,0:T(8,128)} %param.8) | data formatting | bytes 8388608 | tf_op args[0]
  60.1 5.0 %all-to-all-start = ((f32[4,256,1024]{1,0,2:T(4,128)}), f32[4,256,1024]{1,0,2:T(4,128)}, u32[]{:S(2)}, u32[]{:S(2)}) async-start(f32[4,256,1024]{1,0,2:T(4,128)} %copy.15), calls=%async_computation | async-start | bytes 8388608 | tf_op jit(solution)/shard_map/all_to_all | solution.py:39
  65.1 5.7 %collective-permute-done.4 = f32[256,1024]{1,0:T(8,128)S(1)} collective-permute-done((f32[256,1024]{1,0:T(8,128)S(1)}, f32[256,1024]{1,0:T(8,128)S(1)}, u32[]{:S(2)}, u32[]{:S(2)}) %collective-permute-start.4) | collective-permute-done | bytes 1048608 | tf_op jit(solution)/shard_map/ppermute | solution.py:12
  70.8 16.0 %collective-permute-done.6 = f32[256,1024]{1,0:T(8,128)S(1)} collective-permute-done((f32[256,1024]{1,0:T(8,128)S(1)}, f32[256,1024]{1,0:T(8,128)S(1)}, u32[]{:S(2)}, u32[]{:S(2)}) %collective-permute-start.6) | collective-permute-done | bytes 1048608 | tf_op jit(solution)/shard_map/ppermute | solution.py:12
  86.8 1.1 copy-done.1
  87.9 16.1 %collective-permute-done.8 = f32[256,1024]{1,0:T(8,128)} collective-permute-done((f32[256,1024]{1,0:T(8,128)S(1)}, f32[256,1024]{1,0:T(8,128)}, u32[]{:S(2)}, u32[]{:S(2)}) %collective-permute-start.8) | collective-permute-done | bytes 1048608 | tf_op jit(solution)/shard_map/ppermute | solution.py:12
  104.4 3.0 collective-permute-done.1
  107.4 3.0 collective-permute-start.3
  110.3 10.6 %collective-permute-done.3 = f32[256]{0:T(256)S(1)} collective-permute-done((f32[256]{0:T(256)S(1)}, f32[256]{0:T(256)S(1)}, u32[]{:S(2)}, u32[]{:S(2)}) %collective-permute-start.3) | collective-permute-done | bytes 1056 | tf_op jit(solution)/shard_map/ppermute | solution.py:12
  120.9 4.8 %collective-permute-done.5 = f32[256]{0:T(256)S(1)} collective-permute-done((f32[256]{0:T(256)S(1)}, f32[256]{0:T(256)S(1)}, u32[]{:S(2)}, u32[]{:S(2)}) %collective-permute-start.5) | collective-permute-done | bytes 1056 | tf_op jit(solution)/shard_map/ppermute | solution.py:12
  125.7 4.8 %collective-permute-done.7 = f32[256]{0:T(256)S(1)} collective-permute-done((f32[256]{0:T(256)S(1)}, f32[256]{0:T(256)S(1)}, u32[]{:S(2)}, u32[]{:S(2)}) %collective-permute-start.7) | collective-permute-done | bytes 1056 | tf_op jit(solution)/shard_map/ppermute | solution.py:12
  130.5 4.8 %collective-permute-done.9 = f32[256]{0:T(256)S(1)} collective-permute-done((f32[256]{0:T(256)S(1)}, f32[256]{0:T(256)S(1)}, u32[]{:S(2)}, u32[]{:S(2)}) %collective-permute-start.9) | collective-permute-done | bytes 1056 | tf_op jit(solution)/shard_map/ppermute | solution.py:12
  135.6 5.2 %copy.16 = f32[4,4,256,256]{3,2,1,0:T(8,128)} copy(f32[4,4,256,256]{2,0,3,1:T(4,128)} %bitcast.11) | data formatting | bytes 8388608 | tf_op jit(solution)/shard_map/all_to_all | solution.py:39
  140.8 225.5 %while.10 = (s32[]{:T(128)}, f32[4,1024,256]{2,0,1:T(4,128)}, f32[4,1024,256]{2,1,0:T(8,128)}, f32[256,1024]{1,0:T(8,128)S(1)}, f32[256]{0:T(256)S(1)}, /*index=...) while((s32[]{:T(128)}, f32[4,1024,256]{2,0,1:T(4,128)}, ...), condition=%wide.region_3.4_spmd, body=%wide.region_2.3_spmd.sunk | while | flops 9666166784 | bytes 58733852 | solution.py:57
  141.7 4.1 fusion.100
  146.8 2.5 fusion.102
  149.4 1.0 convolution_add_fusion.9
  150.4 2.5 fusion.103
  154.0 2.5 fusion.104
  157.5 3.7 fusion.105
  161.3 2.3 convolution_add_fusion.12
  163.5 3.7 fusion.106
  167.3 3.2 fusion.107
  170.5 3.6 copy.24
  174.1 23.2 %dynamic_update_slice.5 = f32[4,1024,256]{2,0,1:T(4,128)} dynamic-update-slice(f32[4,1024,256]{2,0,1:T(4,128)} %get-tuple-element.250, f32[1,1024,256]{2,0,1:T(1,128)} %copy.24, s32[]{:T(128)} %get-tuple-element.249, s32[]{:T(128)} %constant.3.clone.1..sunk, s32[]{:T(128)} %constant.3.clone.1..sunk) | dynamic-update-slice | bytes 2097156 | tf_op jit(solution)/shard_map/while/body/jit(dynamic_update_index_in_dim)/dynamic_update_slice | solution.py:57
  198.0 4.1 fusion.100
  203.2 2.5 fusion.102
  206.7 2.5 fusion.103
  210.3 2.5 fusion.104
  213.9 3.7 fusion.105
  217.6 2.3 convolution_add_fusion.12
  219.9 3.7 fusion.106
  223.6 3.2 fusion.107
  226.8 3.6 copy.24
  230.5 23.2 %dynamic_update_slice.5 = f32[4,1024,256]{2,0,1:T(4,128)} dynamic-update-slice(f32[4,1024,256]{2,0,1:T(4,128)} %get-tuple-element.250, f32[1,1024,256]{2,0,1:T(1,128)} %copy.24, s32[]{:T(128)} %get-tuple-element.249, s32[]{:T(128)} %constant.3.clone.1..sunk, s32[]{:T(128)} %constant.3.clone.1..sunk) | dynamic-update-slice | bytes 2097156 | tf_op jit(solution)/shard_map/while/body/jit(dynamic_update_index_in_dim)/dynamic_update_slice | solution.py:57
  254.4 4.1 fusion.100
  259.5 2.5 fusion.102
  262.0 1.0 convolution_add_fusion.9
  263.1 2.5 fusion.103
  266.6 2.5 fusion.104
  270.2 3.7 fusion.105
  273.9 2.3 convolution_add_fusion.12
  276.2 3.7 fusion.106
  279.9 3.2 fusion.107
  283.2 3.6 copy.24
  286.8 23.2 %dynamic_update_slice.5 = f32[4,1024,256]{2,0,1:T(4,128)} dynamic-update-slice(f32[4,1024,256]{2,0,1:T(4,128)} %get-tuple-element.250, f32[1,1024,256]{2,0,1:T(1,128)} %copy.24, s32[]{:T(128)} %get-tuple-element.249, s32[]{:T(128)} %constant.3.clone.1..sunk, s32[]{:T(128)} %constant.3.clone.1..sunk) | dynamic-update-slice | bytes 2097156 | tf_op jit(solution)/shard_map/while/body/jit(dynamic_update_index_in_dim)/dynamic_update_slice | solution.py:57
  310.7 4.1 fusion.100
  315.8 2.5 fusion.102
  318.4 1.0 convolution_add_fusion.9
  319.4 2.5 fusion.103
  323.0 2.5 fusion.104
  326.5 3.7 fusion.105
  330.3 2.3 convolution_add_fusion.12
  332.5 3.7 fusion.106
  336.3 3.2 fusion.107
  339.5 3.6 copy.24
  343.1 23.2 %dynamic_update_slice.5 = f32[4,1024,256]{2,0,1:T(4,128)} dynamic-update-slice(f32[4,1024,256]{2,0,1:T(4,128)} %get-tuple-element.250, f32[1,1024,256]{2,0,1:T(1,128)} %copy.24, s32[]{:T(128)} %get-tuple-element.249, s32[]{:T(128)} %constant.3.clone.1..sunk, s32[]{:T(128)} %constant.3.clone.1..sunk) | dynamic-update-slice | bytes 2097156 | tf_op jit(solution)/shard_map/while/body/jit(dynamic_update_index_in_dim)/dynamic_update_slice | solution.py:57
  366.4 48.4 %all_to_all.36 = f32[4,1024,256]{2,0,1:T(4,128)S(1)} all-to-all(f32[4,1024,256]{2,0,1:T(4,128)} %get-tuple-element.92), channel_id=1, replica_groups=mesh['blk'=8,'vb'=4] {'vb'}, dimensions={1} | all-to-all | bytes 8388608 | tf_op jit(solution)/shard_map/all_to_all | solution.py:58
  414.8 4.7 %copy.18 = f32[4,256,4,256]{3,2,1,0:T(4,128)} copy(f32[4,256,4,256]{3,0,1,2:T(4,128)S(1)} %bitcast.132) | data formatting | bytes 8388608 | tf_op jit(solution)/shard_map/all_to_all | solution.py:58
  419.5 5.8 %all_to_all.33 = f32[4,256,1024]{2,1,0:T(8,128)} reshape(f32[4,256,4,256]{3,2,1,0:T(4,128)} %copy.18) | data formatting | bytes 8388608 | tf_op jit(solution)/shard_map/all_to_all | solution.py:58
  (58 shorter events, 16.7 us)
Async XLA Ops:
  0.0 26.4 %collective-permute-start = (f32[256,1024]{1,0:T(8,128)}, f32[256,1024]{1,0:T(8,128)S(1)}, u32[]{:S(2)}, u32[]{:S(2)}) collective-permute-start(f32[256,1024]{1,0:T(8,128)} %param.9), channel_id=1, source_target_pairs={{12,0},{16,4},{20,8},{24,12},{28,16},{0,20},{4,24},{8,28},{13,1},{... | collective-permute-start | bytes 3145736 | tf_op jit(solution)/shard_map/ppermute | solution.py:12
  26.4 28.4 %collective-permute-start.2 = (f32[256,1024]{1,0:T(8,128)S(1)}, f32[256,1024]{1,0:T(8,128)S(1)}, u32[]{:S(2)}, u32[]{:S(2)}) collective-permute-start(f32[256,1024]{1,0:T(8,128)S(1)} %collective-permute-done), channel_id=1, source_target_pairs={{28,0},{0,4},{4,8},{8,12},{12,16},{16,20},{20,24},{24,28},{29,1},{... | collective-permute-start | bytes 3145736 | tf_op jit(solution)/shard_map/ppermute | solution.py:12
  54.8 16.0 %collective-permute-start.4 = (f32[256,1024]{1,0:T(8,128)S(1)}, f32[256,1024]{1,0:T(8,128)S(1)}, u32[]{:S(2)}, u32[]{:S(2)}) collective-permute-start(f32[256,1024]{1,0:T(8,128)S(1)} %collective-permute-done.2), channel_id=1, source_target_pairs={{28,0},{0,4},{4,8},{8,12},{12,16},{16,20},{20,24},{24,28},{29,1},{... | collective-permute-start | bytes 3145736 | tf_op jit(solution)/shard_map/ppermute | solution.py:12
  60.1 44.0 %copy-start.3 = (f32[1024]{0:T(1024)S(1)}, f32[1024]{0:T(1024)}, u32[]{:S(2)}) copy-start(f32[1024]{0:T(1024)} %param.13) | copy-start | bytes 12292
  60.1 44.0 %copy-start.6 = (s32[256]{0:T(256)S(1)}, s32[256]{0:T(256)}, u32[]{:S(2)}) copy-start(s32[256]{0:T(256)} %param.10) | copy-start | bytes 3076
  60.1 75.2 %copy-start.4 = (f32[256]{0:T(256)S(1)}, f32[256]{0:T(256)}, u32[]{:S(2)}) copy-start(f32[256]{0:T(256)} %param.12) | copy-start | bytes 3076
  60.1 75.2 %copy-start.5 = (s32[4,2]{0,1:T(2,128)S(1)}, s32[4,2]{0,1:T(2,128)}, u32[]{:S(2)}) copy-start(s32[4,2]{0,1:T(2,128)} %param.11) | copy-start | bytes 100
  60.1 75.5 %all-to-all-start = ((f32[4,256,1024]{1,0,2:T(4,128)}), f32[4,256,1024]{1,0,2:T(4,128)}, u32[]{:S(2)}, u32[]{:S(2)}) async-start(f32[4,256,1024]{1,0,2:T(4,128)} %copy.15), calls=%async_computation | async-start | bytes 8388608 | tf_op jit(solution)/shard_map/all_to_all | solution.py:39
  70.8 16.0 %collective-permute-start.6 = (f32[256,1024]{1,0:T(8,128)S(1)}, f32[256,1024]{1,0:T(8,128)S(1)}, u32[]{:S(2)}, u32[]{:S(2)}) collective-permute-start(f32[256,1024]{1,0:T(8,128)S(1)} %collective-permute-done.4), channel_id=1, source_target_pairs={{28,0},{0,4},{4,8},{8,12},{12,16},{16,20},{20,24},{24,28},{29,1},{... | collective-permute-start | bytes 3145736 | tf_op jit(solution)/shard_map/ppermute | solution.py:12
  86.8 1.1 copy-start.1
  87.9 16.1 %collective-permute-start.8 = (f32[256,1024]{1,0:T(8,128)S(1)}, f32[256,1024]{1,0:T(8,128)}, u32[]{:S(2)}, u32[]{:S(2)}) collective-permute-start(f32[256,1024]{1,0:T(8,128)S(1)} %collective-permute-done.6), channel_id=1, source_target_pairs={{28,0},{0,4},{4,8},{8,12},{12,16},{16,20},{20,24},{24,28},{29,1},{... | collective-permute-start | bytes 3145736 | tf_op jit(solution)/shard_map/ppermute | solution.py:12
  104.0 36.8 %collective-permute-start.10 = (f32[256,1024]{1,0:T(8,128)}, f32[256,1024]{1,0:T(8,128)}, u32[]{:S(2)}, u32[]{:S(2)}) collective-permute-start(f32[256,1024]{1,0:T(8,128)} %collective-permute-done.8), channel_id=1, source_target_pairs={{28,0},{0,4},{4,8},{8,12},{12,16},{16,20},{20,24},{24,28},{29,1},{... | collective-permute-start | bytes 3145736 | tf_op jit(solution)/shard_map/ppermute | solution.py:12
  104.3 3.1 collective-permute-start.1
  107.4 13.5 %collective-permute-start.3 = (f32[256]{0:T(256)S(1)}, f32[256]{0:T(256)S(1)}, u32[]{:S(2)}, u32[]{:S(2)}) collective-permute-start(f32[256]{0:T(256)S(1)} %collective-permute-done.1), channel_id=1, source_target_pairs={{28,0},{0,4},{4,8},{8,12},{12,16},{16,20},{20,24},{24,28},{29,1},{... | collective-permute-start | bytes 3080 | tf_op jit(solution)/shard_map/ppermute | solution.py:12
  120.9 4.8 %collective-permute-start.5 = (f32[256]{0:T(256)S(1)}, f32[256]{0:T(256)S(1)}, u32[]{:S(2)}, u32[]{:S(2)}) collective-permute-start(f32[256]{0:T(256)S(1)} %collective-permute-done.3), channel_id=1, source_target_pairs={{28,0},{0,4},{4,8},{8,12},{12,16},{16,20},{20,24},{24,28},{29,1},{... | collective-permute-start | bytes 3080 | tf_op jit(solution)/shard_map/ppermute | solution.py:12
  125.7 4.8 %collective-permute-start.7 = (f32[256]{0:T(256)S(1)}, f32[256]{0:T(256)S(1)}, u32[]{:S(2)}, u32[]{:S(2)}) collective-permute-start(f32[256]{0:T(256)S(1)} %collective-permute-done.5), channel_id=1, source_target_pairs={{28,0},{0,4},{4,8},{8,12},{12,16},{16,20},{20,24},{24,28},{29,1},{... | collective-permute-start | bytes 3080 | tf_op jit(solution)/shard_map/ppermute | solution.py:12
  130.5 4.8 %collective-permute-start.9 = (f32[256]{0:T(256)S(1)}, f32[256]{0:T(256)S(1)}, u32[]{:S(2)}, u32[]{:S(2)}) collective-permute-start(f32[256]{0:T(256)S(1)} %collective-permute-done.7), channel_id=1, source_target_pairs={{28,0},{0,4},{4,8},{8,12},{12,16},{16,20},{20,24},{24,28},{29,1},{... | collective-permute-start | bytes 3080 | tf_op jit(solution)/shard_map/ppermute | solution.py:12
  135.3 5.5 %collective-permute-start.11 = (f32[256]{0:T(256)S(1)}, f32[256]{0:T(256)S(1)}, u32[]{:S(2)}, u32[]{:S(2)}) collective-permute-start(f32[256]{0:T(256)S(1)} %collective-permute-done.9), channel_id=1, source_target_pairs={{28,0},{0,4},{4,8},{8,12},{12,16},{16,20},{20,24},{24,28},{29,1},{... | collective-permute-start | bytes 3080 | tf_op jit(solution)/shard_map/ppermute | solution.py:12
  141.0 5.8 %copy-start = (f32[4,1024,256]{2,1,0:T(8,128)S(1)}, f32[4,1024,256]{2,1,0:T(8,128)}, u32[]{:S(2)}) copy-start(f32[4,1024,256]{2,1,0:T(8,128)} %get-tuple-element.270) | copy-start | bytes 12582916 | tf_op jit(solution)/shard_map/while
  149.3 4.6 %copy-start.2 = (f32[256,1024]{1,0:T(8,128)S(1)}, f32[256,1024]{1,0:T(8,128)}, u32[]{:S(2)}) copy-start(f32[256,1024]{1,0:T(8,128)} %get-tuple-element.279) | copy-start | bytes 3145732 | tf_op jit(solution)/shard_map/while
  197.4 5.8 %copy-start = (f32[4,1024,256]{2,1,0:T(8,128)S(1)}, f32[4,1024,256]{2,1,0:T(8,128)}, u32[]{:S(2)}) copy-start(f32[4,1024,256]{2,1,0:T(8,128)} %get-tuple-element.270) | copy-start | bytes 12582916 | tf_op jit(solution)/shard_map/while
  205.7 4.6 %copy-start.2 = (f32[256,1024]{1,0:T(8,128)S(1)}, f32[256,1024]{1,0:T(8,128)}, u32[]{:S(2)}) copy-start(f32[256,1024]{1,0:T(8,128)} %get-tuple-element.279) | copy-start | bytes 3145732 | tf_op jit(solution)/shard_map/while
  253.7 5.8 %copy-start = (f32[4,1024,256]{2,1,0:T(8,128)S(1)}, f32[4,1024,256]{2,1,0:T(8,128)}, u32[]{:S(2)}) copy-start(f32[4,1024,256]{2,1,0:T(8,128)} %get-tuple-element.270) | copy-start | bytes 12582916 | tf_op jit(solution)/shard_map/while
  262.0 4.6 %copy-start.2 = (f32[256,1024]{1,0:T(8,128)S(1)}, f32[256,1024]{1,0:T(8,128)}, u32[]{:S(2)}) copy-start(f32[256,1024]{1,0:T(8,128)} %get-tuple-element.279) | copy-start | bytes 3145732 | tf_op jit(solution)/shard_map/while
  310.1 5.8 %copy-start = (f32[4,1024,256]{2,1,0:T(8,128)S(1)}, f32[4,1024,256]{2,1,0:T(8,128)}, u32[]{:S(2)}) copy-start(f32[4,1024,256]{2,1,0:T(8,128)} %get-tuple-element.270) | copy-start | bytes 12582916 | tf_op jit(solution)/shard_map/while
  318.4 4.6 %copy-start.2 = (f32[256,1024]{1,0:T(8,128)S(1)}, f32[256,1024]{1,0:T(8,128)}, u32[]{:S(2)}) copy-start(f32[256,1024]{1,0:T(8,128)} %get-tuple-element.279) | copy-start | bytes 3145732 | tf_op jit(solution)/shard_map/while
where the time goes:
time: 429 us; the launch traced here: 425 us
  local copies, waits for them, and re-layouts  132 us (31%)
  matrix products  115 us (27%)
  waiting for transfers between devices  104 us (24%)
  blocking collectives  48.4 us (11%)
  starting transfers between devices  24.3 us (6%)
    dynamic_update_slice x8, local copies, waits for them, and re-layouts, local(): totals = lax.map(pair_columns, (factors, pair_energy))  107 us
    ppermute x12, waiting for transfers between devices, passed_along(): return lax.ppermute(block, axis, route)  104 us
    dot_general x24, matrix products, pair_columns(): jnp.dot(block, factor, precision=lax.Precision.HIGHEST, preferred_element...  76.2 us
    all_to_all x1, blocking collectives, local(): return lax.all_to_all(totals, 'vb', split_axis=1, concat_axis=2, tiled=True)  48.4 us
    dot_general x24, matrix products, pair_columns(): jnp.dot(block.T, weighted / denom, precision=lax.Precision.HIGHEST, prefe...  38.5 us
    ppermute x12, starting transfers between devices, passed_along(): return lax.ppermute(block, axis, route)  19.3 us
    all_to_all x2, local copies, waits for them, and re-layouts, local(): return lax.all_to_all(totals, 'vb', split_axis=1, concat_axis=2, tiled=True)  10.4 us
  transfers between devices with their start and end apart: 13, of which 10 were waited for; matrix products, arithmetic and copies ran while one was open for 3% of the time, Pallas kernels for 0%

commit v1 on v0

v1 whole, which is shorter than its diff:
```python
import jax
import jax.numpy as jnp
from jax import lax
from jax.sharding import PartitionSpec as P

HOPS = 5
PREC = lax.Precision.HIGH


def fetch(block, axis, offset):
    n = lax.axis_size(axis)
    route = [((i + offset) % n, i) for i in range(n)]
    return lax.ppermute(block, axis, route)


def local(amplitudes, integrals, row_orbitals, pair_orbitals, occupied_energy, virtual_energy):
    width = virtual_energy.shape[0]
    quarter = width // lax.axis_size("vb")
    qstart = lax.axis_index("vb") * quarter
    row_energy = jnp.take(virtual_energy, row_orbitals, axis=0)
    pair_energy = (
        jnp.take(occupied_energy, pair_orbitals[:, 0], axis=0)
        + jnp.take(occupied_energy, pair_orbitals[:, 1], axis=0)
    )
    own_virtual = lax.dynamic_slice_in_dim(virtual_energy, qstart, quarter, 0)

    low = -(HOPS // 2)
    high = HOPS - HOPS // 2
    offsets = [0] + [o for k in range(1, high + 1) for o in (-k, k) if low <= o <= high and o != 0]
    window = []
    for o in offsets:
        if o == 0:
            window.append((integrals, row_energy))
        else:
            window.append((fetch(integrals, "blk", o), fetch(row_energy, "blk", o)))

    factors = lax.all_to_all(amplitudes, "vb", split_axis=2, concat_axis=1, tiled=True)

    total = None
    for block, energies in window:
        weighted = jnp.einsum(
            "rb,pba->rpa", block, factors, precision=PREC, preferred_element_type=jnp.float32
        )
        denom = (energies[:, None] + own_virtual[None, :])[:, None, :] - pair_energy[None, :, None]
        scaled = weighted / denom
        part = jnp.einsum(
            "rc,rpa->pca", block, scaled, precision=PREC, preferred_element_type=jnp.float32
        )
        total = part if total is None else total + part
    return lax.all_to_all(total, "vb", split_axis=1, concat_axis=2, tiled=True)


def solution(mesh):
    return jax.shard_map(
        local,
        mesh=mesh,
        in_specs=(P("blk", "vb", None), P("blk", None), P("blk"), P("blk", None), P(), P()),
        out_specs=P("blk", "vb", None),
        check_vma=False,
    )
```

time: 429 us -> 208 us (0.48)
  the two profiles are of different devices: /device:TPU:0 before, /device:TPU:8 now
where the time goes in v1:
time: 208 us; the launch traced here: 207 us
  waiting for transfers between devices  64.6 us (31%)
  blocking collectives  51.5 us (25%)
  matrix products  38.3 us (18%)
  local copies, waits for them, and re-layouts  34.1 us (16%)
  starting transfers between devices  16.9 us (8%)
    all_to_all x1, blocking collectives, local(): return lax.all_to_all(total, 'vb', split_axis=1, concat_axis=2, tiled=True)  51.5 us
    ppermute x10, waiting for transfers between devices, fetch(): return lax.ppermute(block, axis, route)  33.1 us
    all_to_all x1, waiting for transfers between devices, local(): lax.all_to_all(amplitudes, 'vb', split_axis=2, concat_axis=1, tiled=True)  31.5 us
    dot_general x6, matrix products, local(): jnp.einsum('rb,pba->rpa', block, factors, precision=PREC, preferred_eleme...  19.7 us
    dot_general x6, matrix products, local(): jnp.einsum('rc,rpa->pca', block, scaled, precision=PREC, preferred_elemen...  18.7 us
    ppermute x10, starting transfers between devices, fetch(): return lax.ppermute(block, axis, route)  11.9 us
    all_to_all x2, local copies, waits for them, and re-layouts, local(): return lax.all_to_all(total, 'vb', split_axis=1, concat_axis=2, tiled=True)  10.4 us
    all_to_all x2, local copies, waits for them, and re-layouts, local(): lax.all_to_all(amplitudes, 'vb', split_axis=2, concat_axis=1, tiled=True)  10.2 us
  transfers between devices with their start and end apart: 11, of which 2 were waited for; matrix products, arithmetic and copies ran while one was open for 21% of the time, Pallas kernels for 0%

profile of v1, /device:TPU:8, one launch (start us, length us, event | category | flops | bytes accessed | tf_op | source)
XLA Modules:
  0.0 207.1 jit_solution(16664658198773020466)
XLA Ops:
  0.0 0.0 copy-start
  0.0 5.2 %copy.18 = f32[4,256,1024]{1,0,2:T(4,128)} copy(f32[4,256,1024]{2,1,0:T(8,128)} %param.8) | data formatting | bytes 8388608 | tf_op args[0]
  5.2 0.0 copy-start.9
  5.3 5.0 %all-to-all-start = ((f32[4,256,1024]{1,0,2:T(4,128)}), f32[4,256,1024]{1,0,2:T(4,128)}, u32[]{:S(2)}, u32[]{:S(2)}) async-start(f32[4,256,1024]{1,0,2:T(4,128)} %copy.18), calls=%async_computation | async-start | bytes 8388608 | tf_op jit(solution)/shard_map/all_to_all | solution.py:37
  10.3 0.0 copy-done.9
  10.3 0.0 copy-done.2
  10.3 1.4 gather_fusion
  11.7 2.1 %collective-permute-start.9 = (f32[256]{0:T(256)S(1)}, f32[256]{0:T(256)S(1)}, u32[]{:S(2)}, u32[]{:S(2)}) collective-permute-start(f32[256]{0:T(256)S(1)} %and_select_fusion.2), channel_id=1, source_target_pairs={{12,0},{16,4},{20,8},{24,12},{28,16},{0,20},{4,24},{8,28},{13,1},{... | collective-permute-start | bytes 3080 | tf_op jit(solution)/shard_map/ppermute | solution.py:13
  13.8 0.4 collective-permute-start.7
  14.2 1.6 collective-permute-start.5
  15.8 1.2 collective-permute-start.3
  17.0 0.0 collective-permute-start.1
  17.0 0.0 copy-done.10
  17.0 0.0 copy-done
  17.0 0.6 gather_fusion.2
  17.7 0.6 gather_fusion.1
  18.3 0.0 collective-permute-done.9
  18.3 0.0 copy-done.4
  18.3 0.4 collective-permute-start
  18.8 0.1 dynamic_slice.3
  18.8 0.0 collective-permute-done.7
  18.9 1.4 collective-permute-start.2
  20.2 0.0 collective-permute-done.5
  20.2 0.3 collective-permute-start.4
  20.5 0.0 collective-permute-done.3
  20.5 2.8 %collective-permute-start.8 = (f32[256,1024]{1,0:T(8,128)S(1)}, f32[256,1024]{1,0:T(8,128)}, u32[]{:S(2)}, u32[]{:S(2)}) collective-permute-start(f32[256,1024]{1,0:T(8,128)S(1)} %copy-done.4), channel_id=1, source_target_pairs={{12,0},{16,4},{20,8},{24,12},{28,16},{0,20},{4,24},{8,28},{13,1},{... | collective-permute-start | bytes 3145736 | tf_op jit(solution)/shard_map/ppermute | solution.py:13
  23.4 0.0 collective-permute-done.1
  23.4 1.7 collective-permute-start.6
  25.1 1.4 broadcast_add_fusion
  26.5 31.5 %all-to-all-done = f32[4,256,1024]{1,0,2:T(4,128)} async-done(((f32[4,256,1024]{1,0,2:T(4,128)}), f32[4,256,1024]{1,0,2:T(4,128)}, u32[]{:S(2)}, u32[]{:S(2)}) %all-to-all-start) | async-done | bytes 4194336 | tf_op jit(solution)/shard_map/all_to_all | solution.py:37
  58.0 5.0 %copy.19 = f32[4,256,1024]{1,2,0:T(8,128)} copy(f32[4,256,1024]{1,0,2:T(4,128)} %all-to-all-done) | data formatting | bytes 8388608 | tf_op jit(solution)/shard_map/all_to_all | solution.py:37
  63.0 5.2 %copy.20 = f32[4,4,256,256]{3,2,1,0:T(8,128)} copy(f32[4,4,256,256]{2,3,1,0:T(8,128)} %bitcast.67) | data formatting | bytes 8388608 | tf_op jit(solution)/shard_map/all_to_all | solution.py:37
  68.2 4.3 %convolution_divide_fusion.5 = f32[256,4,256]{2,0,1:T(8,128)S(1)} fusion(f32[4,1024,256]{2,1,0:T(8,128)} %bitcast.61, f32[256,1024]{1,0:T(8,128)S(1)} %copy-done.4, f32[4]{0:T(128)S(1)} %fusion.20, f32[256,256]{1,0:T(8,128)} %get-tuple-element.11), kind=kOutput, calls=%fused_computation.9 | convolution fusion | flops 1611137024 | bytes 6553616 | tf_op jit(solution)/shard_map/rb,pba->rpa/dot_general | solution.py:41
  72.5 0.0 copy-start.3
  72.5 0.0 copy-start.8
  72.5 1.9 fusion.17
  74.4 0.0 collective-permute-done
  74.5 0.2 copy-done.3
  74.7 0.0 copy-done.8
  74.7 2.3 %convolution_divide_fusion.4 = f32[256,4,256]{2,0,1:T(8,128)S(1)} fusion(f32[4,1024,256]{2,1,0:T(8,128)S(1)} %bitcast.62, f32[256,1024]{1,0:T(8,128)S(1)} %collective-permute-done, f32[256,256]{1,0:T(8,128)S(1)} %copy-done.8, f32[4]{0:T(128)S(1)} %fusion.20), kind=kOutput, calls=%fused_computation.8 | convolution fusion | flops 1611137024 | bytes 6553616 | tf_op jit(solution)/shard_map/rb,pba->rpa/dot_general | solution.py:41
  77.0 0.0 copy-start.7
  77.0 1.9 fusion.14
  79.0 0.0 collective-permute-done.2
  79.0 0.0 copy-done.7
  79.0 3.5 %convolution_divide_fusion.3 = f32[256,4,256]{2,0,1:T(8,128)S(1)} fusion(f32[4,1024,256]{2,1,0:T(8,128)S(1)} %bitcast.63, f32[256,1024]{1,0:T(8,128)} %collective-permute-done.2, f32[256,256]{1,0:T(8,128)S(1)} %copy-done.7, f32[4]{0:T(128)S(1)} %fusion.20), kind=kOutput, calls=%fused_computation.7 | convolution fusion | flops 1611137024 | bytes 6553616 | tf_op jit(solution)/shard_map/rb,pba->rpa/dot_general | solution.py:41
  82.5 0.0 copy-start.6
  82.5 3.2 %fusion.11 = f32[4,256,1024]{2,1,0:T(8,128)S(1)} fusion(f32[256,4,256]{2,0,1:T(8,128)S(1)} %convolution_divide_fusion.3, f32[256,1024]{1,0:T(8,128)} %collective-permute-done.2), kind=kOutput, calls=%fused_computation.19 | convolution fusion | flops 1610612736 | bytes 6291456 | tf_op jit(solution)/shard_map/rc,rpa->pca/dot_general | solution.py:46
  85.7 0.0 collective-permute-done.4
  85.7 0.0 copy-done.6
  85.8 2.5 %convolution_divide_fusion.2 = f32[256,4,256]{2,0,1:T(8,128)S(1)} fusion(f32[4,1024,256]{2,1,0:T(8,128)S(1)} %bitcast.64, f32[256,1024]{1,0:T(8,128)S(1)} %collective-permute-done.4, f32[256,256]{1,0:T(8,128)S(1)} %copy-done.6, f32[4]{0:T(128)S(1)} %fusion.20), kind=kOutput, calls=%fused_computation.6 | convolution fusion | flops 1611137024 | bytes 6553616 | tf_op jit(solution)/shard_map/rb,pba->rpa/dot_general | solution.py:41
  88.3 0.0 copy-start.5
  88.3 1.9 fusion.8
  90.2 33.0 %collective-permute-done.6 = f32[256,1024]{1,0:T(8,128)} collective-permute-done((f32[256,1024]{1,0:T(8,128)S(1)}, f32[256,1024]{1,0:T(8,128)}, u32[]{:S(2)}, u32[]{:S(2)}) %collective-permute-start.6) | collective-permute-done | bytes 1048608 | tf_op jit(solution)/shard_map/ppermute | solution.py:13
  123.3 0.0 copy-done.5
  123.3 3.5 %convolution_divide_fusion.1 = f32[256,4,256]{2,0,1:T(8,128)S(1)} fusion(f32[4,1024,256]{2,1,0:T(8,128)S(1)} %bitcast.65, f32[256,1024]{1,0:T(8,128)} %collective-permute-done.6, f32[256,256]{1,0:T(8,128)S(1)} %copy-done.5, f32[4]{0:T(128)S(1)} %fusion.20), kind=kOutput, calls=%fused_computation.5 | convolution fusion | flops 1611137024 | bytes 6553616 | tf_op jit(solution)/shard_map/rb,pba->rpa/dot_general | solution.py:41
  126.8 3.2 %fusion.5 = f32[4,256,1024]{2,1,0:T(8,128)S(1)} fusion(f32[256,4,256]{2,0,1:T(8,128)S(1)} %convolution_divide_fusion.1, f32[256,1024]{1,0:T(8,128)} %collective-permute-done.6), kind=kOutput, calls=%fused_computation.13 | convolution fusion | flops 1610612736 | bytes 6291456 | tf_op jit(solution)/shard_map/rc,rpa->pca/dot_general | solution.py:46
  130.0 0.0 collective-permute-done.8
  130.0 3.5 %convolution_divide_fusion = f32[256,4,256]{2,0,1:T(8,128)S(1)} fusion(f32[4,1024,256]{2,1,0:T(8,128)S(1)} %bitcast.66, f32[256,1024]{1,0:T(8,128)} %collective-permute-done.8, f32[256,256]{1,0:T(8,128)S(1)} %get-tuple-element.6, f32[4]{0:T(128)S(1)} %fusion.20), kind=kOutput, calls=%fused_computation.4 | convolution fusion | flops 1611137024 | bytes 6553616 | tf_op jit(solution)/shard_map/rb,pba->rpa/dot_general | solution.py:41
  133.5 6.5 %add_bitcast_fusion = f32[4,1024,256]{1,2,0:T(8,128)} fusion(f32[4,256,1024]{2,1,0:T(8,128)S(1)} %fusion.5, f32[4,256,1024]{2,1,0:T(8,128)S(1)} %fusion.8, f32[4,256,1024]{2,1,0:T(8,128)S(1)} %fusion.11, f32[4,256,1024]{2,1,0:T(8,128)S(1)} %fusion.17, f32[4,256,1024]{2,1,0:T(8,128)S(1)} %fusion.14, f32[256,4,256]{2,0,1:T(8,128)S(1)} %convolution_divide_fusion, ...), kind=kOutput, calls=%fused_computation.3 | convolution fusion | flops 1615855616 | bytes 27262976 | tf_op jit(solution)/shard_map/rc,rpa->pca/dot_general | solution.py:46
  140.0 5.2 %copy.27 = f32[4,1024,256]{2,0,1:T(4,128)} copy(f32[4,1024,256]{1,2,0:T(8,128)} %add_bitcast_fusion) | data formatting | bytes 8388608 | tf_op jit(solution)/shard_map/add | solution.py:49
  145.2 51.5 %all_to_all.36 = f32[4,1024,256]{2,0,1:T(4,128)S(1)} all-to-all(f32[4,1024,256]{2,0,1:T(4,128)} %copy.27), channel_id=1, replica_groups=mesh['blk'=8,'vb'=4] {'vb'}, dimensions={1} | all-to-all | bytes 8388608 | tf_op jit(solution)/shard_map/all_to_all | solution.py:50
  196.7 4.6 %copy.28 = f32[4,256,4,256]{3,2,1,0:T(4,128)} copy(f32[4,256,4,256]{3,0,1,2:T(4,128)S(1)} %bitcast.68) | data formatting | bytes 8388608 | tf_op jit(solution)/shard_map/all_to_all | solution.py:50
  201.4 5.8 %all_to_all.33 = f32[4,256,1024]{2,1,0:T(8,128)} reshape(f32[4,256,4,256]{3,2,1,0:T(4,128)} %copy.28) | data formatting | bytes 8388608 | tf_op jit(solution)/shard_map/all_to_all | solution.py:50
  207.1 0.0 copy-done.1
  (10 shorter events, 0.0 us)
Async XLA Ops:
  0.0 17.0 %copy-start = (f32[256]{0:T(256)S(1)}, f32[256]{0:T(256)}, u32[]{:S(2)}) copy-start(f32[256]{0:T(256)} %param.12) | copy-start | bytes 3076
  5.2 5.0 %copy-start.9 = (s32[256]{0:T(256)S(1)}, s32[256]{0:T(256)}, u32[]{:S(2)}) copy-start(s32[256]{0:T(256)} %param.10) | copy-start | bytes 3076
  5.2 5.1 %copy-start.2 = (f32[1024]{0:T(1024)S(1)}, f32[1024]{0:T(1024)}, u32[]{:S(2)}) copy-start(f32[1024]{0:T(1024)} %param.13) | copy-start | bytes 12292
  5.2 11.8 %copy-start.10 = (s32[4,2]{0,1:T(2,128)S(1)}, s32[4,2]{0,1:T(2,128)}, u32[]{:S(2)}) copy-start(s32[4,2]{0,1:T(2,128)} %param.11) | copy-start | bytes 100
  5.2 13.1 %copy-start.4 = (f32[256,1024]{1,0:T(8,128)S(1)}, f32[256,1024]{1,0:T(8,128)}, u32[]{:S(2)}) copy-start(f32[256,1024]{1,0:T(8,128)} %param.9) | copy-start | bytes 3145732
  5.3 52.7 %all-to-all-start = ((f32[4,256,1024]{1,0,2:T(4,128)}), f32[4,256,1024]{1,0,2:T(4,128)}, u32[]{:S(2)}, u32[]{:S(2)}) async-start(f32[4,256,1024]{1,0,2:T(4,128)} %copy.18), calls=%async_computation | async-start | bytes 8388608 | tf_op jit(solution)/shard_map/all_to_all | solution.py:37
  11.7 6.6 %collective-permute-start.9 = (f32[256]{0:T(256)S(1)}, f32[256]{0:T(256)S(1)}, u32[]{:S(2)}, u32[]{:S(2)}) collective-permute-start(f32[256]{0:T(256)S(1)} %and_select_fusion.2), channel_id=1, source_target_pairs={{12,0},{16,4},{20,8},{24,12},{28,16},{0,20},{4,24},{8,28},{13,1},{... | collective-permute-start | bytes 3080 | tf_op jit(solution)/shard_map/ppermute | solution.py:13
  13.8 5.1 %collective-permute-start.7 = (f32[256]{0:T(256)S(1)}, f32[256]{0:T(256)S(1)}, u32[]{:S(2)}, u32[]{:S(2)}) collective-permute-start(f32[256]{0:T(256)S(1)} %and_select_fusion.2), channel_id=1, source_target_pairs={{8,0},{12,4},{16,8},{20,12},{24,16},{28,20},{0,24},{4,28},{9,1},{1... | collective-permute-start | bytes 3080 | tf_op jit(solution)/shard_map/ppermute | solution.py:13
  14.2 6.0 %collective-permute-start.5 = (f32[256]{0:T(256)S(1)}, f32[256]{0:T(256)S(1)}, u32[]{:S(2)}, u32[]{:S(2)}) collective-permute-start(f32[256]{0:T(256)S(1)} %and_select_fusion.2), channel_id=1, source_target_pairs={{24,0},{28,4},{0,8},{4,12},{8,16},{12,20},{16,24},{20,28},{25,1},{... | collective-permute-start | bytes 3080 | tf_op jit(solution)/shard_map/ppermute | solution.py:13
  15.8 4.7 %collective-permute-start.3 = (f32[256]{0:T(256)S(1)}, f32[256]{0:T(256)S(1)}, u32[]{:S(2)}, u32[]{:S(2)}) collective-permute-start(f32[256]{0:T(256)S(1)} %and_select_fusion.2), channel_id=1, source_target_pairs={{4,0},{8,4},{12,8},{16,12},{20,16},{24,20},{28,24},{0,28},{5,1},{9... | collective-permute-start | bytes 3080 | tf_op jit(solution)/shard_map/ppermute | solution.py:13
  17.0 6.4 %collective-permute-start.1 = (f32[256]{0:T(256)S(1)}, f32[256]{0:T(256)S(1)}, u32[]{:S(2)}, u32[]{:S(2)}) collective-permute-start(f32[256]{0:T(256)S(1)} %and_select_fusion.2), channel_id=1, source_target_pairs={{28,0},{0,4},{4,8},{8,12},{12,16},{16,20},{20,24},{24,28},{29,1},{... | collective-permute-start | bytes 3080 | tf_op jit(solution)/shard_map/ppermute | solution.py:13
  18.3 56.1 %collective-permute-start = (f32[256,1024]{1,0:T(8,128)S(1)}, f32[256,1024]{1,0:T(8,128)S(1)}, u32[]{:S(2)}, u32[]{:S(2)}) collective-permute-start(f32[256,1024]{1,0:T(8,128)S(1)} %copy-done.4), channel_id=1, source_target_pairs={{28,0},{0,4},{4,8},{8,12},{12,16},{16,20},{20,24},{24,28},{29,1},{... | collective-permute-start | bytes 3145736 | tf_op jit(solution)/shard_map/ppermute | solution.py:13
  18.9 60.1 %collective-permute-start.2 = (f32[256,1024]{1,0:T(8,128)S(1)}, f32[256,1024]{1,0:T(8,128)}, u32[]{:S(2)}, u32[]{:S(2)}) collective-permute-start(f32[256,1024]{1,0:T(8,128)S(1)} %copy-done.4), channel_id=1, source_target_pairs={{4,0},{8,4},{12,8},{16,12},{20,16},{24,20},{28,24},{0,28},{5,1},{9... | collective-permute-start | bytes 3145736 | tf_op jit(solution)/shard_map/ppermute | solution.py:13
  20.2 65.5 %collective-permute-start.4 = (f32[256,1024]{1,0:T(8,128)S(1)}, f32[256,1024]{1,0:T(8,128)S(1)}, u32[]{:S(2)}, u32[]{:S(2)}) collective-permute-start(f32[256,1024]{1,0:T(8,128)S(1)} %copy-done.4), channel_id=1, source_target_pairs={{24,0},{28,4},{0,8},{4,12},{8,16},{12,20},{16,24},{20,28},{25,1},{... | collective-permute-start | bytes 3145736 | tf_op jit(solution)/shard_map/ppermute | solution.py:13
  20.5 109.5 %collective-permute-start.8 = (f32[256,1024]{1,0:T(8,128)S(1)}, f32[256,1024]{1,0:T(8,128)}, u32[]{:S(2)}, u32[]{:S(2)}) collective-permute-start(f32[256,1024]{1,0:T(8,128)S(1)} %copy-done.4), channel_id=1, source_target_pairs={{12,0},{16,4},{20,8},{24,12},{28,16},{0,20},{4,24},{8,28},{13,1},{... | collective-permute-start | bytes 3145736 | tf_op jit(solution)/shard_map/ppermute | solution.py:13
  23.4 99.9 %collective-permute-start.6 = (f32[256,1024]{1,0:T(8,128)S(1)}, f32[256,1024]{1,0:T(8,128)}, u32[]{:S(2)}, u32[]{:S(2)}) collective-permute-start(f32[256,1024]{1,0:T(8,128)S(1)} %copy-done.4), channel_id=1, source_target_pairs={{8,0},{12,4},{16,8},{20,12},{24,16},{28,20},{0,24},{4,28},{9,1},{1... | collective-permute-start | bytes 3145736 | tf_op jit(solution)/shard_map/ppermute | solution.py:13
  72.5 2.2 %copy-start.3 = (f32[4,4,256,256]{3,2,1,0:T(8,128)S(1)}, f32[4,4,256,256]{3,2,1,0:T(8,128)}, u32[]{:S(2)}) copy-start(f32[4,4,256,256]{3,2,1,0:T(8,128)} %copy.20) | copy-start | bytes 12582916
  72.5 2.2 %copy-start.8 = (f32[256,256]{1,0:T(8,128)S(1)}, f32[256,256]{1,0:T(8,128)}, u32[]{:S(2)}) copy-start(f32[256,256]{1,0:T(8,128)} %get-tuple-element.7) | copy-start | bytes 786436
  77.0 2.0 copy-start.7
  82.5 3.2 %copy-start.6 = (f32[256,256]{1,0:T(8,128)S(1)}, f32[256,256]{1,0:T(8,128)}, u32[]{:S(2)}) copy-start(f32[256,256]{1,0:T(8,128)} %get-tuple-element.9) | copy-start | bytes 786436
  88.3 35.0 %copy-start.5 = (f32[256,256]{1,0:T(8,128)S(1)}, f32[256,256]{1,0:T(8,128)}, u32[]{:S(2)}) copy-start(f32[256,256]{1,0:T(8,128)} %get-tuple-element.10) | copy-start | bytes 786436
  196.7 10.4 %copy-start.1 = (f32[256]{0:T(256)S(1)}, f32[256]{0:T(256)}, u32[]{:S(2)}) copy-start(f32[256]{0:T(256)} %param.12) | copy-start | bytes 3076

commit v2 on v1

v2 whole, which is shorter than its diff:
```python
import jax
import jax.numpy as jnp
from jax import lax
from jax.sharding import PartitionSpec as P

HOPS = 5
PREC = lax.Precision.HIGH


def fetch(block, axis, offset):
    n = lax.axis_size(axis)
    route = [((i + offset) % n, i) for i in range(n)]
    return lax.ppermute(block, axis, route)


def roll_lanes(x, shift, axis):
    size = x.shape[axis]
    doubled = jnp.concatenate([x, x], axis=axis)
    return lax.dynamic_slice_in_dim(doubled, (size - shift) % size, size, axis)


def local(amplitudes, integrals, row_orbitals, pair_orbitals, occupied_energy, virtual_energy):
    width = virtual_energy.shape[0]
    nv = lax.axis_size("vb")
    quarter = width // nv
    q = lax.axis_index("vb")
    qstart = q * quarter
    row_energy = jnp.take(virtual_energy, row_orbitals, axis=0)
    pair_energy = (
        jnp.take(occupied_energy, pair_orbitals[:, 0], axis=0)
        + jnp.take(occupied_energy, pair_orbitals[:, 1], axis=0)
    )
    own_virtual = lax.dynamic_slice_in_dim(virtual_energy, qstart, quarter, 0)

    pieces = [lax.dynamic_slice_in_dim(amplitudes, qstart, quarter, 2)]
    for k in range(1, nv):
        dest_start = ((q + k) % nv) * quarter
        send = lax.dynamic_slice_in_dim(amplitudes, dest_start, quarter, 2)
        pieces.append(lax.ppermute(send, "vb", [(i, (i + k) % nv) for i in range(nv)]))

    reversed_cols = jnp.concatenate(
        [integrals[:, ((-k) % nv) * quarter:((-k) % nv + 1) * quarter] for k in range(nv)], axis=1
    )
    rotated = roll_lanes(reversed_cols, qstart, 1)

    low = -(HOPS // 2)
    high = HOPS - HOPS // 2
    offsets = [0] + [o for k in range(1, high + 1) for o in (-k, k) if low <= o <= high and o != 0]
    window = []
    for o in offsets:
        if o == 0:
            window.append((rotated, row_energy))
        else:
            window.append((fetch(rotated, "blk", o), fetch(row_energy, "blk", o)))

    scaled_blocks = []
    for block, energies in window:
        weighted = None
        for k in range(nv):
            part = jnp.einsum(
                "rb,pba->rpa",
                block[:, k * quarter:(k + 1) * quarter],
                pieces[k],
                precision=PREC,
                preferred_element_type=jnp.float32,
            )
            weighted = part if weighted is None else weighted + part
        denom = (energies[:, None] + own_virtual[None, :])[:, None, :] - pair_energy[None, :, None]
        scaled_blocks.append(weighted / denom)

    received = [None] * nv
    for k in list(range(1, nv)) + [0]:
        total = None
        for (block, _), scaled in zip(window, scaled_blocks):
            part = jnp.einsum(
                "rc,rpa->pca",
                block[:, k * quarter:(k + 1) * quarter],
                scaled,
                precision=PREC,
                preferred_element_type=jnp.float32,
            )
            total = part if total is None else total + part
        if k == 0:
            received[0] = total
        else:
            received[k] = lax.ppermute(total, "vb", [(i, (i - k) % nv) for i in range(nv)])
    gathered = jnp.concatenate(received, axis=2)
    return roll_lanes(gathered, qstart, 2)


def solution(mesh):
    return jax.shard_map(
        local,
        mesh=mesh,
        in_specs=(P("blk", "vb", None), P("blk", None), P("blk"), P("blk", None), P(), P()),
        out_specs=P("blk", "vb", None),
        check_vma=False,
    )
```

time: 208 us -> 211 us (1.014)
  the two profiles are of different devices: /device:TPU:8 before, /device:TPU:18 now
where the time goes in v2:
time: 211 us; the launch traced here: 207 us
  waiting for transfers between devices  98 us (46%)
  matrix products  58.5 us (28%)
  starting transfers between devices  26 us (12%)
  local copies, waits for them, and re-layouts  23.1 us (11%)
    ppermute x10, waiting for transfers between devices, fetch(): return lax.ppermute(block, axis, route)  43.3 us
    dot_general x24, matrix products, local(): jnp.einsum('rc,rpa->pca', block[:, k * quarter:(k + 1) * quarter], scaled...  32.4 us
    ppermute x3, waiting for transfers between devices, local(): lax.ppermute(total, 'vb', [(i, (i - k) % nv) for i in range(nv)])  31.4 us
    dot_general x24, matrix products, local(): jnp.einsum('rb,pba->rpa', block[:, k * quarter:(k + 1) * quarter], pieces...  26.1 us
    ppermute x3, waiting for transfers between devices, local(): lax.ppermute(send, 'vb', [(i, (i + k) % nv) for i in range(nv)])  23.2 us
    ppermute x10, starting transfers between devices, fetch(): return lax.ppermute(block, axis, route)  20.5 us
    dynamic_slice x3, local copies, waits for them, and re-layouts, roll_lanes(): return lax.dynamic_slice_in_dim(doubled, (size - shift) % size, size, axis)  10.3 us
    unnamed x29, local copies, waits for them, and re-layouts  5.52 us
  transfers between devices with their start and end apart: 16, of which 7 were waited for; matrix products, arithmetic and copies ran while one was open for 27% of the time, Pallas kernels for 0%

profile of v2, /device:TPU:18, one launch (start us, length us, event | category | flops | bytes accessed | tf_op | source)
XLA Modules:
  0.0 206.6 jit_solution(7125071084946641439)
XLA Ops:
  0.0 3.7 %constant_dynamic-slice_fusion.3 = (f32[4,256,256]{2,1,0:T(8,128)}, f32[4,256,256]{2,1,0:T(8,128)}, f32[4,256,256]{2,1,0:T(8,128)}) fusion(f32[4,256,1024]{2,1,0:T(8,128)} %param.8, s32[]{:T(128)S(6)} %select_n.60, s32[]{:T(128)S(6)} %select_n.64, s32[]{:T(128)S(6)} %select_n.62), kind=kLoop, calls=%fused_computation.157 | loop fusion | bytes 6291468 | tf_op jit(solution)/shard_map/dynamic_slice | solution.py:38
  3.8 1.5 collective-permute-start
  5.3 0.7 slice_dynamic-update-slice_fusion.6
  6.0 0.7 slice_dynamic-update-slice_fusion.4
  6.7 0.7 slice_dynamic-update-slice_fusion.2
  7.5 0.7 slice_dynamic-update-slice_fusion
  8.2 0.7 slice_dynamic-update-slice_fusion.7
  8.9 0.7 slice_dynamic-update-slice_fusion.5
  9.6 0.7 slice_dynamic-update-slice_fusion.3
  11.1 2.6 %constant_dynamic-slice_fusion.4 = f32[256,1024]{1,0:T(8,128)} fusion(f32[256,2048]{1,0:T(8,128)} %slice_dynamic-update-slice_fusion.1, s32[]{:T(128)S(6)} %select_n.57), kind=kLoop, calls=%fused_computation.159 | loop fusion | bytes 2097156 | tf_op jit(solution)/shard_map/dynamic_slice | solution.py:19
  13.7 1.4 gather_fusion
  15.6 3.1 %collective-permute-start.12 = (f32[256]{0:T(256)S(1)}, f32[256]{0:T(256)S(1)}, u32[]{:S(2)}, u32[]{:S(2)}) collective-permute-start(f32[256]{0:T(256)S(1)} %and_select_fusion.2), channel_id=1, source_target_pairs={{12,0},{16,4},{20,8},{24,12},{28,16},{0,20},{4,24},{8,28},{13,1},{... | collective-permute-start | bytes 3080 | tf_op jit(solution)/shard_map/ppermute | solution.py:13
  18.8 9.3 %collective-permute-start.4 = (f32[256]{0:T(256)S(1)}, f32[256]{0:T(256)S(1)}, u32[]{:S(2)}, u32[]{:S(2)}) collective-permute-start(f32[256]{0:T(256)S(1)} %and_select_fusion.2), channel_id=1, source_target_pairs={{28,0},{0,4},{4,8},{8,12},{12,16},{16,20},{20,24},{24,28},{29,1},{... | collective-permute-start | bytes 3080 | tf_op jit(solution)/shard_map/ppermute | solution.py:13
  30.8 1.6 collective-permute-start.8
  32.4 3.0 %fusion.38 = f32[256,4,256]{2,0,1:T(8,128)} fusion(f32[4,256,1024]{2,1,0:T(8,128)} %param.8, s32[]{:T(128)S(6)} %select_n.58, f32[256,2048]{1,0:T(8,128)} %slice_dynamic-update-slice_fusion.1, s32[]{:T(128)S(6)} %select_n.57), kind=kOutput, calls=%fused_computation.56 | convolution fusion | flops 402653184 | bytes 2359304 | tf_op jit(solution)/shard_map/rb,pba->rpa/dot_general | solution.py:60
  35.4 3.0 %collective-permute-start.7 = (f32[256,1024]{1,0:T(8,128)}, f32[256,1024]{1,0:T(8,128)S(1)}, u32[]{:S(2)}, u32[]{:S(2)}) collective-permute-start(f32[256,1024]{1,0:T(8,128)} %constant_dynamic-slice_fusion.4), channel_id=1, source_target_pairs={{24,0},{28,4},{0,8},{4,12},{8,16},{12,20},{16,24},{20,28},{25,1},{... | collective-permute-start | bytes 3145736 | tf_op jit(solution)/shard_map/ppermute | solution.py:13
  38.7 1.2 collective-permute-start.5
  39.9 1.6 fusion.40
  41.5 23.2 %collective-permute-done.1 = f32[4,256,256]{2,1,0:T(8,128)S(1)} collective-permute-done((f32[4,256,256]{2,1,0:T(8,128)}, f32[4,256,256]{2,1,0:T(8,128)S(1)}, u32[]{:S(2)}, u32[]{:S(2)}) %collective-permute-start.1) | collective-permute-done | bytes 1048608 | tf_op jit(solution)/shard_map/ppermute | solution.py:39
  64.8 1.7 collective-permute-start.11
  66.4 1.6 fusion.41
  68.1 1.6 fusion.42
  69.7 1.7 fusion.71
  71.4 1.7 convolution_add_fusion.14
  73.1 1.8 fusion.32
  74.9 2.1 %fusion.70 = f32[4,256,256]{2,1,0:T(8,128)S(1)} fusion(f32[256,4,256]{2,0,1:T(8,128)S(1)} %fusion.32, f32[256,2048]{1,0:T(8,128)} %slice_dynamic-update-slice_fusion.1, s32[]{:T(128)S(6)} %add.363), kind=kOutput, calls=%fused_computation.120 | convolution fusion | flops 402653184 | bytes 2359300 | tf_op jit(solution)/shard_map/rc,rpa->pca/dot_general | solution.py:75
  79.0 5.9 %collective-permute-done.5 = f32[256,1024]{1,0:T(8,128)S(1)} collective-permute-done((f32[256,1024]{1,0:T(8,128)}, f32[256,1024]{1,0:T(8,128)S(1)}, u32[]{:S(2)}, u32[]{:S(2)}) %collective-permute-start.5) | collective-permute-done | bytes 1048608 | tf_op jit(solution)/shard_map/ppermute | solution.py:13
  85.6 2.1 %fusion.69 = f32[4,256,256]{2,1,0:T(8,128)S(1)} fusion(f32[256,4,256]{2,0,1:T(8,128)S(1)} %fusion.32, f32[256,2048]{1,0:T(8,128)} %slice_dynamic-update-slice_fusion.1, s32[]{:T(128)S(6)} %add.362), kind=kOutput, calls=%fused_computation.119 | convolution fusion | flops 402653184 | bytes 2359300 | tf_op jit(solution)/shard_map/rc,rpa->pca/dot_general | solution.py:75
  89.0 2.1 %fusion.68 = f32[4,256,256]{2,1,0:T(8,128)S(1)} fusion(f32[256,4,256]{2,0,1:T(8,128)S(1)} %fusion.32, f32[256,2048]{1,0:T(8,128)} %slice_dynamic-update-slice_fusion.1, s32[]{:T(128)S(6)} %add.361), kind=kOutput, calls=%fused_computation.118 | convolution fusion | flops 402653184 | bytes 2359300 | tf_op jit(solution)/shard_map/rc,rpa->pca/dot_general | solution.py:75
  91.1 17.2 %collective-permute-done.9 = f32[256,1024]{1,0:T(8,128)S(1)} collective-permute-done((f32[256,1024]{1,0:T(8,128)}, f32[256,1024]{1,0:T(8,128)S(1)}, u32[]{:S(2)}, u32[]{:S(2)}) %collective-permute-start.9) | collective-permute-done | bytes 1048608 | tf_op jit(solution)/shard_map/ppermute | solution.py:13
  110.2 19.5 %collective-permute-done.11 = f32[256,1024]{1,0:T(8,128)S(1)} collective-permute-done((f32[256,1024]{1,0:T(8,128)}, f32[256,1024]{1,0:T(8,128)S(1)}, u32[]{:S(2)}, u32[]{:S(2)}) %collective-permute-start.11) | collective-permute-done | bytes 1048608 | tf_op jit(solution)/shard_map/ppermute | solution.py:13
  129.7 0.9 fusion.62
  131.9 0.8 fusion.20
  132.8 1.0 fusion.51
  133.8 0.8 fusion.17
  134.6 1.0 fusion.58
  135.6 0.8 fusion.14
  136.5 1.0 fusion.65
  137.5 1.8 fusion.30
  139.3 2.0 convolution_add_fusion.1
  141.2 0.8 fusion.27
  142.1 1.0 fusion.3
  143.1 1.8 collective-permute-start.15
  144.9 1.0 fusion.49
  145.9 1.0 fusion.56
  146.9 1.0 fusion.63
  147.9 2.0 convolution_add_fusion.3
  149.9 1.0 fusion.7
  151.5 1.0 fusion.47
  152.6 1.0 fusion.54
  153.6 1.0 fusion.61
  154.6 2.0 convolution_add_fusion.5
  156.6 1.0 fusion.11
  157.6 0.9 collective-permute-start.13
  158.5 1.0 fusion.46
  159.5 1.0 fusion.53
  160.5 1.0 fusion.60
  161.6 2.1 %fusion.67 = f32[4,256,256]{2,1,0:T(8,128)S(1)} fusion(f32[256,4,256]{2,0,1:T(8,128)S(1)} %fusion.32, f32[256,2048]{1,0:T(8,128)} %slice_dynamic-update-slice_fusion.1, s32[]{:T(128)S(6)} %select_n.57), kind=kOutput, calls=%fused_computation.117 | convolution fusion | flops 402653184 | bytes 2359300 | tf_op jit(solution)/shard_map/rc,rpa->pca/dot_general | solution.py:75
  163.7 2.0 convolution_add_fusion.11
  165.6 1.0 constant_dynamic-update-slice_fusion.7
  166.7 24.0 %collective-permute-done.13 = f32[4,256,256]{1,2,0:T(8,128)S(1)} collective-permute-done((f32[4,256,256]{1,2,0:T(8,128)S(1)}, f32[4,256,256]{1,2,0:T(8,128)S(1)}, u32[]{:S(2)}, u32[]{:S(2)}) %collective-permute-start.13) | collective-permute-done | bytes 1048608 | tf_op jit(solution)/shard_map/ppermute | solution.py:86
  190.8 7.4 %collective-permute-done.14 = f32[4,256,256]{1,2,0:T(8,128)S(1)} collective-permute-done((f32[4,256,256]{1,2,0:T(8,128)S(1)}, f32[4,256,256]{1,2,0:T(8,128)S(1)}, u32[]{:S(2)}, u32[]{:S(2)}) %collective-permute-start.14) | collective-permute-done | bytes 1048608 | tf_op jit(solution)/shard_map/ppermute | solution.py:86
  198.7 2.3 %constant_dynamic-slice_fusion = f32[4,256,1024]{1,2,0:T(8,128)} fusion(f32[4,256,2048]{1,2,0:T(8,128)S(1)} %constant_dynamic-update-slice_fusion, s32[]{:T(128)S(6)} %select_n.57), kind=kLoop, calls=%fused_computation.154 | loop fusion | bytes 8388612 | tf_op jit(solution)/shard_map/dynamic_slice | solution.py:19
  201.0 5.3 %copy.56 = f32[4,256,1024]{2,1,0:T(8,128)} copy(f32[4,256,1024]{1,2,0:T(8,128)} %constant_dynamic-slice_fusion) | data formatting | bytes 8388608 | tf_op jit(solution)/shard_map/dynamic_slice | solution.py:19
  (62 shorter events, 12.6 us)
Async XLA Ops:
  0.0 28.2 %copy-start = (f32[256]{0:T(256)S(1)}, f32[256]{0:T(256)}, u32[]{:S(2)}) copy-start(f32[256]{0:T(256)} %param.12) | copy-start | bytes 3076
  0.0 5.3 %copy-start.4 = (f32[256,1024]{1,0:T(8,128)S(1)}, f32[256,1024]{1,0:T(8,128)}, u32[]{:S(2)}) copy-start(f32[256,1024]{1,0:T(8,128)} %param.9) | copy-start | bytes 3145732
  3.7 9.9 %copy-start.6 = (s32[256]{0:T(256)S(1)}, s32[256]{0:T(256)}, u32[]{:S(2)}) copy-start(s32[256]{0:T(256)} %param.10) | copy-start | bytes 3076
  3.7 10.0 %copy-start.2 = (f32[1024]{0:T(1024)S(1)}, f32[1024]{0:T(1024)}, u32[]{:S(2)}) copy-start(f32[1024]{0:T(1024)} %param.13) | copy-start | bytes 12292
  3.8 15.1 %copy-start.7 = (s32[4,2]{0,1:T(2,128)S(1)}, s32[4,2]{0,1:T(2,128)}, u32[]{:S(2)}) copy-start(s32[4,2]{0,1:T(2,128)} %param.11) | copy-start | bytes 100
  3.8 35.0 %collective-permute-start = (f32[4,256,256]{2,1,0:T(8,128)}, f32[4,256,256]{2,1,0:T(8,128)S(1)}, u32[]{:S(2)}, u32[]{:S(2)}) collective-permute-start(f32[4,256,256]{2,1,0:T(8,128)} %get-tuple-element.6), channel_id=1, source_target_pairs={{0,1},{1,2},{2,3},{3,0},{4,5},{5,6},{6,7},{7,4},{8,9},{9,10},{10,1... | collective-permute-start | bytes 3145736 | tf_op jit(solution)/shard_map/ppermute | solution.py:39
  13.7 26.2 %collective-permute-start.3 = (f32[256,1024]{1,0:T(8,128)}, f32[256,1024]{1,0:T(8,128)}, u32[]{:S(2)}, u32[]{:S(2)}) collective-permute-start(f32[256,1024]{1,0:T(8,128)} %constant_dynamic-slice_fusion.4), channel_id=1, source_target_pairs={{28,0},{0,4},{4,8},{8,12},{12,16},{16,20},{20,24},{24,28},{29,1},{... | collective-permute-start | bytes 3145736 | tf_op jit(solution)/shard_map/ppermute | solution.py:13
  15.1 3.7 %collective-permute-start.10 = (f32[256]{0:T(256)S(1)}, f32[256]{0:T(256)S(1)}, u32[]{:S(2)}, u32[]{:S(2)}) collective-permute-start(f32[256]{0:T(256)S(1)} %and_select_fusion.2), channel_id=1, source_target_pairs={{8,0},{12,4},{16,8},{20,12},{24,16},{28,20},{0,24},{4,28},{9,1},{1... | collective-permute-start | bytes 3080 | tf_op jit(solution)/shard_map/ppermute | solution.py:13
  15.6 13.8 %collective-permute-start.12 = (f32[256]{0:T(256)S(1)}, f32[256]{0:T(256)S(1)}, u32[]{:S(2)}, u32[]{:S(2)}) collective-permute-start(f32[256]{0:T(256)S(1)} %and_select_fusion.2), channel_id=1, source_target_pairs={{12,0},{16,4},{20,8},{24,12},{28,16},{0,20},{4,24},{8,28},{13,1},{... | collective-permute-start | bytes 3080 | tf_op jit(solution)/shard_map/ppermute | solution.py:13
  18.8 46.0 %collective-permute-start.1 = (f32[4,256,256]{2,1,0:T(8,128)}, f32[4,256,256]{2,1,0:T(8,128)S(1)}, u32[]{:S(2)}, u32[]{:S(2)}) collective-permute-start(f32[4,256,256]{2,1,0:T(8,128)} %get-tuple-element.8), channel_id=1, source_target_pairs={{0,2},{1,3},{2,0},{3,1},{4,6},{5,7},{6,4},{7,5},{8,10},{9,11},{10,... | collective-permute-start | bytes 3145736 | tf_op jit(solution)/shard_map/ppermute | solution.py:39
  18.8 10.7 %collective-permute-start.4 = (f32[256]{0:T(256)S(1)}, f32[256]{0:T(256)S(1)}, u32[]{:S(2)}, u32[]{:S(2)}) collective-permute-start(f32[256]{0:T(256)S(1)} %and_select_fusion.2), channel_id=1, source_target_pairs={{28,0},{0,4},{4,8},{8,12},{12,16},{16,20},{20,24},{24,28},{29,1},{... | collective-permute-start | bytes 3080 | tf_op jit(solution)/shard_map/ppermute | solution.py:13
  29.4 1.3 collective-permute-start.6
  29.5 38.6 %collective-permute-start.2 = (f32[4,256,256]{2,1,0:T(8,128)}, f32[4,256,256]{2,1,0:T(8,128)S(1)}, u32[]{:S(2)}, u32[]{:S(2)}) collective-permute-start(f32[4,256,256]{2,1,0:T(8,128)} %get-tuple-element.7), channel_id=1, source_target_pairs={{0,3},{1,0},{2,1},{3,2},{4,7},{5,4},{6,5},{7,6},{8,11},{9,8},{10,9... | collective-permute-start | bytes 3145736 | tf_op jit(solution)/shard_map/ppermute | solution.py:39
  30.8 4.7 %collective-permute-start.8 = (f32[256]{0:T(256)S(1)}, f32[256]{0:T(256)S(1)}, u32[]{:S(2)}, u32[]{:S(2)}) collective-permute-start(f32[256]{0:T(256)S(1)} %and_select_fusion.2), channel_id=1, source_target_pairs={{24,0},{28,4},{0,8},{4,12},{8,16},{12,20},{16,24},{20,28},{25,1},{... | collective-permute-start | bytes 3080 | tf_op jit(solution)/shard_map/ppermute | solution.py:13
  35.4 41.5 %collective-permute-start.7 = (f32[256,1024]{1,0:T(8,128)}, f32[256,1024]{1,0:T(8,128)S(1)}, u32[]{:S(2)}, u32[]{:S(2)}) collective-permute-start(f32[256,1024]{1,0:T(8,128)} %constant_dynamic-slice_fusion.4), channel_id=1, source_target_pairs={{24,0},{28,4},{0,8},{4,12},{8,16},{12,20},{16,24},{20,28},{25,1},{... | collective-permute-start | bytes 3145736 | tf_op jit(solution)/shard_map/ppermute | solution.py:13
  38.7 32.7 %copy-start.5 = (f32[256,4,256]{2,0,1:T(8,128)S(1)}, f32[256,4,256]{2,0,1:T(8,128)}, u32[]{:S(2)}) copy-start(f32[256,4,256]{2,0,1:T(8,128)} %fusion.38) | copy-start | bytes 3145732
  38.7 46.2 %collective-permute-start.5 = (f32[256,1024]{1,0:T(8,128)}, f32[256,1024]{1,0:T(8,128)S(1)}, u32[]{:S(2)}, u32[]{:S(2)}) collective-permute-start(f32[256,1024]{1,0:T(8,128)} %constant_dynamic-slice_fusion.4), channel_id=1, source_target_pairs={{4,0},{8,4},{12,8},{16,12},{20,16},{24,20},{28,24},{0,28},{5,1},{9... | collective-permute-start | bytes 3145736 | tf_op jit(solution)/shard_map/ppermute | solution.py:13
  39.9 68.3 %collective-permute-start.9 = (f32[256,1024]{1,0:T(8,128)}, f32[256,1024]{1,0:T(8,128)S(1)}, u32[]{:S(2)}, u32[]{:S(2)}) collective-permute-start(f32[256,1024]{1,0:T(8,128)} %constant_dynamic-slice_fusion.4), channel_id=1, source_target_pairs={{8,0},{12,4},{16,8},{20,12},{24,16},{28,20},{0,24},{4,28},{9,1},{1... | collective-permute-start | bytes 3145736 | tf_op jit(solution)/shard_map/ppermute | solution.py:13
  64.8 65.0 %collective-permute-start.11 = (f32[256,1024]{1,0:T(8,128)}, f32[256,1024]{1,0:T(8,128)S(1)}, u32[]{:S(2)}, u32[]{:S(2)}) collective-permute-start(f32[256,1024]{1,0:T(8,128)} %constant_dynamic-slice_fusion.4), channel_id=1, source_target_pairs={{12,0},{16,4},{20,8},{24,12},{28,16},{0,20},{4,24},{8,28},{13,1},{... | collective-permute-start | bytes 3145736 | tf_op jit(solution)/shard_map/ppermute | solution.py:13
  109.6 22.3 %copy-start.3 = (f32[4,256,1024]{2,1,0:T(8,128)S(1)}, f32[4,256,1024]{2,1,0:T(8,128)}, u32[]{:S(2)}) copy-start(f32[4,256,1024]{2,1,0:T(8,128)} %param.8) | copy-start | bytes 12582916
  143.1 55.2 %collective-permute-start.15 = (f32[4,256,256]{1,2,0:T(8,128)S(1)}, f32[4,256,256]{1,2,0:T(8,128)S(1)}, u32[]{:S(2)}, u32[]{:S(2)}) collective-permute-start(f32[4,256,256]{1,2,0:T(8,128)S(1)} %fusion.3), channel_id=1, source_target_pairs={{0,1},{1,2},{2,3},{3,0},{4,5},{5,6},{6,7},{7,4},{8,9},{9,10},{10,1... | collective-permute-start | bytes 3145736 | tf_op jit(solution)/shard_map/ppermute | solution.py:86
  150.9 47.3 %collective-permute-start.14 = (f32[4,256,256]{1,2,0:T(8,128)S(1)}, f32[4,256,256]{1,2,0:T(8,128)S(1)}, u32[]{:S(2)}, u32[]{:S(2)}) collective-permute-start(f32[4,256,256]{1,2,0:T(8,128)S(1)} %fusion.7), channel_id=1, source_target_pairs={{0,2},{1,3},{2,0},{3,1},{4,6},{5,7},{6,4},{7,5},{8,10},{9,11},{10,... | collective-permute-start | bytes 3145736 | tf_op jit(solution)/shard_map/ppermute | solution.py:86
  157.6 33.1 %collective-permute-start.13 = (f32[4,256,256]{1,2,0:T(8,128)S(1)}, f32[4,256,256]{1,2,0:T(8,128)S(1)}, u32[]{:S(2)}, u32[]{:S(2)}) collective-permute-start(f32[4,256,256]{1,2,0:T(8,128)S(1)} %fusion.11), channel_id=1, source_target_pairs={{0,3},{1,0},{2,1},{3,2},{4,7},{5,4},{6,5},{7,6},{8,11},{9,8},{10,9... | collective-permute-start | bytes 3145736 | tf_op jit(solution)/shard_map/ppermute | solution.py:86
  198.7 7.7 %copy-start.1 = (f32[256]{0:T(256)S(1)}, f32[256]{0:T(256)}, u32[]{:S(2)}) copy-start(f32[256]{0:T(256)} %param.12) | copy-start | bytes 3076

commit v3 on v1

v3 whole, which is shorter than its diff:
```python
import jax
import jax.numpy as jnp
from jax import lax
from jax.sharding import PartitionSpec as P

HOPS = 5
PREC = lax.Precision.HIGH


def roll_lanes(x, shift, axis):
    size = x.shape[axis]
    doubled = jnp.concatenate([x, x], axis=axis)
    return lax.dynamic_slice_in_dim(doubled, (size - shift) % size, size, axis)


def window_blocks(packed):
    nb = lax.axis_size("blk")
    even = range(0, nb, 2)
    core = lax.axis_index("blk") % 2

    def perm(x, pairs):
        return lax.ppermute(x, "blk", [(s % nb, t % nb) for s, t in pairs])

    a = perm(packed, [(d - 2, d) for d in even] + [(d + 3, d + 1) for d in even])
    b = perm(packed, [(d - 1, d) for d in even] + [(d + 2, d + 1) for d in even])
    c = perm(packed, [(d + 4, d + 1) for d in even])
    swap = [(d, d + 1) for d in even] + [(d + 1, d) for d in even]
    e = perm(packed, swap)
    f = perm(b, swap)
    g = perm(a, [(d + 1, d) for d in even])
    last = jnp.where(core == 0, g, c)
    return [packed, e, b, a, f, last]


def local(amplitudes, integrals, row_orbitals, pair_orbitals, occupied_energy, virtual_energy):
    assert HOPS == 5 and lax.axis_size("blk") % 2 == 0
    width = virtual_energy.shape[0]
    rows = integrals.shape[0]
    nv = lax.axis_size("vb")
    quarter = width // nv
    q = lax.axis_index("vb")
    qstart = q * quarter
    row_energy = jnp.take(virtual_energy, row_orbitals, axis=0)
    pair_energy = (
        jnp.take(occupied_energy, pair_orbitals[:, 0], axis=0)
        + jnp.take(occupied_energy, pair_orbitals[:, 1], axis=0)
    )
    own_virtual = lax.dynamic_slice_in_dim(virtual_energy, qstart, quarter, 0)

    pieces = [lax.dynamic_slice_in_dim(amplitudes, qstart, quarter, 2)]
    for k in range(1, nv):
        dest_start = ((q + k) % nv) * quarter
        send = lax.dynamic_slice_in_dim(amplitudes, dest_start, quarter, 2)
        pieces.append(lax.ppermute(send, "vb", [(i, (i + k) % nv) for i in range(nv)]))
    rest = jnp.concatenate(pieces[1:], axis=1)

    reversed_cols = jnp.concatenate(
        [integrals[:, ((-k) % nv) * quarter:((-k) % nv + 1) * quarter] for k in range(nv)], axis=1
    )
    rotated = roll_lanes(reversed_cols, qstart, 1)
    erows = -(-rows // width)
    erows_padded = -(-erows // 8) * 8
    energy_rows = jnp.pad(row_energy, (0, erows_padded * width - rows)).reshape(erows_padded, width)
    packed = jnp.concatenate([rotated, energy_rows], axis=0)

    remote = None
    scaled_blocks = []
    window = window_blocks(packed)
    for item in window:
        block = item[:rows]
        energies = item[rows:].reshape(-1)[:rows]
        weighted = jnp.einsum(
            "rb,pba->rpa", block[:, :quarter], pieces[0], precision=PREC, preferred_element_type=jnp.float32
        ) + jnp.einsum(
            "rb,pba->rpa", block[:, quarter:], rest, precision=PREC, preferred_element_type=jnp.float32
        )
        denom = (energies[:, None] + own_virtual[None, :])[:, None, :] - pair_energy[None, :, None]
        scaled = weighted / denom
        scaled_blocks.append((block, scaled))
        part = jnp.einsum(
            "rc,rpa->pca", block[:, quarter:], scaled, precision=PREC, preferred_element_type=jnp.float32
        )
        remote = part if remote is None else remote + part

    received = [None] * nv
    for k in range(1, nv):
        chunk = remote[:, (k - 1) * quarter:k * quarter]
        received[k] = lax.ppermute(chunk, "vb", [(i, (i - k) % nv) for i in range(nv)])
    own = None
    for block, scaled in scaled_blocks:
        part = jnp.einsum(
            "rc,rpa->pca", block[:, :quarter], scaled, precision=PREC, preferred_element_type=jnp.float32
        )
        own = part if own is None else own + part
    received[0] = own
    gathered = jnp.concatenate(received, axis=2)
    return roll_lanes(gathered, qstart, 2)


def solution(mesh):
    return jax.shard_map(
        local,
        mesh=mesh,
        in_specs=(P("blk", "vb", None), P("blk", None), P("blk"), P("blk", None), P(), P()),
        out_specs=P("blk", "vb", None),
        check_vma=False,
    )
```

time: 208 us -> 165 us (0.79)
  the two profiles are of different devices: /device:TPU:8 before, /device:TPU:18 now
where the time goes in v3:
time: 165 us; the launch traced here: 164 us
  waiting for transfers between devices  90 us (55%)
  matrix products  38.8 us (24%)
  local copies, waits for them, and re-layouts  20.8 us (13%)
  starting transfers between devices  12.5 us (8%)
    ppermute x3, waiting for transfers between devices, local(): lax.ppermute(chunk, 'vb', [(i, (i - k) % nv) for i in range(nv)])  40.4 us
    ppermute x3, waiting for transfers between devices, local(): lax.ppermute(send, 'vb', [(i, (i + k) % nv) for i in range(nv)])  36.3 us
    ppermute x6, waiting for transfers between devices, perm(): return lax.ppermute(x, 'blk', [(s % nb, t % nb) for s, t in pairs])  13.4 us
    dot_general x6, matrix products, local(): jnp.einsum('rc,rpa->pca', block[:, quarter:], scaled, precision=PREC, pre...  12.7 us
    dot_general x6, matrix products, local(): jnp.einsum('rb,pba->rpa', block[:, quarter:], rest, precision=PREC, prefe...  11.6 us
    dynamic_slice x3, local copies, waits for them, and re-layouts, roll_lanes(): return lax.dynamic_slice_in_dim(doubled, (size - shift) % size, size, axis)  8.05 us
    dot_general x6, matrix products, local(): jnp.einsum('rc,rpa->pca', block[:, :quarter], scaled, precision=PREC, pre...  7.48 us
    dot_general x6, matrix products, local(): jnp.einsum('rb,pba->rpa', block[:, :quarter], pieces[0], precision=PREC,...  7 us
  transfers between devices with their start and end apart: 12, of which 4 were waited for; matrix products, arithmetic and copies ran while one was open for 14% of the time, Pallas kernels for 0%

profile of v3, /device:TPU:18, one launch (start us, length us, event | category | flops | bytes accessed | tf_op | source)
XLA Modules:
  0.0 164.4 jit_solution(9561656694305658395)
XLA Ops:
  0.0 3.8 %constant_dynamic-slice_fusion.1 = (f32[4,256,256]{2,1,0:T(8,128)}, f32[4,256,256]{2,1,0:T(8,128)}, f32[4,256,256]{2,1,0:T(8,128)}) fusion(f32[4,256,1024]{2,1,0:T(8,128)} %param.8, s32[]{:T(128)S(6)} %select_n.76, s32[]{:T(128)S(6)} %select_n.72, s32[]{:T(128)S(6)} %select_n.74), kind=kLoop, calls=%fused_computation.107 | loop fusion | bytes 6291468 | tf_op jit(solution)/shard_map/dynamic_slice | solution.py:53
  3.8 0.5 collective-permute-start.2
  4.4 2.4 %collective-permute-start = (f32[4,256,256]{2,1,0:T(8,128)}, f32[4,256,256]{2,1,0:T(8,128)}, u32[]{:S(2)}, u32[]{:S(2)}) collective-permute-start(f32[4,256,256]{2,1,0:T(8,128)} %get-tuple-element.7), channel_id=1, source_target_pairs={{0,1},{1,2},{2,3},{3,0},{4,5},{5,6},{6,7},{7,4},{8,9},{9,10},{10,1... | collective-permute-start | bytes 3145736 | tf_op jit(solution)/shard_map/ppermute | solution.py:54
  6.8 1.5 collective-permute-start.1
  8.5 1.4 gather_fusion
  10.0 0.3 constant_dynamic-slice_fusion.4
  10.3 1.1 pad_maximum_fusion
  11.4 1.6 collective-permute-start.5
  13.0 0.1 dynamic_slice.26
  13.1 0.6 gather_fusion.2
  13.8 0.6 gather_fusion.1
  14.4 1.9 %fusion.14 = f32[256,4,256]{2,0,1:T(8,128)S(1)} fusion(f32[4,256,1024]{2,1,0:T(8,128)} %param.8, s32[]{:T(128)S(6)} %select_n.70, f32[256,2048]{1,0:T(8,128)S(1)} %slice_dynamic-update-slice_fusion.1, s32[]{:T(128)S(6)} %select_n.69), kind=kOutput, calls=%fused_computation.34 | convolution fusion | flops 402653184 | bytes 2359304 | tf_op jit(solution)/shard_map/rb,pba->rpa/dot_general | solution.py:72
  16.3 36.2 %collective-permute-done = f32[4,256,256]{2,1,0:T(8,128)} collective-permute-done((f32[4,256,256]{2,1,0:T(8,128)}, f32[4,256,256]{2,1,0:T(8,128)}, u32[]{:S(2)}, u32[]{:S(2)}) %collective-permute-start) | collective-permute-done | bytes 1048608 | tf_op jit(solution)/shard_map/ppermute | solution.py:54
  52.5 1.3 constant_dynamic-update-slice_fusion.2
  53.8 2.4 %collective-permute-start.8 = (f32[264,1024]{1,0:T(8,128)}, f32[264,1024]{1,0:T(8,128)S(1)}, u32[]{:S(2)}, u32[]{:S(2)}) collective-permute-start(f32[264,1024]{1,0:T(8,128)} %pad_maximum_fusion), channel_id=1, source_target_pairs={{16,4},{24,12},{0,20},{8,28},{17,5},{25,13},{1,21},{9,29},{18,6},{... | collective-permute-start | bytes 3244040 | tf_op jit(solution)/shard_map/ppermute | solution.py:22
  56.3 1.3 constant_dynamic-update-slice_fusion.1
  57.6 1.3 constant_dynamic-update-slice_fusion
  58.9 1.8 %collective-permute-done.5 = f32[264,1024]{1,0:T(8,128)S(1)} collective-permute-done((f32[264,1024]{1,0:T(8,128)}, f32[264,1024]{1,0:T(8,128)S(1)}, u32[]{:S(2)}, u32[]{:S(2)}) %collective-permute-start.5) | collective-permute-done | bytes 1081376 | tf_op jit(solution)/shard_map/ppermute | solution.py:22
  60.6 1.5 collective-permute-start.7
  62.1 11.6 %collective-permute-done.4 = f32[264,1024]{1,0:T(8,128)} collective-permute-done((f32[264,1024]{1,0:T(8,128)}, f32[264,1024]{1,0:T(8,128)}, u32[]{:S(2)}, u32[]{:S(2)}) %collective-permute-start.4) | collective-permute-done | bytes 1081376 | tf_op jit(solution)/shard_map/ppermute | solution.py:22
  73.7 0.8 slice_bitcast_fusion.35
  74.6 0.1 collective-permute-start.6
  74.6 1.7 %fusion.21 = f32[256,4,256]{2,0,1:T(8,128)S(1)} fusion(f32[4,768,256]{2,1,0:T(8,128)S(1)} %constant_dynamic-update-slice_fusion, f32[264,1024]{1,0:T(8,128)S(1)} %collective-permute-done.5), kind=kOutput, calls=%fused_computation.41 | convolution fusion | flops 1207959552 | bytes 4980736 | tf_op jit(solution)/shard_map/rb,pba->rpa/dot_general | solution.py:74
  76.4 2.9 %fusion.19 = f32[256,4,256]{2,0,1:T(8,128)S(1)} fusion(f32[4,768,256]{2,1,0:T(8,128)S(1)} %constant_dynamic-update-slice_fusion, f32[264,1024]{1,0:T(8,128)} %collective-permute-done.4), kind=kOutput, calls=%fused_computation.39 | convolution fusion | flops 1207959552 | bytes 4980736 | tf_op jit(solution)/shard_map/rb,pba->rpa/dot_general | solution.py:74
  79.3 1.7 %fusion.17 = f32[256,4,256]{2,0,1:T(8,128)S(1)} fusion(f32[4,768,256]{2,1,0:T(8,128)S(1)} %constant_dynamic-update-slice_fusion, f32[264,1024]{1,0:T(8,128)S(1)} %collective-permute-done.3), kind=kOutput, calls=%fused_computation.37 | convolution fusion | flops 1207959552 | bytes 4980736 | tf_op jit(solution)/shard_map/rb,pba->rpa/dot_general | solution.py:74
  81.0 0.2 broadcast_select_fusion
  81.3 0.3 broadcast_add_fusion.1
  81.6 1.8 %fusion = f32[256,4,256]{2,0,1:T(8,128)S(1)} fusion(f32[256,4,256]{2,0,1:T(8,128)S(1)} %fusion.14, f32[4,768,256]{2,1,0:T(8,128)S(1)} %constant_dynamic-update-slice_fusion, f32[256,2048]{1,0:T(8,128)S(1)} %slice_dynamic-update-slice_fusion.1, s32[]{:T(128)S(6)} %add.263, f32[4]{0:T(128)S(1)} %fusion.39, f32[256,256]{1,0:T(8,128)S(1)} %get-tuple-element.17), kind=kOutput, calls=%fused_computation.5 | convolution fusion | flops 1208745984 | bytes 6291972 | tf_op jit(solution)/shard_map/rb,pba->rpa/dot_general | solution.py:74
  83.4 1.1 fusion.29
  84.6 1.9 %fusion.26 = f32[4,256,768]{2,1,0:T(8,128)S(1)} fusion(f32[256,4,256]{2,0,1:T(8,128)S(1)} %fusion, f32[256,2048]{1,0:T(8,128)S(1)} %slice_dynamic-update-slice_fusion.1, s32[]{:T(128)S(6)} %add.263), kind=kOutput, calls=%fused_computation.46 | convolution fusion | flops 1207959552 | bytes 4980740 | tf_op jit(solution)/shard_map/rc,rpa->pca/dot_general | solution.py:80
  86.4 0.0 copy-start.4
  86.4 1.7 %fusion.25 = f32[256,4,256]{2,0,1:T(8,128)S(1)} fusion(f32[4,768,256]{2,1,0:T(8,128)S(1)} %constant_dynamic-update-slice_fusion, f32[264,1024]{1,0:T(8,128)S(1)} %broadcast_select_fusion), kind=kOutput, calls=%fused_computation.45 | convolution fusion | flops 1207959552 | bytes 4980736 | tf_op jit(solution)/shard_map/rb,pba->rpa/dot_general | solution.py:74
  88.2 0.4 copy-done.4
  88.6 0.8 fusion.1
  89.5 1.3 fusion.28
  90.7 1.7 %fusion.23 = f32[256,4,256]{2,0,1:T(8,128)S(1)} fusion(f32[4,768,256]{2,1,0:T(8,128)S(1)} %constant_dynamic-update-slice_fusion, f32[264,1024]{1,0:T(8,128)S(1)} %collective-permute-done.6), kind=kOutput, calls=%fused_computation.43 | convolution fusion | flops 1207959552 | bytes 4980736 | tf_op jit(solution)/shard_map/rb,pba->rpa/dot_general | solution.py:74
  92.5 0.9 fusion.5
  93.3 1.7 %fusion.20 = f32[4,256,768]{2,1,0:T(8,128)S(1)} fusion(f32[256,4,256]{2,0,1:T(8,128)S(1)} %fusion.5, f32[264,1024]{1,0:T(8,128)S(1)} %collective-permute-done.5), kind=kOutput, calls=%fused_computation.40 | convolution fusion | flops 1207959552 | bytes 4980736 | tf_op jit(solution)/shard_map/rc,rpa->pca/dot_general | solution.py:80
  95.0 1.8 %fusion.7 = f32[256,4,256]{2,0,1:T(8,128)S(1)} fusion(f32[256,4,256]{2,0,1:T(8,128)S(1)} %fusion.19, f32[4,256,1024]{2,1,0:T(8,128)S(1)} %copy-done.4, s32[]{:T(128)S(6)} %select_n.70, f32[256,256]{1,0:T(8,128)S(1)} %get-tuple-element.14, f32[4]{0:T(128)S(1)} %fusion.39, f32[264,1024]{1,0:T(8,128)} %collective-permute-done.4), kind=kOutput, calls=%fused_computation.18 | convolution fusion | flops 403439616 | bytes 3670532 | tf_op jit(solution)/shard_map/rb,pba->rpa/dot_general | solution.py:72
  96.8 2.8 %fusion.18 = f32[4,256,768]{2,1,0:T(8,128)S(1)} fusion(f32[256,4,256]{2,0,1:T(8,128)S(1)} %fusion.7, f32[264,1024]{1,0:T(8,128)} %collective-permute-done.4), kind=kOutput, calls=%fused_computation.38 | convolution fusion | flops 1207959552 | bytes 4980736 | tf_op jit(solution)/shard_map/rc,rpa->pca/dot_general | solution.py:80
  99.7 0.8 fusion.8
  100.5 1.7 %fusion.16 = f32[4,256,768]{2,1,0:T(8,128)S(1)} fusion(f32[256,4,256]{2,0,1:T(8,128)S(1)} %fusion.8, f32[264,1024]{1,0:T(8,128)S(1)} %collective-permute-done.3), kind=kOutput, calls=%fused_computation.36 | convolution fusion | flops 1207959552 | bytes 4980736 | tf_op jit(solution)/shard_map/rc,rpa->pca/dot_general | solution.py:80
  102.2 0.8 fusion.4
  103.0 1.7 %fusion.22 = f32[4,256,768]{2,1,0:T(8,128)S(1)} fusion(f32[256,4,256]{2,0,1:T(8,128)S(1)} %fusion.4, f32[264,1024]{1,0:T(8,128)S(1)} %collective-permute-done.6), kind=kOutput, calls=%fused_computation.42 | convolution fusion | flops 1207959552 | bytes 4980736 | tf_op jit(solution)/shard_map/rc,rpa->pca/dot_general | solution.py:80
  104.8 2.9 %add_bitcast_fusion = f32[4,768,256]{1,2,0:T(8,128)S(1)} fusion(f32[4,256,768]{2,1,0:T(8,128)S(1)} %fusion.22, f32[4,256,768]{2,1,0:T(8,128)S(1)} %fusion.20, f32[4,256,768]{2,1,0:T(8,128)S(1)} %fusion.18, f32[4,256,768]{2,1,0:T(8,128)S(1)} %fusion.26, f32[4,256,768]{2,1,0:T(8,128)S(1)} %fusion.16, f32[256,4,256]{2,0,1:T(8,128)S(1)} %fusion.1, ...), kind=kOutput, calls=%fused_computation.3 | convolution fusion | flops 1211891712 | bytes 20709376 | tf_op jit(solution)/shard_map/rc,rpa->pca/dot_general | solution.py:80
  107.6 0.3 fusion.40
  107.9 0.1 collective-permute-start.11
  108.0 1.7 %collective-permute-start.10 = (f32[4,256,256]{1,2,0:T(8,128)S(1)}, f32[4,256,256]{1,2,0:T(8,128)S(1)}, u32[]{:S(2)}, u32[]{:S(2)}) collective-permute-start(f32[4,256,256]{1,2,0:T(8,128)S(1)} %get-tuple-element.10), channel_id=1, source_target_pairs={{0,2},{1,3},{2,0},{3,1},{4,6},{5,7},{6,4},{7,5},{8,10},{9,11},{10,... | collective-permute-start | bytes 3145736 | tf_op jit(solution)/shard_map/ppermute | solution.py:88
  109.7 0.8 collective-permute-start.9
  110.5 1.0 convolution_add_fusion.7
  111.6 1.0 fusion.27
  112.6 2.0 %fusion.6 = f32[4,256,256]{2,1,0:T(8,128)S(1)} fusion(f32[4,256,256]{2,1,0:T(8,128)S(1)} %fusion.27, f32[4,256,256]{2,1,0:T(8,128)S(1)} %convolution_add_fusion.7, f32[256,4,256]{2,0,1:T(8,128)S(1)} %fusion.7, f32[264,1024]{1,0:T(8,128)} %collective-permute-done.4), kind=kOutput, calls=%fused_computation.16 | convolution fusion | flops 403177472 | bytes 4456448 | tf_op jit(solution)/shard_map/rc,rpa->pca/dot_general | solution.py:91
  114.6 1.0 constant_dynamic-update-slice_fusion.10
  115.7 40.4 %collective-permute-done.9 = f32[4,256,256]{1,2,0:T(8,128)S(1)} collective-permute-done((f32[4,256,256]{1,2,0:T(8,128)S(1)}, f32[4,256,256]{1,2,0:T(8,128)S(1)}, u32[]{:S(2)}, u32[]{:S(2)}) %collective-permute-start.9) | collective-permute-done | bytes 1048608 | tf_op jit(solution)/shard_map/ppermute | solution.py:88
  156.1 0.1 constant_dynamic-update-slice_fusion.9
  156.2 0.1 constant_dynamic-update-slice_fusion.8
  156.3 0.1 constant_dynamic-update-slice_fusion.7
  156.3 0.1 constant_dynamic-update-slice_fusion.6
  156.4 0.1 constant_dynamic-update-slice_fusion.5
  156.5 0.1 constant_dynamic-update-slice_fusion.4
  156.6 0.1 constant_dynamic-update-slice_fusion.3
  156.7 0.0 copy-start.1
  156.7 2.4 %constant_dynamic-slice_fusion = f32[4,256,1024]{1,2,0:T(8,128)} fusion(f32[4,256,2048]{1,2,0:T(8,128)S(1)} %constant_dynamic-update-slice_fusion.3, s32[]{:T(128)S(6)} %select_n.69), kind=kLoop, calls=%fused_computation.106 | loop fusion | bytes 8388612 | tf_op jit(solution)/shard_map/dynamic_slice | solution.py:13
  159.0 5.3 %copy.32 = f32[4,256,1024]{2,1,0:T(8,128)} copy(f32[4,256,1024]{1,2,0:T(8,128)} %constant_dynamic-slice_fusion) | data formatting | bytes 8388608 | tf_op jit(solution)/shard_map/dynamic_slice | solution.py:13
  (51 shorter events, 0.3 us)
Async XLA Ops:
  0.0 13.1 %copy-start = (f32[256]{0:T(256)S(1)}, f32[256]{0:T(256)}, u32[]{:S(2)}) copy-start(f32[256]{0:T(256)} %param.12) | copy-start | bytes 3076
  0.0 8.3 %copy-start.5 = (s32[256]{0:T(256)S(1)}, s32[256]{0:T(256)}, u32[]{:S(2)}) copy-start(s32[256]{0:T(256)} %param.10) | copy-start | bytes 3076
  0.0 8.3 %copy-start.3 = (f32[256,1024]{1,0:T(8,128)S(1)}, f32[256,1024]{1,0:T(8,128)}, u32[]{:S(2)}) copy-start(f32[256,1024]{1,0:T(8,128)} %param.9) | copy-start | bytes 3145732
  3.8 4.7 %copy-start.2 = (f32[1024]{0:T(1024)S(1)}, f32[1024]{0:T(1024)}, u32[]{:S(2)}) copy-start(f32[1024]{0:T(1024)} %param.13) | copy-start | bytes 12292
  3.8 53.7 %collective-permute-start.2 = (f32[4,256,256]{2,1,0:T(8,128)}, f32[4,256,256]{2,1,0:T(8,128)}, u32[]{:S(2)}, u32[]{:S(2)}) collective-permute-start(f32[4,256,256]{2,1,0:T(8,128)} %get-tuple-element.6), channel_id=1, source_target_pairs={{0,3},{1,0},{2,1},{3,2},{4,7},{5,4},{6,5},{7,6},{8,11},{9,8},{10,9... | collective-permute-start | bytes 3145736 | tf_op jit(solution)/shard_map/ppermute | solution.py:54
  4.4 48.1 %collective-permute-start = (f32[4,256,256]{2,1,0:T(8,128)}, f32[4,256,256]{2,1,0:T(8,128)}, u32[]{:S(2)}, u32[]{:S(2)}) collective-permute-start(f32[4,256,256]{2,1,0:T(8,128)} %get-tuple-element.7), channel_id=1, source_target_pairs={{0,1},{1,2},{2,3},{3,0},{4,5},{5,6},{6,7},{7,4},{8,9},{9,10},{10,1... | collective-permute-start | bytes 3145736 | tf_op jit(solution)/shard_map/ppermute | solution.py:54
  6.8 47.1 %collective-permute-start.1 = (f32[4,256,256]{2,1,0:T(8,128)}, f32[4,256,256]{2,1,0:T(8,128)}, u32[]{:S(2)}, u32[]{:S(2)}) collective-permute-start(f32[4,256,256]{2,1,0:T(8,128)} %get-tuple-element.8), channel_id=1, source_target_pairs={{0,2},{1,3},{2,0},{3,1},{4,6},{5,7},{6,4},{7,5},{8,10},{9,11},{10,... | collective-permute-start | bytes 3145736 | tf_op jit(solution)/shard_map/ppermute | solution.py:54
  8.5 4.6 %copy-start.6 = (s32[4,2]{0,1:T(2,128)S(1)}, s32[4,2]{0,1:T(2,128)}, u32[]{:S(2)}) copy-start(s32[4,2]{0,1:T(2,128)} %param.11) | copy-start | bytes 100
  11.4 49.2 %collective-permute-start.5 = (f32[264,1024]{1,0:T(8,128)}, f32[264,1024]{1,0:T(8,128)S(1)}, u32[]{:S(2)}, u32[]{:S(2)}) collective-permute-start(f32[264,1024]{1,0:T(8,128)} %pad_maximum_fusion), channel_id=1, source_target_pairs={{24,0},{0,8},{8,16},{16,24},{12,4},{20,12},{28,20},{4,28},{25,1},{... | collective-permute-start | bytes 3244040 | tf_op jit(solution)/shard_map/ppermute | solution.py:22
  13.0 60.7 %collective-permute-start.4 = (f32[264,1024]{1,0:T(8,128)}, f32[264,1024]{1,0:T(8,128)}, u32[]{:S(2)}, u32[]{:S(2)}) collective-permute-start(f32[264,1024]{1,0:T(8,128)} %pad_maximum_fusion), channel_id=1, source_target_pairs={{28,0},{4,8},{12,16},{20,24},{8,4},{16,12},{24,20},{0,28},{29,1},{... | collective-permute-start | bytes 3244040 | tf_op jit(solution)/shard_map/ppermute | solution.py:22
  52.5 22.0 %collective-permute-start.3 = (f32[264,1024]{1,0:T(8,128)}, f32[264,1024]{1,0:T(8,128)S(1)}, u32[]{:S(2)}, u32[]{:S(2)}) collective-permute-start(f32[264,1024]{1,0:T(8,128)} %pad_maximum_fusion), channel_id=1, source_target_pairs={{0,4},{8,12},{16,20},{24,28},{4,0},{12,8},{20,16},{28,24},{1,5},{9... | collective-permute-start | bytes 3244040 | tf_op jit(solution)/shard_map/ppermute | solution.py:22
  53.8 27.2 %collective-permute-start.8 = (f32[264,1024]{1,0:T(8,128)}, f32[264,1024]{1,0:T(8,128)S(1)}, u32[]{:S(2)}, u32[]{:S(2)}) collective-permute-start(f32[264,1024]{1,0:T(8,128)} %pad_maximum_fusion), channel_id=1, source_target_pairs={{16,4},{24,12},{0,20},{8,28},{17,5},{25,13},{1,21},{9,29},{18,6},{... | collective-permute-start | bytes 3244040 | tf_op jit(solution)/shard_map/ppermute | solution.py:22
  60.6 20.4 %collective-permute-start.7 = (f32[264,1024]{1,0:T(8,128)S(1)}, f32[264,1024]{1,0:T(8,128)S(1)}, u32[]{:S(2)}, u32[]{:S(2)}) collective-permute-start(f32[264,1024]{1,0:T(8,128)S(1)} %collective-permute-done.5), channel_id=1, source_target_pairs={{4,0},{12,8},{20,16},{28,24},{5,1},{13,9},{21,17},{29,25},{6,2},{1... | collective-permute-start | bytes 3244040 | tf_op jit(solution)/shard_map/ppermute | solution.py:22
  74.6 6.7 %collective-permute-start.6 = (f32[264,1024]{1,0:T(8,128)}, f32[264,1024]{1,0:T(8,128)S(1)}, u32[]{:S(2)}, u32[]{:S(2)}) collective-permute-start(f32[264,1024]{1,0:T(8,128)} %collective-permute-done.4), channel_id=1, source_target_pairs={{0,4},{8,12},{16,20},{24,28},{4,0},{12,8},{20,16},{28,24},{1,5},{9... | collective-permute-start | bytes 3244040 | tf_op jit(solution)/shard_map/ppermute | solution.py:22
  86.4 2.2 %copy-start.4 = (f32[4,256,1024]{2,1,0:T(8,128)S(1)}, f32[4,256,1024]{2,1,0:T(8,128)}, u32[]{:S(2)}) copy-start(f32[4,256,1024]{2,1,0:T(8,128)} %param.8) | copy-start | bytes 12582916
  107.9 48.3 %collective-permute-start.11 = (f32[4,256,256]{1,2,0:T(8,128)S(1)}, f32[4,256,256]{1,2,0:T(8,128)S(1)}, u32[]{:S(2)}, u32[]{:S(2)}) collective-permute-start(f32[4,256,256]{1,2,0:T(8,128)S(1)} %get-tuple-element.9), channel_id=1, source_target_pairs={{0,1},{1,2},{2,3},{3,0},{4,5},{5,6},{6,7},{7,4},{8,9},{9,10},{10,1... | collective-permute-start | bytes 3145736 | tf_op jit(solution)/shard_map/ppermute | solution.py:88
  108.0 48.1 %collective-permute-start.10 = (f32[4,256,256]{1,2,0:T(8,128)S(1)}, f32[4,256,256]{1,2,0:T(8,128)S(1)}, u32[]{:S(2)}, u32[]{:S(2)}) collective-permute-start(f32[4,256,256]{1,2,0:T(8,128)S(1)} %get-tuple-element.10), channel_id=1, source_target_pairs={{0,2},{1,3},{2,0},{3,1},{4,6},{5,7},{6,4},{7,5},{8,10},{9,11},{10,... | collective-permute-start | bytes 3145736 | tf_op jit(solution)/shard_map/ppermute | solution.py:88
  109.7 46.3 %collective-permute-start.9 = (f32[4,256,256]{1,2,0:T(8,128)S(1)}, f32[4,256,256]{1,2,0:T(8,128)S(1)}, u32[]{:S(2)}, u32[]{:S(2)}) collective-permute-start(f32[4,256,256]{1,2,0:T(8,128)S(1)} %get-tuple-element.11), channel_id=1, source_target_pairs={{0,3},{1,0},{2,1},{3,2},{4,7},{5,4},{6,5},{7,6},{8,11},{9,8},{10,9... | collective-permute-start | bytes 3145736 | tf_op jit(solution)/shard_map/ppermute | solution.py:88
  156.7 7.7 %copy-start.1 = (f32[256]{0:T(256)S(1)}, f32[256]{0:T(256)}, u32[]{:S(2)}) copy-start(f32[256]{0:T(256)} %param.12) | copy-start | bytes 3076

commit v4 on v3

--- a/solution.py
+++ b/solution.py
@@ -23,7 +23,7 @@
 
     a = perm(packed, [(d - 2, d) for d in even] + [(d + 3, d + 1) for d in even])
     b = perm(packed, [(d - 1, d) for d in even] + [(d + 2, d + 1) for d in even])
-    c = perm(packed, [(d + 4, d + 1) for d in even])
+    c = perm(b, [(d + 3, d + 1) for d in even])
     swap = [(d, d + 1) for d in even] + [(d + 1, d) for d in even]
     e = perm(packed, swap)
     f = perm(b, swap)

time: 165 us -> 162 us (0.982)
  the two profiles are of different devices: /device:TPU:18 before, /device:TPU:0 now
where the time goes in v4:
time: 162 us; the launch traced here: 161 us
  waiting for transfers between devices  78.5 us (48%)
  matrix products  38.7 us (24%)
  starting transfers between devices  21.1 us (13%)
  local copies, waits for them, and re-layouts  20.8 us (13%)
    ppermute x3, waiting for transfers between devices, local(): lax.ppermute(chunk, 'vb', [(i, (i - k) % nv) for i in range(nv)])  40.1 us
    ppermute x3, waiting for transfers between devices, local(): lax.ppermute(send, 'vb', [(i, (i + k) % nv) for i in range(nv)])  36.4 us
    dot_general x6, matrix products, local(): jnp.einsum('rc,rpa->pca', block[:, quarter:], scaled, precision=PREC, pre...  12.7 us
    ppermute x6, starting transfers between devices, perm(): return lax.ppermute(x, 'blk', [(s % nb, t % nb) for s, t in pairs])  12.1 us
    dot_general x6, matrix products, local(): jnp.einsum('rb,pba->rpa', block[:, quarter:], rest, precision=PREC, prefe...  11.6 us
    dynamic_slice x3, local copies, waits for them, and re-layouts, roll_lanes(): return lax.dynamic_slice_in_dim(doubled, (size - shift) % size, size, axis)  8.05 us
    dot_general x6, matrix products, local(): jnp.einsum('rc,rpa->pca', block[:, :quarter], scaled, precision=PREC, pre...  7.47 us
    dot_general x6, matrix products, local(): jnp.einsum('rb,pba->rpa', block[:, :quarter], pieces[0], precision=PREC,...  6.96 us
  transfers between devices with their start and end apart: 12, of which 4 were waited for; matrix products, arithmetic and copies ran while one was open for 14% of the time, Pallas kernels for 0%

profile of v4, /device:TPU:0, one launch (start us, length us, event | category | flops | bytes accessed | tf_op | source)
XLA Modules:
  0.0 161.4 jit_solution(6845981834330771350)
XLA Ops:
  0.0 3.8 %constant_dynamic-slice_fusion.1 = (f32[4,256,256]{2,1,0:T(8,128)}, f32[4,256,256]{2,1,0:T(8,128)}, f32[4,256,256]{2,1,0:T(8,128)}) fusion(f32[4,256,1024]{2,1,0:T(8,128)} %param.8, s32[]{:T(128)S(6)} %select_n.76, s32[]{:T(128)S(6)} %select_n.72, s32[]{:T(128)S(6)} %select_n.74), kind=kLoop, calls=%fused_computation.107 | loop fusion | bytes 6291468 | tf_op jit(solution)/shard_map/dynamic_slice | solution.py:53
  3.8 3.9 %collective-permute-start.2 = (f32[4,256,256]{2,1,0:T(8,128)}, f32[4,256,256]{2,1,0:T(8,128)}, u32[]{:S(2)}, u32[]{:S(2)}) collective-permute-start(f32[4,256,256]{2,1,0:T(8,128)} %get-tuple-element.6), channel_id=1, source_target_pairs={{0,3},{1,0},{2,1},{3,2},{4,7},{5,4},{6,5},{7,6},{8,11},{9,8},{10,9... | collective-permute-start | bytes 3145736 | tf_op jit(solution)/shard_map/ppermute | solution.py:54
  7.8 1.1 collective-permute-start.1
  9.0 0.0 copy-start.6
  9.1 1.4 gather_fusion
  10.6 0.3 constant_dynamic-slice_fusion.4
  10.9 1.1 pad_maximum_fusion
  12.0 1.6 collective-permute-start.5
  13.6 0.8 collective-permute-start.4
  14.4 0.1 dynamic_slice.26
  14.5 0.6 gather_fusion.2
  15.1 0.6 gather_fusion.1
  15.8 1.9 %fusion.14 = f32[256,4,256]{2,0,1:T(8,128)S(1)} fusion(f32[4,256,1024]{2,1,0:T(8,128)} %param.8, s32[]{:T(128)S(6)} %select_n.70, f32[256,2048]{1,0:T(8,128)S(1)} %slice_dynamic-update-slice_fusion.1, s32[]{:T(128)S(6)} %select_n.69), kind=kOutput, calls=%fused_computation.34 | convolution fusion | flops 402653184 | bytes 2359304 | tf_op jit(solution)/shard_map/rb,pba->rpa/dot_general | solution.py:72
  17.6 36.4 %collective-permute-done = f32[4,256,256]{2,1,0:T(8,128)} collective-permute-done((f32[4,256,256]{2,1,0:T(8,128)}, f32[4,256,256]{2,1,0:T(8,128)}, u32[]{:S(2)}, u32[]{:S(2)}) %collective-permute-start) | collective-permute-done | bytes 1048608 | tf_op jit(solution)/shard_map/ppermute | solution.py:54
  54.1 1.3 constant_dynamic-update-slice_fusion.2
  55.4 1.3 constant_dynamic-update-slice_fusion.1
  56.7 1.3 constant_dynamic-update-slice_fusion
  58.0 1.3 collective-permute-start.7
  59.3 2.0 %collective-permute-done.4 = f32[264,1024]{1,0:T(8,128)} collective-permute-done((f32[264,1024]{1,0:T(8,128)}, f32[264,1024]{1,0:T(8,128)}, u32[]{:S(2)}, u32[]{:S(2)}) %collective-permute-start.4) | collective-permute-done | bytes 1081376 | tf_op jit(solution)/shard_map/ppermute | solution.py:22
  61.3 0.9 collective-permute-start.8
  62.2 0.8 slice_bitcast_fusion.35
  63.0 7.5 %collective-permute-start.6 = (f32[264,1024]{1,0:T(8,128)}, f32[264,1024]{1,0:T(8,128)S(1)}, u32[]{:S(2)}, u32[]{:S(2)}) collective-permute-start(f32[264,1024]{1,0:T(8,128)} %collective-permute-done.4), channel_id=1, source_target_pairs={{0,4},{8,12},{16,20},{24,28},{4,0},{12,8},{20,16},{28,24},{1,5},{9... | collective-permute-start | bytes 3244040 | tf_op jit(solution)/shard_map/ppermute | solution.py:22
  70.5 1.7 %fusion.21 = f32[256,4,256]{2,0,1:T(8,128)S(1)} fusion(f32[4,768,256]{2,1,0:T(8,128)S(1)} %constant_dynamic-update-slice_fusion, f32[264,1024]{1,0:T(8,128)S(1)} %collective-permute-done.5), kind=kOutput, calls=%fused_computation.41 | convolution fusion | flops 1207959552 | bytes 4980736 | tf_op jit(solution)/shard_map/rb,pba->rpa/dot_general | solution.py:74
  72.3 2.9 %fusion.19 = f32[256,4,256]{2,0,1:T(8,128)S(1)} fusion(f32[4,768,256]{2,1,0:T(8,128)S(1)} %constant_dynamic-update-slice_fusion, f32[264,1024]{1,0:T(8,128)} %collective-permute-done.4), kind=kOutput, calls=%fused_computation.39 | convolution fusion | flops 1207959552 | bytes 4980736 | tf_op jit(solution)/shard_map/rb,pba->rpa/dot_general | solution.py:74
  75.2 1.7 %fusion.17 = f32[256,4,256]{2,0,1:T(8,128)S(1)} fusion(f32[4,768,256]{2,1,0:T(8,128)S(1)} %constant_dynamic-update-slice_fusion, f32[264,1024]{1,0:T(8,128)S(1)} %collective-permute-done.3), kind=kOutput, calls=%fused_computation.37 | convolution fusion | flops 1207959552 | bytes 4980736 | tf_op jit(solution)/shard_map/rb,pba->rpa/dot_general | solution.py:74
  76.9 0.2 broadcast_select_fusion
  77.2 0.3 broadcast_add_fusion.1
  77.5 1.8 %fusion = f32[256,4,256]{2,0,1:T(8,128)S(1)} fusion(f32[256,4,256]{2,0,1:T(8,128)S(1)} %fusion.14, f32[4,768,256]{2,1,0:T(8,128)S(1)} %constant_dynamic-update-slice_fusion, f32[256,2048]{1,0:T(8,128)S(1)} %slice_dynamic-update-slice_fusion.1, s32[]{:T(128)S(6)} %add.263, f32[4]{0:T(128)S(1)} %fusion.39, f32[256,256]{1,0:T(8,128)S(1)} %get-tuple-element.17), kind=kOutput, calls=%fused_computation.5 | convolution fusion | flops 1208745984 | bytes 6291972 | tf_op jit(solution)/shard_map/rb,pba->rpa/dot_general | solution.py:74
  79.3 1.1 fusion.29
  80.4 1.9 %fusion.26 = f32[4,256,768]{2,1,0:T(8,128)S(1)} fusion(f32[256,4,256]{2,0,1:T(8,128)S(1)} %fusion, f32[256,2048]{1,0:T(8,128)S(1)} %slice_dynamic-update-slice_fusion.1, s32[]{:T(128)S(6)} %add.263), kind=kOutput, calls=%fused_computation.46 | convolution fusion | flops 1207959552 | bytes 4980740 | tf_op jit(solution)/shard_map/rc,rpa->pca/dot_general | solution.py:80
  82.3 1.7 %fusion.25 = f32[256,4,256]{2,0,1:T(8,128)S(1)} fusion(f32[4,768,256]{2,1,0:T(8,128)S(1)} %constant_dynamic-update-slice_fusion, f32[264,1024]{1,0:T(8,128)S(1)} %broadcast_select_fusion), kind=kOutput, calls=%fused_computation.45 | convolution fusion | flops 1207959552 | bytes 4980736 | tf_op jit(solution)/shard_map/rb,pba->rpa/dot_general | solution.py:74
  84.0 0.4 copy-done.4
  84.5 0.8 fusion.1
  85.3 1.3 fusion.28
  86.6 1.7 %fusion.23 = f32[256,4,256]{2,0,1:T(8,128)S(1)} fusion(f32[4,768,256]{2,1,0:T(8,128)S(1)} %constant_dynamic-update-slice_fusion, f32[264,1024]{1,0:T(8,128)S(1)} %collective-permute-done.6), kind=kOutput, calls=%fused_computation.43 | convolution fusion | flops 1207959552 | bytes 4980736 | tf_op jit(solution)/shard_map/rb,pba->rpa/dot_general | solution.py:74
  88.3 0.8 fusion.5
  89.2 1.7 %fusion.20 = f32[4,256,768]{2,1,0:T(8,128)S(1)} fusion(f32[256,4,256]{2,0,1:T(8,128)S(1)} %fusion.5, f32[264,1024]{1,0:T(8,128)S(1)} %collective-permute-done.5), kind=kOutput, calls=%fused_computation.40 | convolution fusion | flops 1207959552 | bytes 4980736 | tf_op jit(solution)/shard_map/rc,rpa->pca/dot_general | solution.py:80
  90.9 1.8 %fusion.7 = f32[256,4,256]{2,0,1:T(8,128)S(1)} fusion(f32[256,4,256]{2,0,1:T(8,128)S(1)} %fusion.19, f32[4,256,1024]{2,1,0:T(8,128)S(1)} %copy-done.4, s32[]{:T(128)S(6)} %select_n.70, f32[256,256]{1,0:T(8,128)S(1)} %get-tuple-element.14, f32[4]{0:T(128)S(1)} %fusion.39, f32[264,1024]{1,0:T(8,128)} %collective-permute-done.4), kind=kOutput, calls=%fused_computation.18 | convolution fusion | flops 403439616 | bytes 3670532 | tf_op jit(solution)/shard_map/rb,pba->rpa/dot_general | solution.py:72
  92.7 2.8 %fusion.18 = f32[4,256,768]{2,1,0:T(8,128)S(1)} fusion(f32[256,4,256]{2,0,1:T(8,128)S(1)} %fusion.7, f32[264,1024]{1,0:T(8,128)} %collective-permute-done.4), kind=kOutput, calls=%fused_computation.38 | convolution fusion | flops 1207959552 | bytes 4980736 | tf_op jit(solution)/shard_map/rc,rpa->pca/dot_general | solution.py:80
  95.5 0.8 fusion.8
  96.4 1.7 %fusion.16 = f32[4,256,768]{2,1,0:T(8,128)S(1)} fusion(f32[256,4,256]{2,0,1:T(8,128)S(1)} %fusion.8, f32[264,1024]{1,0:T(8,128)S(1)} %collective-permute-done.3), kind=kOutput, calls=%fused_computation.36 | convolution fusion | flops 1207959552 | bytes 4980736 | tf_op jit(solution)/shard_map/rc,rpa->pca/dot_general | solution.py:80
  98.1 0.8 fusion.4
  98.9 1.7 %fusion.22 = f32[4,256,768]{2,1,0:T(8,128)S(1)} fusion(f32[256,4,256]{2,0,1:T(8,128)S(1)} %fusion.4, f32[264,1024]{1,0:T(8,128)S(1)} %collective-permute-done.6), kind=kOutput, calls=%fused_computation.42 | convolution fusion | flops 1207959552 | bytes 4980736 | tf_op jit(solution)/shard_map/rc,rpa->pca/dot_general | solution.py:80
  100.6 2.9 %add_bitcast_fusion = f32[4,768,256]{1,2,0:T(8,128)S(1)} fusion(f32[4,256,768]{2,1,0:T(8,128)S(1)} %fusion.22, f32[4,256,768]{2,1,0:T(8,128)S(1)} %fusion.20, f32[4,256,768]{2,1,0:T(8,128)S(1)} %fusion.18, f32[4,256,768]{2,1,0:T(8,128)S(1)} %fusion.26, f32[4,256,768]{2,1,0:T(8,128)S(1)} %fusion.16, f32[256,4,256]{2,0,1:T(8,128)S(1)} %fusion.1, ...), kind=kOutput, calls=%fused_computation.3 | convolution fusion | flops 1211891712 | bytes 20709376 | tf_op jit(solution)/shard_map/rc,rpa->pca/dot_general | solution.py:80
  103.5 0.3 fusion.40
  103.8 2.5 %collective-permute-start.11 = (f32[4,256,256]{1,2,0:T(8,128)S(1)}, f32[4,256,256]{1,2,0:T(8,128)S(1)}, u32[]{:S(2)}, u32[]{:S(2)}) collective-permute-start(f32[4,256,256]{1,2,0:T(8,128)S(1)} %get-tuple-element.9), channel_id=1, source_target_pairs={{0,1},{1,2},{2,3},{3,0},{4,5},{5,6},{6,7},{7,4},{8,9},{9,10},{10,1... | collective-permute-start | bytes 3145736 | tf_op jit(solution)/shard_map/ppermute | solution.py:88
  106.3 0.5 collective-permute-start.10
  106.8 1.0 collective-permute-start.9
  107.8 1.0 convolution_add_fusion.7
  108.9 1.0 fusion.27
  109.9 2.0 %fusion.6 = f32[4,256,256]{2,1,0:T(8,128)S(1)} fusion(f32[4,256,256]{2,1,0:T(8,128)S(1)} %fusion.27, f32[4,256,256]{2,1,0:T(8,128)S(1)} %convolution_add_fusion.7, f32[256,4,256]{2,0,1:T(8,128)S(1)} %fusion.7, f32[264,1024]{1,0:T(8,128)} %collective-permute-done.4), kind=kOutput, calls=%fused_computation.16 | convolution fusion | flops 403177472 | bytes 4456448 | tf_op jit(solution)/shard_map/rc,rpa->pca/dot_general | solution.py:91
  111.9 1.0 constant_dynamic-update-slice_fusion.10
  113.0 35.8 %collective-permute-done.9 = f32[4,256,256]{1,2,0:T(8,128)S(1)} collective-permute-done((f32[4,256,256]{1,2,0:T(8,128)S(1)}, f32[4,256,256]{1,2,0:T(8,128)S(1)}, u32[]{:S(2)}, u32[]{:S(2)}) %collective-permute-start.9) | collective-permute-done | bytes 1048608 | tf_op jit(solution)/shard_map/ppermute | solution.py:88
  148.7 0.1 constant_dynamic-update-slice_fusion.9
  148.8 4.3 %collective-permute-done.10 = f32[4,256,256]{1,2,0:T(8,128)S(1)} collective-permute-done((f32[4,256,256]{1,2,0:T(8,128)S(1)}, f32[4,256,256]{1,2,0:T(8,128)S(1)}, u32[]{:S(2)}, u32[]{:S(2)}) %collective-permute-start.10) | collective-permute-done | bytes 1048608 | tf_op jit(solution)/shard_map/ppermute | solution.py:88
  153.1 0.1 constant_dynamic-update-slice_fusion.8
  153.2 0.1 constant_dynamic-update-slice_fusion.7
  153.3 0.1 constant_dynamic-update-slice_fusion.6
  153.4 0.1 constant_dynamic-update-slice_fusion.5
  153.5 0.1 constant_dynamic-update-slice_fusion.4
  153.6 0.1 constant_dynamic-update-slice_fusion.3
  153.7 0.0 copy-start.1
  153.7 2.4 %constant_dynamic-slice_fusion = f32[4,256,1024]{1,2,0:T(8,128)} fusion(f32[4,256,2048]{1,2,0:T(8,128)S(1)} %constant_dynamic-update-slice_fusion.3, s32[]{:T(128)S(6)} %select_n.69), kind=kLoop, calls=%fused_computation.106 | loop fusion | bytes 8388612 | tf_op jit(solution)/shard_map/dynamic_slice | solution.py:13
  156.0 5.3 %copy.32 = f32[4,256,1024]{2,1,0:T(8,128)} copy(f32[4,256,1024]{1,2,0:T(8,128)} %constant_dynamic-slice_fusion) | data formatting | bytes 8388608 | tf_op jit(solution)/shard_map/dynamic_slice | solution.py:13
  (51 shorter events, 0.3 us)
Async XLA Ops:
  0.0 14.5 %copy-start = (f32[256]{0:T(256)S(1)}, f32[256]{0:T(256)}, u32[]{:S(2)}) copy-start(f32[256]{0:T(256)} %param.12) | copy-start | bytes 3076
  0.0 8.8 %copy-start.5 = (s32[256]{0:T(256)S(1)}, s32[256]{0:T(256)}, u32[]{:S(2)}) copy-start(s32[256]{0:T(256)} %param.10) | copy-start | bytes 3076
  0.0 8.9 %copy-start.3 = (f32[256,1024]{1,0:T(8,128)S(1)}, f32[256,1024]{1,0:T(8,128)}, u32[]{:S(2)}) copy-start(f32[256,1024]{1,0:T(8,128)} %param.9) | copy-start | bytes 3145732
  3.8 5.3 %copy-start.2 = (f32[1024]{0:T(1024)S(1)}, f32[1024]{0:T(1024)}, u32[]{:S(2)}) copy-start(f32[1024]{0:T(1024)} %param.13) | copy-start | bytes 12292
  3.8 52.9 %collective-permute-start.2 = (f32[4,256,256]{2,1,0:T(8,128)}, f32[4,256,256]{2,1,0:T(8,128)}, u32[]{:S(2)}, u32[]{:S(2)}) collective-permute-start(f32[4,256,256]{2,1,0:T(8,128)} %get-tuple-element.6), channel_id=1, source_target_pairs={{0,3},{1,0},{2,1},{3,2},{4,7},{5,4},{6,5},{7,6},{8,11},{9,8},{10,9... | collective-permute-start | bytes 3145736 | tf_op jit(solution)/shard_map/ppermute | solution.py:54
  7.8 46.3 %collective-permute-start = (f32[4,256,256]{2,1,0:T(8,128)}, f32[4,256,256]{2,1,0:T(8,128)}, u32[]{:S(2)}, u32[]{:S(2)}) collective-permute-start(f32[4,256,256]{2,1,0:T(8,128)} %get-tuple-element.7), channel_id=1, source_target_pairs={{0,1},{1,2},{2,3},{3,0},{4,5},{5,6},{6,7},{7,4},{8,9},{9,10},{10,1... | collective-permute-start | bytes 3145736 | tf_op jit(solution)/shard_map/ppermute | solution.py:54
  7.8 47.6 %collective-permute-start.1 = (f32[4,256,256]{2,1,0:T(8,128)}, f32[4,256,256]{2,1,0:T(8,128)}, u32[]{:S(2)}, u32[]{:S(2)}) collective-permute-start(f32[4,256,256]{2,1,0:T(8,128)} %get-tuple-element.8), channel_id=1, source_target_pairs={{0,2},{1,3},{2,0},{3,1},{4,6},{5,7},{6,4},{7,5},{8,10},{9,11},{10,... | collective-permute-start | bytes 3145736 | tf_op jit(solution)/shard_map/ppermute | solution.py:54
  9.0 5.4 %copy-start.6 = (s32[4,2]{0,1:T(2,128)S(1)}, s32[4,2]{0,1:T(2,128)}, u32[]{:S(2)}) copy-start(s32[4,2]{0,1:T(2,128)} %param.11) | copy-start | bytes 100
  12.0 46.0 %collective-permute-start.5 = (f32[264,1024]{1,0:T(8,128)}, f32[264,1024]{1,0:T(8,128)S(1)}, u32[]{:S(2)}, u32[]{:S(2)}) collective-permute-start(f32[264,1024]{1,0:T(8,128)} %pad_maximum_fusion), channel_id=1, source_target_pairs={{24,0},{0,8},{8,16},{16,24},{12,4},{20,12},{28,20},{4,28},{25,1},{... | collective-permute-start | bytes 3244040 | tf_op jit(solution)/shard_map/ppermute | solution.py:22
  13.6 47.7 %collective-permute-start.4 = (f32[264,1024]{1,0:T(8,128)}, f32[264,1024]{1,0:T(8,128)}, u32[]{:S(2)}, u32[]{:S(2)}) collective-permute-start(f32[264,1024]{1,0:T(8,128)} %pad_maximum_fusion), channel_id=1, source_target_pairs={{28,0},{4,8},{12,16},{20,24},{8,4},{16,12},{24,20},{0,28},{29,1},{... | collective-permute-start | bytes 3244040 | tf_op jit(solution)/shard_map/ppermute | solution.py:22
  54.0 8.9 %collective-permute-start.3 = (f32[264,1024]{1,0:T(8,128)}, f32[264,1024]{1,0:T(8,128)S(1)}, u32[]{:S(2)}, u32[]{:S(2)}) collective-permute-start(f32[264,1024]{1,0:T(8,128)} %pad_maximum_fusion), channel_id=1, source_target_pairs={{0,4},{8,12},{16,20},{24,28},{4,0},{12,8},{20,16},{28,24},{1,5},{9... | collective-permute-start | bytes 3244040 | tf_op jit(solution)/shard_map/ppermute | solution.py:22
  58.0 18.9 %collective-permute-start.7 = (f32[264,1024]{1,0:T(8,128)S(1)}, f32[264,1024]{1,0:T(8,128)S(1)}, u32[]{:S(2)}, u32[]{:S(2)}) collective-permute-start(f32[264,1024]{1,0:T(8,128)S(1)} %collective-permute-done.5), channel_id=1, source_target_pairs={{4,0},{12,8},{20,16},{28,24},{5,1},{13,9},{21,17},{29,25},{6,2},{1... | collective-permute-start | bytes 3244040 | tf_op jit(solution)/shard_map/ppermute | solution.py:22
  61.3 15.6 %collective-permute-start.8 = (f32[264,1024]{1,0:T(8,128)}, f32[264,1024]{1,0:T(8,128)S(1)}, u32[]{:S(2)}, u32[]{:S(2)}) collective-permute-start(f32[264,1024]{1,0:T(8,128)} %collective-permute-done.4), channel_id=1, source_target_pairs={{12,4},{20,12},{28,20},{4,28},{13,5},{21,13},{29,21},{5,29},{14,6}... | collective-permute-start | bytes 3244040 | tf_op jit(solution)/shard_map/ppermute | solution.py:22
  63.0 14.1 %collective-permute-start.6 = (f32[264,1024]{1,0:T(8,128)}, f32[264,1024]{1,0:T(8,128)S(1)}, u32[]{:S(2)}, u32[]{:S(2)}) collective-permute-start(f32[264,1024]{1,0:T(8,128)} %collective-permute-done.4), channel_id=1, source_target_pairs={{0,4},{8,12},{16,20},{24,28},{4,0},{12,8},{20,16},{28,24},{1,5},{9... | collective-permute-start | bytes 3244040 | tf_op jit(solution)/shard_map/ppermute | solution.py:22
  82.3 2.2 %copy-start.4 = (f32[4,256,1024]{2,1,0:T(8,128)S(1)}, f32[4,256,1024]{2,1,0:T(8,128)}, u32[]{:S(2)}) copy-start(f32[4,256,1024]{2,1,0:T(8,128)} %param.8) | copy-start | bytes 12582916
  103.8 49.4 %collective-permute-start.11 = (f32[4,256,256]{1,2,0:T(8,128)S(1)}, f32[4,256,256]{1,2,0:T(8,128)S(1)}, u32[]{:S(2)}, u32[]{:S(2)}) collective-permute-start(f32[4,256,256]{1,2,0:T(8,128)S(1)} %get-tuple-element.9), channel_id=1, source_target_pairs={{0,1},{1,2},{2,3},{3,0},{4,5},{5,6},{6,7},{7,4},{8,9},{9,10},{10,1... | collective-permute-start | bytes 3145736 | tf_op jit(solution)/shard_map/ppermute | solution.py:88
  106.3 46.9 %collective-permute-start.10 = (f32[4,256,256]{1,2,0:T(8,128)S(1)}, f32[4,256,256]{1,2,0:T(8,128)S(1)}, u32[]{:S(2)}, u32[]{:S(2)}) collective-permute-start(f32[4,256,256]{1,2,0:T(8,128)S(1)} %get-tuple-element.10), channel_id=1, source_target_pairs={{0,2},{1,3},{2,0},{3,1},{4,6},{5,7},{6,4},{7,5},{8,10},{9,11},{10,... | collective-permute-start | bytes 3145736 | tf_op jit(solution)/shard_map/ppermute | solution.py:88
  106.8 41.9 %collective-permute-start.9 = (f32[4,256,256]{1,2,0:T(8,128)S(1)}, f32[4,256,256]{1,2,0:T(8,128)S(1)}, u32[]{:S(2)}, u32[]{:S(2)}) collective-permute-start(f32[4,256,256]{1,2,0:T(8,128)S(1)} %get-tuple-element.11), channel_id=1, source_target_pairs={{0,3},{1,0},{2,1},{3,2},{4,7},{5,4},{6,5},{7,6},{8,11},{9,8},{10,9... | collective-permute-start | bytes 3145736 | tf_op jit(solution)/shard_map/ppermute | solution.py:88
  153.7 7.7 %copy-start.1 = (f32[256]{0:T(256)S(1)}, f32[256]{0:T(256)}, u32[]{:S(2)}) copy-start(f32[256]{0:T(256)} %param.12) | copy-start | bytes 3076

commit v5 on v4

--- a/solution.py
+++ b/solution.py
@@ -93,8 +93,10 @@
         )
         own = part if own is None else own + part
     received[0] = own
-    gathered = jnp.concatenate(received, axis=2)
-    return roll_lanes(gathered, qstart, 2)
+    out = jnp.zeros(received[0].shape[:2] + (width,), received[0].dtype)
+    for k in range(nv):
+        out = lax.dynamic_update_slice_in_dim(out, received[k], ((q + k) % nv) * quarter, 2)
+    return out
 
 
 def solution(mesh):

time: 162 us -> 162 us (level)
  local copies, waits for them, and re-layouts: 20.8 us -> 25.1 us
  waiting for transfers between devices: 78.5 us -> 74.9 us
    dynamic_slice x3 -> x1, local copies, waits for them, and re-layouts: 8.05 us -> 0.34 us  [roll_lanes(): return lax.dynamic_slice_in_dim(doubled, (size - shift) % size, size, axis)]
    ppermute x0 -> x3, local copies, waits for them, and re-layouts: none -> 4.66 us  [local(): lax.ppermute(chunk, 'vb', [(i, (i - k) % nv) for i in range(nv)])]
    ppermute x3, waiting for transfers between devices: 40.1 us -> 36.5 us  [local(): lax.ppermute(chunk, 'vb', [(i, (i - k) % nv) for i in range(nv)])]
    dynamic_update_slice x0 -> x4, local copies, waits for them, and re-layouts: none -> 3.25 us  [local(): lax.dynamic_update_slice_in_dim(out, received[k], (q + k) % nv * quarter, 2)]
    slice x1, local copies, waits for them, and re-layouts: 0.33 us -> 2.08 us  [local(): chunk = remote[:, (k - 1) * quarter:k * quarter]]
    unnamed x39 -> x35, local copies, waits for them, and re-layouts: 4.48 us -> 6.04 us
  transfers between devices with their start and end apart: 12 -> 12, of which waited for: 4 -> 3; matrix products, arithmetic and copies ran while one was open for 14% -> 18% of each run, Pallas kernels for 0% -> 0%
where the time goes in v5:
time: 162 us
  waiting for transfers between devices  74.9 us (46%)
  matrix products  38.5 us (24%)
  local copies, waits for them, and re-layouts  25.1 us (15%)
  starting transfers between devices  21.1 us (13%)
    ppermute x3, waiting for transfers between devices, local(): lax.ppermute(chunk, 'vb', [(i, (i - k) % nv) for i in range(nv)])  36.5 us
    ppermute x3, waiting for transfers between devices, local(): lax.ppermute(send, 'vb', [(i, (i + k) % nv) for i in range(nv)])  36.5 us
    dot_general x6, matrix products, local(): jnp.einsum('rc,rpa->pca', block[:, quarter:], scaled, precision=PREC, pre...  12.4 us
    ppermute x6, starting transfers between devices, perm(): return lax.ppermute(x, 'blk', [(s % nb, t % nb) for s, t in pairs])  12.2 us
    dot_general x6, matrix products, local(): jnp.einsum('rb,pba->rpa', block[:, quarter:], rest, precision=PREC, prefe...  11.9 us
    dot_general x6, matrix products, local(): jnp.einsum('rc,rpa->pca', block[:, :quarter], scaled, precision=PREC, pre...  7.24 us
    dot_general x6, matrix products, local(): jnp.einsum('rb,pba->rpa', block[:, :quarter], pieces[0], precision=PREC,...  7.01 us
    unnamed x35, local copies, waits for them, and re-layouts  6.04 us
  transfers between devices with their start and end apart: 12, of which 3 were waited for; matrix products, arithmetic and copies ran while one was open for 18% of the time, Pallas kernels for 0%

profile of v5, /device:TPU:0, one launch (start us, length us, event | category | flops | bytes accessed | tf_op | source)
XLA Modules:
  0.0 161.8 jit_solution(10302636780808977837)
XLA Ops:
  0.0 3.8 %constant_dynamic-slice_fusion = (f32[4,256,256]{2,1,0:T(8,128)}, f32[4,256,256]{2,1,0:T(8,128)}, f32[4,256,256]{2,1,0:T(8,128)}) fusion(f32[4,256,1024]{2,1,0:T(8,128)} %param.8, s32[]{:T(128)S(6)} %select_n.89, s32[]{:T(128)S(6)} %select_n.85, s32[]{:T(128)S(6)} %select_n.87), kind=kLoop, calls=%fused_computation.102 | loop fusion | bytes 6291468 | tf_op jit(solution)/shard_map/dynamic_slice | solution.py:53
  3.8 3.9 %collective-permute-start.2 = (f32[4,256,256]{2,1,0:T(8,128)}, f32[4,256,256]{2,1,0:T(8,128)}, u32[]{:S(2)}, u32[]{:S(2)}) collective-permute-start(f32[4,256,256]{2,1,0:T(8,128)} %get-tuple-element.6), channel_id=1, source_target_pairs={{0,3},{1,0},{2,1},{3,2},{4,7},{5,4},{6,5},{7,6},{8,11},{9,8},{10,9... | collective-permute-start | bytes 3145736 | tf_op jit(solution)/shard_map/ppermute | solution.py:54
  7.8 1.1 collective-permute-start.1
  9.1 1.4 gather_fusion
  10.5 0.0 copy-start.7
  10.5 0.3 constant_dynamic-slice_fusion.3
  10.9 1.1 pad_maximum_fusion
  12.0 1.6 collective-permute-start.5
  13.5 0.8 collective-permute-start.4
  14.3 0.1 dynamic_slice.23
  14.4 0.6 gather_fusion.2
  15.1 0.6 gather_fusion.1
  15.7 1.9 %fusion.14 = f32[256,4,256]{2,0,1:T(8,128)S(1)} fusion(f32[4,256,1024]{2,1,0:T(8,128)} %param.8, s32[]{:T(128)S(6)} %select_n.83, f32[256,2048]{1,0:T(8,128)S(1)} %slice_dynamic-update-slice_fusion.1, s32[]{:T(128)S(6)} %select_n.82), kind=kOutput, calls=%fused_computation.34 | convolution fusion | flops 402653184 | bytes 2359304 | tf_op jit(solution)/shard_map/rb,pba->rpa/dot_general | solution.py:72
  17.6 36.5 %collective-permute-done = f32[4,256,256]{2,1,0:T(8,128)} collective-permute-done((f32[4,256,256]{2,1,0:T(8,128)}, f32[4,256,256]{2,1,0:T(8,128)}, u32[]{:S(2)}, u32[]{:S(2)}) %collective-permute-start) | collective-permute-done | bytes 1048608 | tf_op jit(solution)/shard_map/ppermute | solution.py:54
  54.1 1.3 constant_dynamic-update-slice_fusion.2
  55.4 1.3 constant_dynamic-update-slice_fusion.1
  56.7 1.3 constant_dynamic-update-slice_fusion
  58.0 1.3 collective-permute-start.7
  59.3 1.9 %collective-permute-done.4 = f32[264,1024]{1,0:T(8,128)S(1)} collective-permute-done((f32[264,1024]{1,0:T(8,128)}, f32[264,1024]{1,0:T(8,128)S(1)}, u32[]{:S(2)}, u32[]{:S(2)}) %collective-permute-start.4) | collective-permute-done | bytes 1081376 | tf_op jit(solution)/shard_map/ppermute | solution.py:22
  61.2 0.9 collective-permute-start.8
  62.1 0.8 slice_bitcast_fusion.34
  63.0 7.6 %collective-permute-start.6 = (f32[264,1024]{1,0:T(8,128)S(1)}, f32[264,1024]{1,0:T(8,128)S(1)}, u32[]{:S(2)}, u32[]{:S(2)}) collective-permute-start(f32[264,1024]{1,0:T(8,128)S(1)} %collective-permute-done.4), channel_id=1, source_target_pairs={{0,4},{8,12},{16,20},{24,28},{4,0},{12,8},{20,16},{28,24},{1,5},{9... | collective-permute-start | bytes 3244040 | tf_op jit(solution)/shard_map/ppermute | solution.py:22
  70.6 2.9 %fusion.21 = f32[256,4,256]{2,0,1:T(8,128)S(1)} fusion(f32[4,768,256]{2,1,0:T(8,128)S(1)} %constant_dynamic-update-slice_fusion, f32[264,1024]{1,0:T(8,128)} %collective-permute-done.5), kind=kOutput, calls=%fused_computation.41 | convolution fusion | flops 1207959552 | bytes 4980736 | tf_op jit(solution)/shard_map/rb,pba->rpa/dot_general | solution.py:74
  73.5 1.7 %fusion.19 = f32[256,4,256]{2,0,1:T(8,128)S(1)} fusion(f32[4,768,256]{2,1,0:T(8,128)S(1)} %constant_dynamic-update-slice_fusion, f32[264,1024]{1,0:T(8,128)S(1)} %collective-permute-done.4), kind=kOutput, calls=%fused_computation.39 | convolution fusion | flops 1207959552 | bytes 4980736 | tf_op jit(solution)/shard_map/rb,pba->rpa/dot_general | solution.py:74
  75.2 1.7 %fusion.17 = f32[256,4,256]{2,0,1:T(8,128)S(1)} fusion(f32[4,768,256]{2,1,0:T(8,128)S(1)} %constant_dynamic-update-slice_fusion, f32[264,1024]{1,0:T(8,128)S(1)} %collective-permute-done.3), kind=kOutput, calls=%fused_computation.37 | convolution fusion | flops 1207959552 | bytes 4980736 | tf_op jit(solution)/shard_map/rb,pba->rpa/dot_general | solution.py:74
  77.0 0.2 broadcast_select_fusion
  77.3 0.3 broadcast_add_fusion.1
  77.5 1.8 %fusion = f32[256,4,256]{2,0,1:T(8,128)S(1)} fusion(f32[256,4,256]{2,0,1:T(8,128)S(1)} %fusion.14, f32[4,768,256]{2,1,0:T(8,128)S(1)} %constant_dynamic-update-slice_fusion, f32[256,2048]{1,0:T(8,128)S(1)} %slice_dynamic-update-slice_fusion.1, s32[]{:T(128)S(6)} %add.278, f32[4]{0:T(128)S(1)} %fusion.39, f32[256,256]{1,0:T(8,128)S(1)} %get-tuple-element.17), kind=kOutput, calls=%fused_computation.5 | convolution fusion | flops 1208745984 | bytes 6291972 | tf_op jit(solution)/shard_map/rb,pba->rpa/dot_general | solution.py:74
  79.4 1.1 fusion.29
  80.5 1.9 %fusion.26 = f32[4,256,768]{2,1,0:T(8,128)S(1)} fusion(f32[256,4,256]{2,0,1:T(8,128)S(1)} %fusion, f32[256,2048]{1,0:T(8,128)S(1)} %slice_dynamic-update-slice_fusion.1, s32[]{:T(128)S(6)} %add.278), kind=kOutput, calls=%fused_computation.46 | convolution fusion | flops 1207959552 | bytes 4980740 | tf_op jit(solution)/shard_map/rc,rpa->pca/dot_general | solution.py:80
  82.4 0.0 copy-start.5
  82.4 1.7 %fusion.25 = f32[256,4,256]{2,0,1:T(8,128)S(1)} fusion(f32[4,768,256]{2,1,0:T(8,128)S(1)} %constant_dynamic-update-slice_fusion, f32[264,1024]{1,0:T(8,128)S(1)} %broadcast_select_fusion), kind=kOutput, calls=%fused_computation.45 | convolution fusion | flops 1207959552 | bytes 4980736 | tf_op jit(solution)/shard_map/rb,pba->rpa/dot_general | solution.py:74
  84.1 0.4 copy-done.5
  84.6 0.8 fusion.1
  85.4 2.0 %fusion.23 = f32[256,4,256]{2,0,1:T(8,128)S(1)} fusion(f32[4,768,256]{2,1,0:T(8,128)S(1)} %constant_dynamic-update-slice_fusion, f32[264,1024]{1,0:T(8,128)S(1)} %collective-permute-done.6), kind=kOutput, calls=%fused_computation.43 | convolution fusion | flops 1207959552 | bytes 4980736 | tf_op jit(solution)/shard_map/rb,pba->rpa/dot_general | solution.py:74
  87.4 1.8 %fusion.5 = f32[256,4,256]{2,0,1:T(8,128)S(1)} fusion(f32[256,4,256]{2,0,1:T(8,128)S(1)} %fusion.21, f32[4,256,1024]{2,1,0:T(8,128)S(1)} %copy-done.5, s32[]{:T(128)S(6)} %select_n.83, f32[256,256]{1,0:T(8,128)S(1)} %get-tuple-element.15, f32[4]{0:T(128)S(1)} %fusion.39, f32[264,1024]{1,0:T(8,128)} %collective-permute-done.5), kind=kOutput, calls=%fused_computation.14 | convolution fusion | flops 403439616 | bytes 3670532 | tf_op jit(solution)/shard_map/rb,pba->rpa/dot_general | solution.py:72
  89.2 2.8 %fusion.20 = f32[4,256,768]{2,1,0:T(8,128)S(1)} fusion(f32[256,4,256]{2,0,1:T(8,128)S(1)} %fusion.5, f32[264,1024]{1,0:T(8,128)} %collective-permute-done.5), kind=kOutput, calls=%fused_computation.40 | convolution fusion | flops 1207959552 | bytes 4980736 | tf_op jit(solution)/shard_map/rc,rpa->pca/dot_general | solution.py:80
  92.0 0.8 fusion.4
  92.9 1.7 %fusion.22 = f32[4,256,768]{2,1,0:T(8,128)S(1)} fusion(f32[256,4,256]{2,0,1:T(8,128)S(1)} %fusion.4, f32[264,1024]{1,0:T(8,128)S(1)} %collective-permute-done.6), kind=kOutput, calls=%fused_computation.42 | convolution fusion | flops 1207959552 | bytes 4980736 | tf_op jit(solution)/shard_map/rc,rpa->pca/dot_general | solution.py:80
  94.6 0.8 fusion.7
  95.4 1.7 %fusion.18 = f32[4,256,768]{2,1,0:T(8,128)S(1)} fusion(f32[256,4,256]{2,0,1:T(8,128)S(1)} %fusion.7, f32[264,1024]{1,0:T(8,128)S(1)} %collective-permute-done.4), kind=kOutput, calls=%fused_computation.38 | convolution fusion | flops 1207959552 | bytes 4980736 | tf_op jit(solution)/shard_map/rc,rpa->pca/dot_general | solution.py:80
  97.1 0.8 fusion.8
  98.0 1.7 %fusion.16 = f32[4,256,768]{2,1,0:T(8,128)S(1)} fusion(f32[256,4,256]{2,0,1:T(8,128)S(1)} %fusion.8, f32[264,1024]{1,0:T(8,128)S(1)} %collective-permute-done.3), kind=kOutput, calls=%fused_computation.36 | convolution fusion | flops 1207959552 | bytes 4980736 | tf_op jit(solution)/shard_map/rc,rpa->pca/dot_general | solution.py:80
  99.7 2.6 %add_bitcast_fusion = f32[4,768,256]{1,2,0:T(8,128)S(1)} fusion(f32[4,256,768]{2,1,0:T(8,128)S(1)} %fusion.22, f32[4,256,768]{2,1,0:T(8,128)S(1)} %fusion.20, f32[4,256,768]{2,1,0:T(8,128)S(1)} %fusion.18, f32[4,256,768]{2,1,0:T(8,128)S(1)} %fusion.26, f32[4,256,768]{2,1,0:T(8,128)S(1)} %fusion.16, f32[256,4,256]{2,0,1:T(8,128)S(1)} %fusion.1, ...), kind=kOutput, calls=%fused_computation.3 | convolution fusion | flops 1211891712 | bytes 20709376 | tf_op jit(solution)/shard_map/rc,rpa->pca/dot_general | solution.py:80
  102.3 2.1 %fusion.40 = (f32[4,256,256]{1,2,0:T(8,128)}, f32[4,256,256]{1,2,0:T(8,128)}, f32[4,256,256]{1,2,0:T(8,128)}) fusion(f32[4,768,256]{1,2,0:T(8,128)S(1)} %add_bitcast_fusion), kind=kLoop, calls=%fused_computation.111 | loop fusion | bytes 6291456 | tf_op jit(solution)/shard_map/slice | solution.py:87
  104.4 2.4 %collective-permute-start.11 = (f32[4,256,256]{1,2,0:T(8,128)}, f32[4,256,256]{1,2,0:T(8,128)}, u32[]{:S(2)}, u32[]{:S(2)}) collective-permute-start(f32[4,256,256]{1,2,0:T(8,128)} %get-tuple-element.9), channel_id=1, source_target_pairs={{0,1},{1,2},{2,3},{3,0},{4,5},{5,6},{6,7},{7,4},{8,9},{9,10},{10,1... | collective-permute-start | bytes 3145736 | tf_op jit(solution)/shard_map/ppermute | solution.py:88
  106.8 0.5 collective-permute-start.10
  107.3 1.0 collective-permute-start.9
  108.3 2.0 %fusion.27 = f32[4,256,256]{2,1,0:T(8,128)S(1)} fusion(f32[256,4,256]{2,0,1:T(8,128)S(1)} %fusion.5, f32[264,1024]{1,0:T(8,128)} %collective-permute-done.5), kind=kOutput, calls=%fused_computation.62 | convolution fusion | flops 402653184 | bytes 2359296 | tf_op jit(solution)/shard_map/rc,rpa->pca/dot_general | solution.py:91
  110.3 1.0 convolution_add_fusion.7
  111.3 1.0 fusion.6
  112.4 1.0 fusion.28
  113.4 1.1 fusion.3
  114.5 0.3 copy.29
  114.8 0.5 broadcast_in_dim.13
  115.3 0.1 constant_dynamic-update-slice_fusion.6
  115.5 2.0 %copy-done.4 = f32[4,256,1024]{2,1,0:T(8,128)} copy-done((f32[4,256,1024]{2,1,0:T(8,128)}, f32[4,256,1024]{2,1,0:T(8,128)S(1)}, u32[]{:S(2)}) %copy-start.4) | copy-done | bytes 4194328
  117.5 36.5 %collective-permute-done.10 = f32[4,256,256]{1,2,0:T(8,128)} collective-permute-done((f32[4,256,256]{1,2,0:T(8,128)}, f32[4,256,256]{1,2,0:T(8,128)}, u32[]{:S(2)}, u32[]{:S(2)}) %collective-permute-start.10) | collective-permute-done | bytes 1048608 | tf_op jit(solution)/shard_map/ppermute | solution.py:88
  154.0 1.6 copy.37
  155.6 1.6 copy.36
  157.1 1.0 constant_dynamic-update-slice_fusion.5
  158.2 1.0 constant_dynamic-update-slice_fusion.4
  159.2 1.6 copy.38
  160.8 1.0 constant_dynamic-update-slice_fusion.3
  (53 shorter events, 0.3 us)
Async XLA Ops:
  0.0 14.4 %copy-start = (f32[256]{0:T(256)S(1)}, f32[256]{0:T(256)}, u32[]{:S(2)}) copy-start(f32[256]{0:T(256)} %param.12) | copy-start | bytes 3076
  0.0 8.9 %copy-start.6 = (s32[256]{0:T(256)S(1)}, s32[256]{0:T(256)}, u32[]{:S(2)}) copy-start(s32[256]{0:T(256)} %param.10) | copy-start | bytes 3076
  0.0 8.9 %copy-start.3 = (f32[256,1024]{1,0:T(8,128)S(1)}, f32[256,1024]{1,0:T(8,128)}, u32[]{:S(2)}) copy-start(f32[256,1024]{1,0:T(8,128)} %param.9) | copy-start | bytes 3145732
  3.8 5.3 %copy-start.2 = (f32[1024]{0:T(1024)S(1)}, f32[1024]{0:T(1024)}, u32[]{:S(2)}) copy-start(f32[1024]{0:T(1024)} %param.13) | copy-start | bytes 12292
  3.8 52.9 %collective-permute-start.2 = (f32[4,256,256]{2,1,0:T(8,128)}, f32[4,256,256]{2,1,0:T(8,128)}, u32[]{:S(2)}, u32[]{:S(2)}) collective-permute-start(f32[4,256,256]{2,1,0:T(8,128)} %get-tuple-element.6), channel_id=1, source_target_pairs={{0,3},{1,0},{2,1},{3,2},{4,7},{5,4},{6,5},{7,6},{8,11},{9,8},{10,9... | collective-permute-start | bytes 3145736 | tf_op jit(solution)/shard_map/ppermute | solution.py:54
  7.8 46.3 %collective-permute-start = (f32[4,256,256]{2,1,0:T(8,128)}, f32[4,256,256]{2,1,0:T(8,128)}, u32[]{:S(2)}, u32[]{:S(2)}) collective-permute-start(f32[4,256,256]{2,1,0:T(8,128)} %get-tuple-element.7), channel_id=1, source_target_pairs={{0,1},{1,2},{2,3},{3,0},{4,5},{5,6},{6,7},{7,4},{8,9},{9,10},{10,1... | collective-permute-start | bytes 3145736 | tf_op jit(solution)/shard_map/ppermute | solution.py:54
  7.8 47.6 %collective-permute-start.1 = (f32[4,256,256]{2,1,0:T(8,128)}, f32[4,256,256]{2,1,0:T(8,128)}, u32[]{:S(2)}, u32[]{:S(2)}) collective-permute-start(f32[4,256,256]{2,1,0:T(8,128)} %get-tuple-element.8), channel_id=1, source_target_pairs={{0,2},{1,3},{2,0},{3,1},{4,6},{5,7},{6,4},{7,5},{8,10},{9,11},{10,... | collective-permute-start | bytes 3145736 | tf_op jit(solution)/shard_map/ppermute | solution.py:54
  10.5 3.9 %copy-start.7 = (s32[4,2]{0,1:T(2,128)S(1)}, s32[4,2]{0,1:T(2,128)}, u32[]{:S(2)}) copy-start(s32[4,2]{0,1:T(2,128)} %param.11) | copy-start | bytes 100
  12.0 46.0 %collective-permute-start.5 = (f32[264,1024]{1,0:T(8,128)}, f32[264,1024]{1,0:T(8,128)}, u32[]{:S(2)}, u32[]{:S(2)}) collective-permute-start(f32[264,1024]{1,0:T(8,128)} %pad_maximum_fusion), channel_id=1, source_target_pairs={{24,0},{0,8},{8,16},{16,24},{12,4},{20,12},{28,20},{4,28},{25,1},{... | collective-permute-start | bytes 3244040 | tf_op jit(solution)/shard_map/ppermute | solution.py:22
  13.5 47.7 %collective-permute-start.4 = (f32[264,1024]{1,0:T(8,128)}, f32[264,1024]{1,0:T(8,128)S(1)}, u32[]{:S(2)}, u32[]{:S(2)}) collective-permute-start(f32[264,1024]{1,0:T(8,128)} %pad_maximum_fusion), channel_id=1, source_target_pairs={{28,0},{4,8},{12,16},{20,24},{8,4},{16,12},{24,20},{0,28},{29,1},{... | collective-permute-start | bytes 3244040 | tf_op jit(solution)/shard_map/ppermute | solution.py:22
  54.0 8.8 %collective-permute-start.3 = (f32[264,1024]{1,0:T(8,128)}, f32[264,1024]{1,0:T(8,128)S(1)}, u32[]{:S(2)}, u32[]{:S(2)}) collective-permute-start(f32[264,1024]{1,0:T(8,128)} %pad_maximum_fusion), channel_id=1, source_target_pairs={{0,4},{8,12},{16,20},{24,28},{4,0},{12,8},{20,16},{28,24},{1,5},{9... | collective-permute-start | bytes 3244040 | tf_op jit(solution)/shard_map/ppermute | solution.py:22
  58.0 19.0 %collective-permute-start.7 = (f32[264,1024]{1,0:T(8,128)}, f32[264,1024]{1,0:T(8,128)S(1)}, u32[]{:S(2)}, u32[]{:S(2)}) collective-permute-start(f32[264,1024]{1,0:T(8,128)} %collective-permute-done.5), channel_id=1, source_target_pairs={{4,0},{12,8},{20,16},{28,24},{5,1},{13,9},{21,17},{29,25},{6,2},{1... | collective-permute-start | bytes 3244040 | tf_op jit(solution)/shard_map/ppermute | solution.py:22
  61.2 15.8 %collective-permute-start.8 = (f32[264,1024]{1,0:T(8,128)S(1)}, f32[264,1024]{1,0:T(8,128)S(1)}, u32[]{:S(2)}, u32[]{:S(2)}) collective-permute-start(f32[264,1024]{1,0:T(8,128)S(1)} %collective-permute-done.4), channel_id=1, source_target_pairs={{12,4},{20,12},{28,20},{4,28},{13,5},{21,13},{29,21},{5,29},{14,6}... | collective-permute-start | bytes 3244040 | tf_op jit(solution)/shard_map/ppermute | solution.py:22
  63.0 14.2 %collective-permute-start.6 = (f32[264,1024]{1,0:T(8,128)S(1)}, f32[264,1024]{1,0:T(8,128)S(1)}, u32[]{:S(2)}, u32[]{:S(2)}) collective-permute-start(f32[264,1024]{1,0:T(8,128)S(1)} %collective-permute-done.4), channel_id=1, source_target_pairs={{0,4},{8,12},{16,20},{24,28},{4,0},{12,8},{20,16},{28,24},{1,5},{9... | collective-permute-start | bytes 3244040 | tf_op jit(solution)/shard_map/ppermute | solution.py:22
  82.4 2.2 %copy-start.5 = (f32[4,256,1024]{2,1,0:T(8,128)S(1)}, f32[4,256,1024]{2,1,0:T(8,128)}, u32[]{:S(2)}) copy-start(f32[4,256,1024]{2,1,0:T(8,128)} %param.8) | copy-start | bytes 12582916
  104.4 54.8 %collective-permute-start.11 = (f32[4,256,256]{1,2,0:T(8,128)}, f32[4,256,256]{1,2,0:T(8,128)}, u32[]{:S(2)}, u32[]{:S(2)}) collective-permute-start(f32[4,256,256]{1,2,0:T(8,128)} %get-tuple-element.9), channel_id=1, source_target_pairs={{0,1},{1,2},{2,3},{3,0},{4,5},{5,6},{6,7},{7,4},{8,9},{9,10},{10,1... | collective-permute-start | bytes 3145736 | tf_op jit(solution)/shard_map/ppermute | solution.py:88
  106.8 47.2 %collective-permute-start.10 = (f32[4,256,256]{1,2,0:T(8,128)}, f32[4,256,256]{1,2,0:T(8,128)}, u32[]{:S(2)}, u32[]{:S(2)}) collective-permute-start(f32[4,256,256]{1,2,0:T(8,128)} %get-tuple-element.10), channel_id=1, source_target_pairs={{0,2},{1,3},{2,0},{3,1},{4,6},{5,7},{6,4},{7,5},{8,10},{9,11},{10,... | collective-permute-start | bytes 3145736 | tf_op jit(solution)/shard_map/ppermute | solution.py:88
  107.3 48.2 %collective-permute-start.9 = (f32[4,256,256]{1,2,0:T(8,128)}, f32[4,256,256]{1,2,0:T(8,128)}, u32[]{:S(2)}, u32[]{:S(2)}) collective-permute-start(f32[4,256,256]{1,2,0:T(8,128)} %get-tuple-element.11), channel_id=1, source_target_pairs={{0,3},{1,0},{2,1},{3,2},{4,7},{5,4},{6,5},{7,6},{8,11},{9,8},{10,9... | collective-permute-start | bytes 3145736 | tf_op jit(solution)/shard_map/ppermute | solution.py:88
  115.5 2.0 %copy-start.4 = (f32[4,256,1024]{2,1,0:T(8,128)}, f32[4,256,1024]{2,1,0:T(8,128)S(1)}, u32[]{:S(2)}) copy-start(f32[4,256,1024]{2,1,0:T(8,128)S(1)} %constant_dynamic-update-slice_fusion.6) | copy-start | bytes 12582916
  158.2 3.7 %copy-start.1 = (f32[256]{0:T(256)S(1)}, f32[256]{0:T(256)}, u32[]{:S(2)}) copy-start(f32[256]{0:T(256)} %param.12) | copy-start | bytes 3076

commit v6 on v4

--- a/solution.py
+++ b/solution.py
@@ -1,6 +1,7 @@
 import jax
 import jax.numpy as jnp
 from jax import lax
+from jax.experimental.layout import Layout, with_layout_constraint
 from jax.sharding import PartitionSpec as P
 
 HOPS = 5
@@ -81,6 +82,7 @@
             "rc,rpa->pca", block[:, quarter:], scaled, precision=PREC, preferred_element_type=jnp.float32
         )
         remote = part if remote is None else remote + part
+    remote = with_layout_constraint(remote, Layout(major_to_minor=(0, 1, 2)))
 
     received = [None] * nv
     for k in range(1, nv):
@@ -92,7 +94,7 @@
             "rc,rpa->pca", block[:, :quarter], scaled, precision=PREC, preferred_element_type=jnp.float32
         )
         own = part if own is None else own + part
-    received[0] = own
+    received[0] = with_layout_constraint(own, Layout(major_to_minor=(0, 1, 2)))
     gathered = jnp.concatenate(received, axis=2)
     return roll_lanes(gathered, qstart, 2)
 

time: 162 us -> 156 us (0.963)
  local copies, waits for them, and re-layouts: 20.8 us -> 16.6 us
  matrix products: 38.7 us -> 35.7 us
    dynamic_slice x3 -> x2, local copies, waits for them, and re-layouts: 8.05 us -> 3.51 us  [roll_lanes(): return lax.dynamic_slice_in_dim(doubled, (size - shift) % size, size, axis)]
    dot_general x6, matrix products: 7.47 us -> 5.14 us  [local(): jnp.einsum('rc,rpa->pca', block[:, :quarter], scaled, precision=PREC, pre...]
where the time goes in v6:
time: 156 us; the launch traced here: 155 us
  waiting for transfers between devices  79.7 us (51%)
  matrix products  35.7 us (23%)
  starting transfers between devices  21.1 us (14%)
  local copies, waits for them, and re-layouts  16.6 us (11%)
  other arithmetic  1.59 us (1%)
    ppermute x3, waiting for transfers between devices, local(): lax.ppermute(chunk, 'vb', [(i, (i - k) % nv) for i in range(nv)])  41.3 us
    ppermute x3, waiting for transfers between devices, local(): lax.ppermute(send, 'vb', [(i, (i + k) % nv) for i in range(nv)])  36.4 us
    ppermute x6, starting transfers between devices, perm(): return lax.ppermute(x, 'blk', [(s % nb, t % nb) for s, t in pairs])  12.1 us
    dot_general x6, matrix products, local(): jnp.einsum('rb,pba->rpa', block[:, quarter:], rest, precision=PREC, prefe...  11.8 us
    dot_general x6, matrix products, local(): jnp.einsum('rc,rpa->pca', block[:, quarter:], scaled, precision=PREC, pre...  11.8 us
    dot_general x6, matrix products, local(): jnp.einsum('rb,pba->rpa', block[:, :quarter], pieces[0], precision=PREC,...  6.96 us
    dot_general x6, matrix products, local(): jnp.einsum('rc,rpa->pca', block[:, :quarter], scaled, precision=PREC, pre...  5.14 us
    ppermute x3, starting transfers between devices, local(): lax.ppermute(send, 'vb', [(i, (i + k) % nv) for i in range(nv)])  5.03 us
  transfers between devices with their start and end apart: 12, of which 4 were waited for; matrix products, arithmetic and copies ran while one was open for 14% of the time, Pallas kernels for 0%

profile of v6, /device:TPU:0, one launch (start us, length us, event | category | flops | bytes accessed | tf_op | source)
XLA Modules:
  0.0 155.4 jit_solution(14125456612582720289)
XLA Ops:
  0.0 3.8 %constant_dynamic-slice_fusion.1 = (f32[4,256,256]{2,1,0:T(8,128)}, f32[4,256,256]{2,1,0:T(8,128)}, f32[4,256,256]{2,1,0:T(8,128)}) fusion(f32[4,256,1024]{2,1,0:T(8,128)} %param.8, s32[]{:T(128)S(6)} %select_n.76, s32[]{:T(128)S(6)} %select_n.72, s32[]{:T(128)S(6)} %select_n.74), kind=kLoop, calls=%fused_computation.107 | loop fusion | bytes 6291468 | tf_op jit(solution)/shard_map/dynamic_slice | solution.py:54
  3.8 3.9 %collective-permute-start.2 = (f32[4,256,256]{2,1,0:T(8,128)}, f32[4,256,256]{2,1,0:T(8,128)}, u32[]{:S(2)}, u32[]{:S(2)}) collective-permute-start(f32[4,256,256]{2,1,0:T(8,128)} %get-tuple-element.6), channel_id=1, source_target_pairs={{0,3},{1,0},{2,1},{3,2},{4,7},{5,4},{6,5},{7,6},{8,11},{9,8},{10,9... | collective-permute-start | bytes 3145736 | tf_op jit(solution)/shard_map/ppermute | solution.py:55
  7.8 1.1 collective-permute-start.1
  9.1 1.4 gather_fusion
  10.5 0.0 copy-start.6
  10.6 0.3 constant_dynamic-slice_fusion.4
  10.9 1.1 pad_maximum_fusion
  12.0 1.6 %collective-permute-start.5 = (f32[264,1024]{1,0:T(8,128)}, f32[264,1024]{1,0:T(8,128)S(1)}, u32[]{:S(2)}, u32[]{:S(2)}) collective-permute-start(f32[264,1024]{1,0:T(8,128)} %pad_maximum_fusion), channel_id=1, source_target_pairs={{24,0},{0,8},{8,16},{16,24},{12,4},{20,12},{28,20},{4,28},{25,1},{... | collective-permute-start | bytes 3244040 | tf_op jit(solution)/shard_map/ppermute | solution.py:23
  13.6 0.8 collective-permute-start.4
  14.4 0.1 dynamic_slice.26
  14.5 0.6 gather_fusion.2
  15.1 0.6 gather_fusion.1
  15.8 1.9 %fusion.14 = f32[256,4,256]{2,0,1:T(8,128)S(1)} fusion(f32[4,256,1024]{2,1,0:T(8,128)} %param.8, s32[]{:T(128)S(6)} %select_n.70, f32[256,2048]{1,0:T(8,128)S(1)} %slice_dynamic-update-slice_fusion.1, s32[]{:T(128)S(6)} %select_n.69), kind=kOutput, calls=%fused_computation.34 | convolution fusion | flops 402653184 | bytes 2359304 | tf_op jit(solution)/shard_map/rb,pba->rpa/dot_general | solution.py:73
  17.6 36.4 %collective-permute-done = f32[4,256,256]{2,1,0:T(8,128)} collective-permute-done((f32[4,256,256]{2,1,0:T(8,128)}, f32[4,256,256]{2,1,0:T(8,128)}, u32[]{:S(2)}, u32[]{:S(2)}) %collective-permute-start) | collective-permute-done | bytes 1048608 | tf_op jit(solution)/shard_map/ppermute | solution.py:55
  54.1 1.3 constant_dynamic-update-slice_fusion.2
  55.4 1.3 constant_dynamic-update-slice_fusion.1
  56.7 1.3 constant_dynamic-update-slice_fusion
  58.0 1.3 collective-permute-start.7
  59.3 2.0 %collective-permute-done.4 = f32[264,1024]{1,0:T(8,128)} collective-permute-done((f32[264,1024]{1,0:T(8,128)}, f32[264,1024]{1,0:T(8,128)}, u32[]{:S(2)}, u32[]{:S(2)}) %collective-permute-start.4) | collective-permute-done | bytes 1081376 | tf_op jit(solution)/shard_map/ppermute | solution.py:23
  61.3 0.9 collective-permute-start.8
  62.2 0.8 slice_bitcast_fusion.35
  63.0 7.5 %collective-permute-start.6 = (f32[264,1024]{1,0:T(8,128)}, f32[264,1024]{1,0:T(8,128)S(1)}, u32[]{:S(2)}, u32[]{:S(2)}) collective-permute-start(f32[264,1024]{1,0:T(8,128)} %collective-permute-done.4), channel_id=1, source_target_pairs={{0,4},{8,12},{16,20},{24,28},{4,0},{12,8},{20,16},{28,24},{1,5},{9... | collective-permute-start | bytes 3244040 | tf_op jit(solution)/shard_map/ppermute | solution.py:23
  70.5 1.7 %fusion.21 = f32[256,4,256]{2,0,1:T(8,128)S(1)} fusion(f32[4,768,256]{2,1,0:T(8,128)S(1)} %constant_dynamic-update-slice_fusion, f32[264,1024]{1,0:T(8,128)S(1)} %collective-permute-done.5), kind=kOutput, calls=%fused_computation.41 | convolution fusion | flops 1207959552 | bytes 4980736 | tf_op jit(solution)/shard_map/rb,pba->rpa/dot_general | solution.py:75
  72.3 2.9 %fusion.19 = f32[256,4,256]{2,0,1:T(8,128)S(1)} fusion(f32[4,768,256]{2,1,0:T(8,128)S(1)} %constant_dynamic-update-slice_fusion, f32[264,1024]{1,0:T(8,128)} %collective-permute-done.4), kind=kOutput, calls=%fused_computation.39 | convolution fusion | flops 1207959552 | bytes 4980736 | tf_op jit(solution)/shard_map/rb,pba->rpa/dot_general | solution.py:75
  75.2 1.7 %fusion.17 = f32[256,4,256]{2,0,1:T(8,128)S(1)} fusion(f32[4,768,256]{2,1,0:T(8,128)S(1)} %constant_dynamic-update-slice_fusion, f32[264,1024]{1,0:T(8,128)S(1)} %collective-permute-done.3), kind=kOutput, calls=%fused_computation.37 | convolution fusion | flops 1207959552 | bytes 4980736 | tf_op jit(solution)/shard_map/rb,pba->rpa/dot_general | solution.py:75
  76.9 0.2 broadcast_select_fusion
  77.2 0.3 broadcast_add_fusion.1
  77.5 1.8 %fusion = f32[256,4,256]{2,0,1:T(8,128)S(1)} fusion(f32[256,4,256]{2,0,1:T(8,128)S(1)} %fusion.14, f32[4,768,256]{2,1,0:T(8,128)S(1)} %constant_dynamic-update-slice_fusion, f32[256,2048]{1,0:T(8,128)S(1)} %slice_dynamic-update-slice_fusion.1, s32[]{:T(128)S(6)} %add.263, f32[4]{0:T(128)S(1)} %fusion.39, f32[256,256]{1,0:T(8,128)S(1)} %get-tuple-element.17), kind=kOutput, calls=%fused_computation.5 | convolution fusion | flops 1208745984 | bytes 6291972 | tf_op jit(solution)/shard_map/rb,pba->rpa/dot_general | solution.py:75
  79.3 0.7 fusion.29
  80.0 1.7 %fusion.26 = f32[4,256,768]{1,2,0:T(8,128)S(1)} fusion(f32[256,4,256]{2,0,1:T(8,128)S(1)} %fusion, f32[256,2048]{1,0:T(8,128)S(1)} %slice_dynamic-update-slice_fusion.1, s32[]{:T(128)S(6)} %add.263), kind=kOutput, calls=%fused_computation.46 | convolution fusion | flops 1207959552 | bytes 4980740 | tf_op jit(solution)/shard_map/rc,rpa->pca/dot_general | solution.py:81
  81.7 0.0 copy-start.4
  81.8 1.7 %fusion.25 = f32[256,4,256]{2,0,1:T(8,128)S(1)} fusion(f32[4,768,256]{2,1,0:T(8,128)S(1)} %constant_dynamic-update-slice_fusion, f32[264,1024]{1,0:T(8,128)S(1)} %broadcast_select_fusion), kind=kOutput, calls=%fused_computation.45 | convolution fusion | flops 1207959552 | bytes 4980736 | tf_op jit(solution)/shard_map/rb,pba->rpa/dot_general | solution.py:75
  83.5 0.4 copy-done.4
  83.9 0.8 fusion.1
  84.8 0.6 fusion.28
  85.4 1.9 %fusion.23 = f32[256,4,256]{2,0,1:T(8,128)S(1)} fusion(f32[4,768,256]{2,1,0:T(8,128)S(1)} %constant_dynamic-update-slice_fusion, f32[264,1024]{1,0:T(8,128)S(1)} %collective-permute-done.6), kind=kOutput, calls=%fused_computation.43 | convolution fusion | flops 1207959552 | bytes 4980736 | tf_op jit(solution)/shard_map/rb,pba->rpa/dot_general | solution.py:75
  87.3 0.8 fusion.5
  88.2 1.5 fusion.20
  89.7 1.8 %fusion.7 = f32[256,4,256]{2,0,1:T(8,128)S(1)} fusion(f32[256,4,256]{2,0,1:T(8,128)S(1)} %fusion.19, f32[4,256,1024]{2,1,0:T(8,128)S(1)} %copy-done.4, s32[]{:T(128)S(6)} %select_n.70, f32[256,256]{1,0:T(8,128)S(1)} %get-tuple-element.14, f32[4]{0:T(128)S(1)} %fusion.39, f32[264,1024]{1,0:T(8,128)} %collective-permute-done.4), kind=kOutput, calls=%fused_computation.18 | convolution fusion | flops 403439616 | bytes 3670532 | tf_op jit(solution)/shard_map/rb,pba->rpa/dot_general | solution.py:73
  91.5 2.6 %fusion.18 = f32[4,256,768]{1,2,0:T(8,128)S(1)} fusion(f32[256,4,256]{2,0,1:T(8,128)S(1)} %fusion.7, f32[264,1024]{1,0:T(8,128)} %collective-permute-done.4), kind=kOutput, calls=%fused_computation.38 | convolution fusion | flops 1207959552 | bytes 4980736 | tf_op jit(solution)/shard_map/rc,rpa->pca/dot_general | solution.py:81
  94.2 0.8 fusion.8
  95.0 1.5 fusion.16
  96.5 0.8 fusion.4
  97.3 1.5 fusion.22
  98.8 2.9 %add_bitcast_fusion = f32[4,768,256]{2,1,0:T(8,128)S(1)} fusion(f32[4,256,768]{1,2,0:T(8,128)S(1)} %fusion.22, f32[4,256,768]{1,2,0:T(8,128)S(1)} %fusion.20, f32[4,256,768]{1,2,0:T(8,128)S(1)} %fusion.18, f32[4,256,768]{1,2,0:T(8,128)S(1)} %fusion.26, f32[4,256,768]{1,2,0:T(8,128)S(1)} %fusion.16, f32[256,4,256]{2,0,1:T(8,128)S(1)} %fusion.1, ...), kind=kOutput, calls=%fused_computation.3 | convolution fusion | flops 1211891712 | bytes 20709376 | tf_op jit(solution)/shard_map/rc,rpa->pca/dot_general | solution.py:81
  101.7 0.2 fusion.40
  102.0 2.5 %collective-permute-start.11 = (f32[4,256,256]{2,1,0:T(8,128)S(1)}, f32[4,256,256]{2,1,0:T(8,128)S(1)}, u32[]{:S(2)}, u32[]{:S(2)}) collective-permute-start(f32[4,256,256]{2,1,0:T(8,128)S(1)} %get-tuple-element.9), channel_id=1, source_target_pairs={{0,1},{1,2},{2,3},{3,0},{4,5},{5,6},{6,7},{7,4},{8,9},{9,10},{10,1... | collective-permute-start | bytes 3145736 | tf_op jit(solution)/shard_map/ppermute | solution.py:90
  104.5 0.5 collective-permute-start.10
  105.0 1.0 collective-permute-start.9
  106.0 0.6 convolution_add_fusion.7
  106.6 0.6 fusion.27
  107.3 1.7 %fusion.6 = f32[4,256,256]{1,2,0:T(8,128)S(1)} fusion(f32[4,256,256]{1,2,0:T(8,128)S(1)} %fusion.27, f32[4,256,256]{1,2,0:T(8,128)S(1)} %convolution_add_fusion.7, f32[256,4,256]{2,0,1:T(8,128)S(1)} %fusion.7, f32[264,1024]{1,0:T(8,128)} %collective-permute-done.4), kind=kOutput, calls=%fused_computation.16 | convolution fusion | flops 403177472 | bytes 4456448 | tf_op jit(solution)/shard_map/rc,rpa->pca/dot_general | solution.py:93
  109.0 0.8 constant_dynamic-update-slice_fusion.10
  109.8 37.0 %collective-permute-done.9 = f32[4,256,256]{2,1,0:T(8,128)S(1)} collective-permute-done((f32[4,256,256]{2,1,0:T(8,128)S(1)}, f32[4,256,256]{2,1,0:T(8,128)S(1)}, u32[]{:S(2)}, u32[]{:S(2)}) %collective-permute-start.9) | collective-permute-done | bytes 1048608 | tf_op jit(solution)/shard_map/ppermute | solution.py:90
  146.9 0.1 constant_dynamic-update-slice_fusion.9
  147.0 4.3 %collective-permute-done.10 = f32[4,256,256]{2,1,0:T(8,128)S(1)} collective-permute-done((f32[4,256,256]{2,1,0:T(8,128)S(1)}, f32[4,256,256]{2,1,0:T(8,128)S(1)}, u32[]{:S(2)}, u32[]{:S(2)}) %collective-permute-start.10) | collective-permute-done | bytes 1048608 | tf_op jit(solution)/shard_map/ppermute | solution.py:90
  151.3 0.1 constant_dynamic-update-slice_fusion.8
  151.5 0.1 constant_dynamic-update-slice_fusion.7
  151.6 0.2 constant_dynamic-update-slice_fusion.6
  151.8 0.2 constant_dynamic-update-slice_fusion.5
  151.9 0.2 constant_dynamic-update-slice_fusion.4
  152.1 0.1 constant_dynamic-update-slice_fusion.3
  152.2 0.0 copy-start.1
  152.2 3.2 %constant_dynamic-slice_fusion = f32[4,256,1024]{2,1,0:T(8,128)} fusion(f32[4,256,2048]{2,1,0:T(8,128)S(1)} %constant_dynamic-update-slice_fusion.3, s32[]{:T(128)S(6)} %select_n.69), kind=kLoop, calls=%fused_computation.106 | loop fusion | bytes 8388612 | tf_op jit(solution)/shard_map/dynamic_slice | solution.py:14
  (50 shorter events, 0.3 us)
Async XLA Ops:
  0.0 14.5 %copy-start = (f32[256]{0:T(256)S(1)}, f32[256]{0:T(256)}, u32[]{:S(2)}) copy-start(f32[256]{0:T(256)} %param.12) | copy-start | bytes 3076
  0.0 8.8 %copy-start.5 = (s32[256]{0:T(256)S(1)}, s32[256]{0:T(256)}, u32[]{:S(2)}) copy-start(s32[256]{0:T(256)} %param.10) | copy-start | bytes 3076
  0.0 8.9 %copy-start.3 = (f32[256,1024]{1,0:T(8,128)S(1)}, f32[256,1024]{1,0:T(8,128)}, u32[]{:S(2)}) copy-start(f32[256,1024]{1,0:T(8,128)} %param.9) | copy-start | bytes 3145732
  3.8 5.3 %copy-start.2 = (f32[1024]{0:T(1024)S(1)}, f32[1024]{0:T(1024)}, u32[]{:S(2)}) copy-start(f32[1024]{0:T(1024)} %param.13) | copy-start | bytes 12292
  3.8 52.9 %collective-permute-start.2 = (f32[4,256,256]{2,1,0:T(8,128)}, f32[4,256,256]{2,1,0:T(8,128)}, u32[]{:S(2)}, u32[]{:S(2)}) collective-permute-start(f32[4,256,256]{2,1,0:T(8,128)} %get-tuple-element.6), channel_id=1, source_target_pairs={{0,3},{1,0},{2,1},{3,2},{4,7},{5,4},{6,5},{7,6},{8,11},{9,8},{10,9... | collective-permute-start | bytes 3145736 | tf_op jit(solution)/shard_map/ppermute | solution.py:55
  7.8 46.3 %collective-permute-start = (f32[4,256,256]{2,1,0:T(8,128)}, f32[4,256,256]{2,1,0:T(8,128)}, u32[]{:S(2)}, u32[]{:S(2)}) collective-permute-start(f32[4,256,256]{2,1,0:T(8,128)} %get-tuple-element.7), channel_id=1, source_target_pairs={{0,1},{1,2},{2,3},{3,0},{4,5},{5,6},{6,7},{7,4},{8,9},{9,10},{10,1... | collective-permute-start | bytes 3145736 | tf_op jit(solution)/shard_map/ppermute | solution.py:55
  7.8 47.6 %collective-permute-start.1 = (f32[4,256,256]{2,1,0:T(8,128)}, f32[4,256,256]{2,1,0:T(8,128)}, u32[]{:S(2)}, u32[]{:S(2)}) collective-permute-start(f32[4,256,256]{2,1,0:T(8,128)} %get-tuple-element.8), channel_id=1, source_target_pairs={{0,2},{1,3},{2,0},{3,1},{4,6},{5,7},{6,4},{7,5},{8,10},{9,11},{10,... | collective-permute-start | bytes 3145736 | tf_op jit(solution)/shard_map/ppermute | solution.py:55
  10.5 3.9 %copy-start.6 = (s32[4,2]{0,1:T(2,128)S(1)}, s32[4,2]{0,1:T(2,128)}, u32[]{:S(2)}) copy-start(s32[4,2]{0,1:T(2,128)} %param.11) | copy-start | bytes 100
  12.0 46.0 %collective-permute-start.5 = (f32[264,1024]{1,0:T(8,128)}, f32[264,1024]{1,0:T(8,128)S(1)}, u32[]{:S(2)}, u32[]{:S(2)}) collective-permute-start(f32[264,1024]{1,0:T(8,128)} %pad_maximum_fusion), channel_id=1, source_target_pairs={{24,0},{0,8},{8,16},{16,24},{12,4},{20,12},{28,20},{4,28},{25,1},{... | collective-permute-start | bytes 3244040 | tf_op jit(solution)/shard_map/ppermute | solution.py:23
  13.6 47.7 %collective-permute-start.4 = (f32[264,1024]{1,0:T(8,128)}, f32[264,1024]{1,0:T(8,128)}, u32[]{:S(2)}, u32[]{:S(2)}) collective-permute-start(f32[264,1024]{1,0:T(8,128)} %pad_maximum_fusion), channel_id=1, source_target_pairs={{28,0},{4,8},{12,16},{20,24},{8,4},{16,12},{24,20},{0,28},{29,1},{... | collective-permute-start | bytes 3244040 | tf_op jit(solution)/shard_map/ppermute | solution.py:23
  54.0 8.9 %collective-permute-start.3 = (f32[264,1024]{1,0:T(8,128)}, f32[264,1024]{1,0:T(8,128)S(1)}, u32[]{:S(2)}, u32[]{:S(2)}) collective-permute-start(f32[264,1024]{1,0:T(8,128)} %pad_maximum_fusion), channel_id=1, source_target_pairs={{0,4},{8,12},{16,20},{24,28},{4,0},{12,8},{20,16},{28,24},{1,5},{9... | collective-permute-start | bytes 3244040 | tf_op jit(solution)/shard_map/ppermute | solution.py:23
  58.0 18.9 %collective-permute-start.7 = (f32[264,1024]{1,0:T(8,128)S(1)}, f32[264,1024]{1,0:T(8,128)S(1)}, u32[]{:S(2)}, u32[]{:S(2)}) collective-permute-start(f32[264,1024]{1,0:T(8,128)S(1)} %collective-permute-done.5), channel_id=1, source_target_pairs={{4,0},{12,8},{20,16},{28,24},{5,1},{13,9},{21,17},{29,25},{6,2},{1... | collective-permute-start | bytes 3244040 | tf_op jit(solution)/shard_map/ppermute | solution.py:23
  61.3 15.6 %collective-permute-start.8 = (f32[264,1024]{1,0:T(8,128)}, f32[264,1024]{1,0:T(8,128)S(1)}, u32[]{:S(2)}, u32[]{:S(2)}) collective-permute-start(f32[264,1024]{1,0:T(8,128)} %collective-permute-done.4), channel_id=1, source_target_pairs={{12,4},{20,12},{28,20},{4,28},{13,5},{21,13},{29,21},{5,29},{14,6}... | collective-permute-start | bytes 3244040 | tf_op jit(solution)/shard_map/ppermute | solution.py:23
  63.0 14.1 %collective-permute-start.6 = (f32[264,1024]{1,0:T(8,128)}, f32[264,1024]{1,0:T(8,128)S(1)}, u32[]{:S(2)}, u32[]{:S(2)}) collective-permute-start(f32[264,1024]{1,0:T(8,128)} %collective-permute-done.4), channel_id=1, source_target_pairs={{0,4},{8,12},{16,20},{24,28},{4,0},{12,8},{20,16},{28,24},{1,5},{9... | collective-permute-start | bytes 3244040 | tf_op jit(solution)/shard_map/ppermute | solution.py:23
  81.7 2.2 %copy-start.4 = (f32[4,256,1024]{2,1,0:T(8,128)S(1)}, f32[4,256,1024]{2,1,0:T(8,128)}, u32[]{:S(2)}) copy-start(f32[4,256,1024]{2,1,0:T(8,128)} %param.8) | copy-start | bytes 12582916
  102.0 49.5 %collective-permute-start.11 = (f32[4,256,256]{2,1,0:T(8,128)S(1)}, f32[4,256,256]{2,1,0:T(8,128)S(1)}, u32[]{:S(2)}, u32[]{:S(2)}) collective-permute-start(f32[4,256,256]{2,1,0:T(8,128)S(1)} %get-tuple-element.9), channel_id=1, source_target_pairs={{0,1},{1,2},{2,3},{3,0},{4,5},{5,6},{6,7},{7,4},{8,9},{9,10},{10,1... | collective-permute-start | bytes 3145736 | tf_op jit(solution)/shard_map/ppermute | solution.py:90
  104.5 46.9 %collective-permute-start.10 = (f32[4,256,256]{2,1,0:T(8,128)S(1)}, f32[4,256,256]{2,1,0:T(8,128)S(1)}, u32[]{:S(2)}, u32[]{:S(2)}) collective-permute-start(f32[4,256,256]{2,1,0:T(8,128)S(1)} %get-tuple-element.10), channel_id=1, source_target_pairs={{0,2},{1,3},{2,0},{3,1},{4,6},{5,7},{6,4},{7,5},{8,10},{9,11},{10,... | collective-permute-start | bytes 3145736 | tf_op jit(solution)/shard_map/ppermute | solution.py:90
  105.0 41.9 %collective-permute-start.9 = (f32[4,256,256]{2,1,0:T(8,128)S(1)}, f32[4,256,256]{2,1,0:T(8,128)S(1)}, u32[]{:S(2)}, u32[]{:S(2)}) collective-permute-start(f32[4,256,256]{2,1,0:T(8,128)S(1)} %get-tuple-element.11), channel_id=1, source_target_pairs={{0,3},{1,0},{2,1},{3,2},{4,7},{5,4},{6,5},{7,6},{8,11},{9,8},{10,9... | collective-permute-start | bytes 3145736 | tf_op jit(solution)/shard_map/ppermute | solution.py:90
  152.2 3.2 %copy-start.1 = (f32[256]{0:T(256)S(1)}, f32[256]{0:T(256)}, u32[]{:S(2)}) copy-start(f32[256]{0:T(256)} %param.12) | copy-start | bytes 3076

commit v7 on v5

--- a/solution.py
+++ b/solution.py
@@ -1,6 +1,7 @@
 import jax
 import jax.numpy as jnp
 from jax import lax
+from jax.experimental.layout import Layout, with_layout_constraint
 from jax.sharding import PartitionSpec as P
 
 HOPS = 5
@@ -81,6 +82,7 @@
             "rc,rpa->pca", block[:, quarter:], scaled, precision=PREC, preferred_element_type=jnp.float32
         )
         remote = part if remote is None else remote + part
+    remote = with_layout_constraint(remote, Layout(major_to_minor=(0, 1, 2)))
 
     received = [None] * nv
     for k in range(1, nv):
@@ -92,7 +94,7 @@
             "rc,rpa->pca", block[:, :quarter], scaled, precision=PREC, preferred_element_type=jnp.float32
         )
         own = part if own is None else own + part
-    received[0] = own
+    received[0] = with_layout_constraint(own, Layout(major_to_minor=(0, 1, 2)))
     out = jnp.zeros(received[0].shape[:2] + (width,), received[0].dtype)
     for k in range(nv):
         out = lax.dynamic_update_slice_in_dim(out, received[k], ((q + k) % nv) * quarter, 2)

time: 162 us -> 155 us (0.957)
  local copies, waits for them, and re-layouts: 25.1 us -> 16.2 us
  waiting for transfers between devices: 74.9 us -> 79.4 us
  matrix products: 38.5 us -> 35.5 us
    ppermute x3 -> x0, local copies, waits for them, and re-layouts: 4.66 us -> none  [local(): lax.ppermute(chunk, 'vb', [(i, (i - k) % nv) for i in range(nv)])]
    ppermute x3, waiting for transfers between devices: 36.5 us -> 41 us  [local(): lax.ppermute(chunk, 'vb', [(i, (i - k) % nv) for i in range(nv)])]
    dot_general x6, matrix products: 7.24 us -> 4.98 us  [local(): jnp.einsum('rc,rpa->pca', block[:, :quarter], scaled, precision=PREC, pre...]
    dynamic_update_slice x4 -> x3, local copies, waits for them, and re-layouts: 3.25 us -> 1.28 us  [local(): lax.dynamic_update_slice_in_dim(out, received[k], (q + k) % nv * quarter, 2)]
    slice x1, local copies, waits for them, and re-layouts: 2.08 us -> 0.2 us  [local(): chunk = remote[:, (k - 1) * quarter:k * quarter]]
  transfers between devices with their start and end apart: 12 -> 12, of which waited for: 3 -> 4; matrix products, arithmetic and copies ran while one was open for 18% -> 14% of each run, Pallas kernels for 0% -> 0%
where the time goes in v7:
time: 155 us; the launch traced here: 154 us
  waiting for transfers between devices  79.4 us (51%)
  matrix products  35.5 us (23%)
  starting transfers between devices  21.1 us (14%)
  local copies, waits for them, and re-layouts  16.2 us (10%)
  other arithmetic  1.55 us (1%)
    ppermute x3, waiting for transfers between devices, local(): lax.ppermute(chunk, 'vb', [(i, (i - k) % nv) for i in range(nv)])  41 us
    ppermute x3, waiting for transfers between devices, local(): lax.ppermute(send, 'vb', [(i, (i + k) % nv) for i in range(nv)])  36.5 us
    ppermute x6, starting transfers between devices, perm(): return lax.ppermute(x, 'blk', [(s % nb, t % nb) for s, t in pairs])  12.1 us
    dot_general x6, matrix products, local(): jnp.einsum('rb,pba->rpa', block[:, quarter:], rest, precision=PREC, prefe...  11.8 us
    dot_general x6, matrix products, local(): jnp.einsum('rc,rpa->pca', block[:, quarter:], scaled, precision=PREC, pre...  11.8 us
    dot_general x6, matrix products, local(): jnp.einsum('rb,pba->rpa', block[:, :quarter], pieces[0], precision=PREC,...  6.92 us
    unnamed x35, local copies, waits for them, and re-layouts  6.03 us
    ppermute x3, starting transfers between devices, local(): lax.ppermute(send, 'vb', [(i, (i + k) % nv) for i in range(nv)])  5.04 us
  transfers between devices with their start and end apart: 12, of which 4 were waited for; matrix products, arithmetic and copies ran while one was open for 14% of the time, Pallas kernels for 0%

profile of v7, /device:TPU:0, one launch (start us, length us, event | category | flops | bytes accessed | tf_op | source)
XLA Modules:
  0.0 154.4 jit_solution(18315763209504940114)
XLA Ops:
  0.0 3.8 %constant_dynamic-slice_fusion = (f32[4,256,256]{2,1,0:T(8,128)}, f32[4,256,256]{2,1,0:T(8,128)}, f32[4,256,256]{2,1,0:T(8,128)}) fusion(f32[4,256,1024]{2,1,0:T(8,128)} %param.8, s32[]{:T(128)S(6)} %select_n.89, s32[]{:T(128)S(6)} %select_n.85, s32[]{:T(128)S(6)} %select_n.87), kind=kLoop, calls=%fused_computation.102 | loop fusion | bytes 6291468 | tf_op jit(solution)/shard_map/dynamic_slice | solution.py:54
  3.8 3.9 %collective-permute-start.2 = (f32[4,256,256]{2,1,0:T(8,128)}, f32[4,256,256]{2,1,0:T(8,128)}, u32[]{:S(2)}, u32[]{:S(2)}) collective-permute-start(f32[4,256,256]{2,1,0:T(8,128)} %get-tuple-element.6), channel_id=1, source_target_pairs={{0,3},{1,0},{2,1},{3,2},{4,7},{5,4},{6,5},{7,6},{8,11},{9,8},{10,9... | collective-permute-start | bytes 3145736 | tf_op jit(solution)/shard_map/ppermute | solution.py:55
  7.8 1.1 collective-permute-start.1
  9.1 1.4 gather_fusion
  10.5 0.0 copy-start.7
  10.5 0.3 constant_dynamic-slice_fusion.3
  10.9 1.1 pad_maximum_fusion
  12.0 1.6 %collective-permute-start.5 = (f32[264,1024]{1,0:T(8,128)}, f32[264,1024]{1,0:T(8,128)S(1)}, u32[]{:S(2)}, u32[]{:S(2)}) collective-permute-start(f32[264,1024]{1,0:T(8,128)} %pad_maximum_fusion), channel_id=1, source_target_pairs={{24,0},{0,8},{8,16},{16,24},{12,4},{20,12},{28,20},{4,28},{25,1},{... | collective-permute-start | bytes 3244040 | tf_op jit(solution)/shard_map/ppermute | solution.py:23
  13.5 0.8 collective-permute-start.4
  14.3 0.1 dynamic_slice.23
  14.4 0.6 gather_fusion.2
  15.1 0.6 gather_fusion.1
  15.7 1.9 %fusion.15 = f32[256,4,256]{2,0,1:T(8,128)S(1)} fusion(f32[4,256,1024]{2,1,0:T(8,128)} %param.8, s32[]{:T(128)S(6)} %select_n.83, f32[256,2048]{1,0:T(8,128)S(1)} %slice_dynamic-update-slice_fusion.1, s32[]{:T(128)S(6)} %select_n.82), kind=kOutput, calls=%fused_computation.35 | convolution fusion | flops 402653184 | bytes 2359304 | tf_op jit(solution)/shard_map/rb,pba->rpa/dot_general | solution.py:73
  17.6 36.5 %collective-permute-done = f32[4,256,256]{2,1,0:T(8,128)} collective-permute-done((f32[4,256,256]{2,1,0:T(8,128)}, f32[4,256,256]{2,1,0:T(8,128)}, u32[]{:S(2)}, u32[]{:S(2)}) %collective-permute-start) | collective-permute-done | bytes 1048608 | tf_op jit(solution)/shard_map/ppermute | solution.py:55
  54.0 0.0 collective-permute-start.3
  54.1 1.3 constant_dynamic-update-slice_fusion.2
  55.4 1.3 constant_dynamic-update-slice_fusion.1
  56.7 1.3 constant_dynamic-update-slice_fusion
  58.0 0.0 collective-permute-done.5
  58.0 1.3 collective-permute-start.7
  59.3 1.9 %collective-permute-done.4 = f32[264,1024]{1,0:T(8,128)} collective-permute-done((f32[264,1024]{1,0:T(8,128)}, f32[264,1024]{1,0:T(8,128)}, u32[]{:S(2)}, u32[]{:S(2)}) %collective-permute-start.4) | collective-permute-done | bytes 1081376 | tf_op jit(solution)/shard_map/ppermute | solution.py:23
  61.2 0.9 collective-permute-start.8
  62.1 0.8 slice_bitcast_fusion.35
  62.9 0.0 collective-permute-done.3
  63.0 7.5 %collective-permute-start.6 = (f32[264,1024]{1,0:T(8,128)}, f32[264,1024]{1,0:T(8,128)S(1)}, u32[]{:S(2)}, u32[]{:S(2)}) collective-permute-start(f32[264,1024]{1,0:T(8,128)} %collective-permute-done.4), channel_id=1, source_target_pairs={{0,4},{8,12},{16,20},{24,28},{4,0},{12,8},{20,16},{28,24},{1,5},{9... | collective-permute-start | bytes 3244040 | tf_op jit(solution)/shard_map/ppermute | solution.py:23
  70.5 1.7 %fusion.22 = f32[256,4,256]{2,0,1:T(8,128)S(1)} fusion(f32[4,768,256]{2,1,0:T(8,128)S(1)} %constant_dynamic-update-slice_fusion, f32[264,1024]{1,0:T(8,128)S(1)} %collective-permute-done.5), kind=kOutput, calls=%fused_computation.42 | convolution fusion | flops 1207959552 | bytes 4980736 | tf_op jit(solution)/shard_map/rb,pba->rpa/dot_general | solution.py:75
  72.2 2.9 %fusion.20 = f32[256,4,256]{2,0,1:T(8,128)S(1)} fusion(f32[4,768,256]{2,1,0:T(8,128)S(1)} %constant_dynamic-update-slice_fusion, f32[264,1024]{1,0:T(8,128)} %collective-permute-done.4), kind=kOutput, calls=%fused_computation.40 | convolution fusion | flops 1207959552 | bytes 4980736 | tf_op jit(solution)/shard_map/rb,pba->rpa/dot_general | solution.py:75
  75.1 1.7 %fusion.18 = f32[256,4,256]{2,0,1:T(8,128)S(1)} fusion(f32[4,768,256]{2,1,0:T(8,128)S(1)} %constant_dynamic-update-slice_fusion, f32[264,1024]{1,0:T(8,128)S(1)} %collective-permute-done.3), kind=kOutput, calls=%fused_computation.38 | convolution fusion | flops 1207959552 | bytes 4980736 | tf_op jit(solution)/shard_map/rb,pba->rpa/dot_general | solution.py:75
  76.9 0.2 broadcast_select_fusion
  77.2 0.3 broadcast_add_fusion.1
  77.4 1.8 %fusion = f32[256,4,256]{2,0,1:T(8,128)S(1)} fusion(f32[256,4,256]{2,0,1:T(8,128)S(1)} %fusion.15, f32[4,768,256]{2,1,0:T(8,128)S(1)} %constant_dynamic-update-slice_fusion, f32[256,2048]{1,0:T(8,128)S(1)} %slice_dynamic-update-slice_fusion.1, s32[]{:T(128)S(6)} %add.278, f32[4]{0:T(128)S(1)} %fusion.40, f32[256,256]{1,0:T(8,128)S(1)} %get-tuple-element.17), kind=kOutput, calls=%fused_computation.5 | convolution fusion | flops 1208745984 | bytes 6291972 | tf_op jit(solution)/shard_map/rb,pba->rpa/dot_general | solution.py:75
  79.3 0.7 fusion.30
  80.0 1.7 %fusion.27 = f32[4,256,768]{1,2,0:T(8,128)S(1)} fusion(f32[256,4,256]{2,0,1:T(8,128)S(1)} %fusion, f32[256,2048]{1,0:T(8,128)S(1)} %slice_dynamic-update-slice_fusion.1, s32[]{:T(128)S(6)} %add.278), kind=kOutput, calls=%fused_computation.47 | convolution fusion | flops 1207959552 | bytes 4980740 | tf_op jit(solution)/shard_map/rc,rpa->pca/dot_general | solution.py:81
  81.7 0.0 copy-start.5
  81.7 1.7 %fusion.26 = f32[256,4,256]{2,0,1:T(8,128)S(1)} fusion(f32[4,768,256]{2,1,0:T(8,128)S(1)} %constant_dynamic-update-slice_fusion, f32[264,1024]{1,0:T(8,128)S(1)} %broadcast_select_fusion), kind=kOutput, calls=%fused_computation.46 | convolution fusion | flops 1207959552 | bytes 4980736 | tf_op jit(solution)/shard_map/rb,pba->rpa/dot_general | solution.py:75
  83.4 0.5 copy-done.5
  83.9 0.8 fusion.1
  84.7 0.6 fusion.29
  85.3 1.9 %fusion.24 = f32[256,4,256]{2,0,1:T(8,128)S(1)} fusion(f32[4,768,256]{2,1,0:T(8,128)S(1)} %constant_dynamic-update-slice_fusion, f32[264,1024]{1,0:T(8,128)S(1)} %collective-permute-done.6), kind=kOutput, calls=%fused_computation.44 | convolution fusion | flops 1207959552 | bytes 4980736 | tf_op jit(solution)/shard_map/rb,pba->rpa/dot_general | solution.py:75
  87.3 0.8 fusion.6
  88.1 1.5 fusion.21
  89.6 1.8 %fusion.8 = f32[256,4,256]{2,0,1:T(8,128)S(1)} fusion(f32[256,4,256]{2,0,1:T(8,128)S(1)} %fusion.20, f32[4,256,1024]{2,1,0:T(8,128)S(1)} %copy-done.5, s32[]{:T(128)S(6)} %select_n.83, f32[256,256]{1,0:T(8,128)S(1)} %get-tuple-element.14, f32[4]{0:T(128)S(1)} %fusion.40, f32[264,1024]{1,0:T(8,128)} %collective-permute-done.4), kind=kOutput, calls=%fused_computation.19 | convolution fusion | flops 403439616 | bytes 3670532 | tf_op jit(solution)/shard_map/rb,pba->rpa/dot_general | solution.py:73
  91.4 2.6 %fusion.19 = f32[4,256,768]{1,2,0:T(8,128)S(1)} fusion(f32[256,4,256]{2,0,1:T(8,128)S(1)} %fusion.8, f32[264,1024]{1,0:T(8,128)} %collective-permute-done.4), kind=kOutput, calls=%fused_computation.39 | convolution fusion | flops 1207959552 | bytes 4980736 | tf_op jit(solution)/shard_map/rc,rpa->pca/dot_general | solution.py:81
  94.1 0.8 fusion.9
  94.9 1.5 fusion.17
  96.4 0.8 fusion.5
  97.2 1.5 fusion.23
  98.8 2.9 %add_bitcast_fusion = f32[4,768,256]{2,1,0:T(8,128)S(1)} fusion(f32[4,256,768]{1,2,0:T(8,128)S(1)} %fusion.23, f32[4,256,768]{1,2,0:T(8,128)S(1)} %fusion.21, f32[4,256,768]{1,2,0:T(8,128)S(1)} %fusion.19, f32[4,256,768]{1,2,0:T(8,128)S(1)} %fusion.27, f32[4,256,768]{1,2,0:T(8,128)S(1)} %fusion.17, f32[256,4,256]{2,0,1:T(8,128)S(1)} %fusion.1, ...), kind=kOutput, calls=%fused_computation.3 | convolution fusion | flops 1211891712 | bytes 20709376 | tf_op jit(solution)/shard_map/rc,rpa->pca/dot_general | solution.py:81
  101.7 0.2 fusion.41
  101.9 2.5 %collective-permute-start.11 = (f32[4,256,256]{2,1,0:T(8,128)S(1)}, f32[4,256,256]{2,1,0:T(8,128)S(1)}, u32[]{:S(2)}, u32[]{:S(2)}) collective-permute-start(f32[4,256,256]{2,1,0:T(8,128)S(1)} %get-tuple-element.9), channel_id=1, source_target_pairs={{0,1},{1,2},{2,3},{3,0},{4,5},{5,6},{6,7},{7,4},{8,9},{9,10},{10,1... | collective-permute-start | bytes 3145736 | tf_op jit(solution)/shard_map/ppermute | solution.py:90
  104.4 0.5 collective-permute-start.10
  104.9 1.0 collective-permute-start.9
  105.9 0.6 convolution_add_fusion.7
  106.6 0.6 fusion.28
  107.2 1.7 %fusion.7 = f32[4,256,256]{1,2,0:T(8,128)S(1)} fusion(f32[4,256,256]{1,2,0:T(8,128)S(1)} %fusion.28, f32[4,256,256]{1,2,0:T(8,128)S(1)} %convolution_add_fusion.7, f32[256,4,256]{2,0,1:T(8,128)S(1)} %fusion.8, f32[264,1024]{1,0:T(8,128)} %collective-permute-done.4), kind=kOutput, calls=%fused_computation.17 | convolution fusion | flops 403177472 | bytes 4456448 | tf_op jit(solution)/shard_map/rc,rpa->pca/dot_general | solution.py:93
  108.9 0.5 broadcast_in_dim.13
  109.4 0.7 fusion.4
  110.1 36.6 %collective-permute-done.9 = f32[4,256,256]{2,1,0:T(8,128)S(1)} collective-permute-done((f32[4,256,256]{2,1,0:T(8,128)S(1)}, f32[4,256,256]{2,1,0:T(8,128)S(1)}, u32[]{:S(2)}, u32[]{:S(2)}) %collective-permute-start.9) | collective-permute-done | bytes 1048608 | tf_op jit(solution)/shard_map/ppermute | solution.py:90
  146.8 0.1 constant_dynamic-update-slice_fusion.5
  146.9 4.3 %collective-permute-done.10 = f32[4,256,256]{2,1,0:T(8,128)S(1)} collective-permute-done((f32[4,256,256]{2,1,0:T(8,128)S(1)}, f32[4,256,256]{2,1,0:T(8,128)S(1)}, u32[]{:S(2)}, u32[]{:S(2)}) %collective-permute-start.10) | collective-permute-done | bytes 1048608 | tf_op jit(solution)/shard_map/ppermute | solution.py:90
  151.2 0.1 constant_dynamic-update-slice_fusion.4
  151.4 0.0 copy-start.4
  151.4 2.0 %copy-done.4 = f32[4,256,1024]{2,1,0:T(8,128)} copy-done((f32[4,256,1024]{2,1,0:T(8,128)}, f32[4,256,1024]{2,1,0:T(8,128)S(1)}, u32[]{:S(2)}) %copy-start.4) | copy-done | bytes 4194328
  153.4 1.0 constant_dynamic-update-slice_fusion.3
  (48 shorter events, 0.3 us)
Async XLA Ops:
  0.0 14.4 %copy-start = (f32[256]{0:T(256)S(1)}, f32[256]{0:T(256)}, u32[]{:S(2)}) copy-start(f32[256]{0:T(256)} %param.12) | copy-start | bytes 3076
  0.0 8.9 %copy-start.6 = (s32[256]{0:T(256)S(1)}, s32[256]{0:T(256)}, u32[]{:S(2)}) copy-start(s32[256]{0:T(256)} %param.10) | copy-start | bytes 3076
  0.0 8.9 %copy-start.3 = (f32[256,1024]{1,0:T(8,128)S(1)}, f32[256,1024]{1,0:T(8,128)}, u32[]{:S(2)}) copy-start(f32[256,1024]{1,0:T(8,128)} %param.9) | copy-start | bytes 3145732
  3.8 5.3 %copy-start.2 = (f32[1024]{0:T(1024)S(1)}, f32[1024]{0:T(1024)}, u32[]{:S(2)}) copy-start(f32[1024]{0:T(1024)} %param.13) | copy-start | bytes 12292
  3.8 52.9 %collective-permute-start.2 = (f32[4,256,256]{2,1,0:T(8,128)}, f32[4,256,256]{2,1,0:T(8,128)}, u32[]{:S(2)}, u32[]{:S(2)}) collective-permute-start(f32[4,256,256]{2,1,0:T(8,128)} %get-tuple-element.6), channel_id=1, source_target_pairs={{0,3},{1,0},{2,1},{3,2},{4,7},{5,4},{6,5},{7,6},{8,11},{9,8},{10,9... | collective-permute-start | bytes 3145736 | tf_op jit(solution)/shard_map/ppermute | solution.py:55
  7.8 46.3 %collective-permute-start = (f32[4,256,256]{2,1,0:T(8,128)}, f32[4,256,256]{2,1,0:T(8,128)}, u32[]{:S(2)}, u32[]{:S(2)}) collective-permute-start(f32[4,256,256]{2,1,0:T(8,128)} %get-tuple-element.7), channel_id=1, source_target_pairs={{0,1},{1,2},{2,3},{3,0},{4,5},{5,6},{6,7},{7,4},{8,9},{9,10},{10,1... | collective-permute-start | bytes 3145736 | tf_op jit(solution)/shard_map/ppermute | solution.py:55
  7.8 47.6 %collective-permute-start.1 = (f32[4,256,256]{2,1,0:T(8,128)}, f32[4,256,256]{2,1,0:T(8,128)}, u32[]{:S(2)}, u32[]{:S(2)}) collective-permute-start(f32[4,256,256]{2,1,0:T(8,128)} %get-tuple-element.8), channel_id=1, source_target_pairs={{0,2},{1,3},{2,0},{3,1},{4,6},{5,7},{6,4},{7,5},{8,10},{9,11},{10,... | collective-permute-start | bytes 3145736 | tf_op jit(solution)/shard_map/ppermute | solution.py:55
  10.5 3.9 %copy-start.7 = (s32[4,2]{0,1:T(2,128)S(1)}, s32[4,2]{0,1:T(2,128)}, u32[]{:S(2)}) copy-start(s32[4,2]{0,1:T(2,128)} %param.11) | copy-start | bytes 100
  12.0 46.0 %collective-permute-start.5 = (f32[264,1024]{1,0:T(8,128)}, f32[264,1024]{1,0:T(8,128)S(1)}, u32[]{:S(2)}, u32[]{:S(2)}) collective-permute-start(f32[264,1024]{1,0:T(8,128)} %pad_maximum_fusion), channel_id=1, source_target_pairs={{24,0},{0,8},{8,16},{16,24},{12,4},{20,12},{28,20},{4,28},{25,1},{... | collective-permute-start | bytes 3244040 | tf_op jit(solution)/shard_map/ppermute | solution.py:23
  13.5 47.7 %collective-permute-start.4 = (f32[264,1024]{1,0:T(8,128)}, f32[264,1024]{1,0:T(8,128)}, u32[]{:S(2)}, u32[]{:S(2)}) collective-permute-start(f32[264,1024]{1,0:T(8,128)} %pad_maximum_fusion), channel_id=1, source_target_pairs={{28,0},{4,8},{12,16},{20,24},{8,4},{16,12},{24,20},{0,28},{29,1},{... | collective-permute-start | bytes 3244040 | tf_op jit(solution)/shard_map/ppermute | solution.py:23
  54.0 8.9 %collective-permute-start.3 = (f32[264,1024]{1,0:T(8,128)}, f32[264,1024]{1,0:T(8,128)S(1)}, u32[]{:S(2)}, u32[]{:S(2)}) collective-permute-start(f32[264,1024]{1,0:T(8,128)} %pad_maximum_fusion), channel_id=1, source_target_pairs={{0,4},{8,12},{16,20},{24,28},{4,0},{12,8},{20,16},{28,24},{1,5},{9... | collective-permute-start | bytes 3244040 | tf_op jit(solution)/shard_map/ppermute | solution.py:23
  58.0 18.8 %collective-permute-start.7 = (f32[264,1024]{1,0:T(8,128)S(1)}, f32[264,1024]{1,0:T(8,128)S(1)}, u32[]{:S(2)}, u32[]{:S(2)}) collective-permute-start(f32[264,1024]{1,0:T(8,128)S(1)} %collective-permute-done.5), channel_id=1, source_target_pairs={{4,0},{12,8},{20,16},{28,24},{5,1},{13,9},{21,17},{29,25},{6,2},{1... | collective-permute-start | bytes 3244040 | tf_op jit(solution)/shard_map/ppermute | solution.py:23
  61.2 15.6 %collective-permute-start.8 = (f32[264,1024]{1,0:T(8,128)}, f32[264,1024]{1,0:T(8,128)S(1)}, u32[]{:S(2)}, u32[]{:S(2)}) collective-permute-start(f32[264,1024]{1,0:T(8,128)} %collective-permute-done.4), channel_id=1, source_target_pairs={{12,4},{20,12},{28,20},{4,28},{13,5},{21,13},{29,21},{5,29},{14,6}... | collective-permute-start | bytes 3244040 | tf_op jit(solution)/shard_map/ppermute | solution.py:23
  63.0 14.1 %collective-permute-start.6 = (f32[264,1024]{1,0:T(8,128)}, f32[264,1024]{1,0:T(8,128)S(1)}, u32[]{:S(2)}, u32[]{:S(2)}) collective-permute-start(f32[264,1024]{1,0:T(8,128)} %collective-permute-done.4), channel_id=1, source_target_pairs={{0,4},{8,12},{16,20},{24,28},{4,0},{12,8},{20,16},{28,24},{1,5},{9... | collective-permute-start | bytes 3244040 | tf_op jit(solution)/shard_map/ppermute | solution.py:23
  81.7 2.2 %copy-start.5 = (f32[4,256,1024]{2,1,0:T(8,128)S(1)}, f32[4,256,1024]{2,1,0:T(8,128)}, u32[]{:S(2)}) copy-start(f32[4,256,1024]{2,1,0:T(8,128)} %param.8) | copy-start | bytes 12582916
  101.9 49.5 %collective-permute-start.11 = (f32[4,256,256]{2,1,0:T(8,128)S(1)}, f32[4,256,256]{2,1,0:T(8,128)S(1)}, u32[]{:S(2)}, u32[]{:S(2)}) collective-permute-start(f32[4,256,256]{2,1,0:T(8,128)S(1)} %get-tuple-element.9), channel_id=1, source_target_pairs={{0,1},{1,2},{2,3},{3,0},{4,5},{5,6},{6,7},{7,4},{8,9},{9,10},{10,1... | collective-permute-start | bytes 3145736 | tf_op jit(solution)/shard_map/ppermute | solution.py:90
  104.4 46.8 %collective-permute-start.10 = (f32[4,256,256]{2,1,0:T(8,128)S(1)}, f32[4,256,256]{2,1,0:T(8,128)S(1)}, u32[]{:S(2)}, u32[]{:S(2)}) collective-permute-start(f32[4,256,256]{2,1,0:T(8,128)S(1)} %get-tuple-element.10), channel_id=1, source_target_pairs={{0,2},{1,3},{2,0},{3,1},{4,6},{5,7},{6,4},{7,5},{8,10},{9,11},{10,... | collective-permute-start | bytes 3145736 | tf_op jit(solution)/shard_map/ppermute | solution.py:90
  104.9 41.9 %collective-permute-start.9 = (f32[4,256,256]{2,1,0:T(8,128)S(1)}, f32[4,256,256]{2,1,0:T(8,128)S(1)}, u32[]{:S(2)}, u32[]{:S(2)}) collective-permute-start(f32[4,256,256]{2,1,0:T(8,128)S(1)} %get-tuple-element.11), channel_id=1, source_target_pairs={{0,3},{1,0},{2,1},{3,2},{4,7},{5,4},{6,5},{7,6},{8,11},{9,8},{10,9... | collective-permute-start | bytes 3145736 | tf_op jit(solution)/shard_map/ppermute | solution.py:90
  146.8 7.6 %copy-start.1 = (f32[256]{0:T(256)S(1)}, f32[256]{0:T(256)}, u32[]{:S(2)}) copy-start(f32[256]{0:T(256)} %param.12) | copy-start | bytes 3076
  151.4 2.0 %copy-start.4 = (f32[4,256,1024]{2,1,0:T(8,128)}, f32[4,256,1024]{2,1,0:T(8,128)S(1)}, u32[]{:S(2)}) copy-start(f32[4,256,1024]{2,1,0:T(8,128)S(1)} %constant_dynamic-update-slice_fusion.4) | copy-start | bytes 12582916

commit v8 on v7

--- a/solution.py
+++ b/solution.py
@@ -53,7 +53,6 @@
         dest_start = ((q + k) % nv) * quarter
         send = lax.dynamic_slice_in_dim(amplitudes, dest_start, quarter, 2)
         pieces.append(lax.ppermute(send, "vb", [(i, (i + k) % nv) for i in range(nv)]))
-    rest = jnp.concatenate(pieces[1:], axis=1)
 
     reversed_cols = jnp.concatenate(
         [integrals[:, ((-k) % nv) * quarter:((-k) % nv + 1) * quarter] for k in range(nv)], axis=1
@@ -70,11 +69,13 @@
     for item in window:
         block = item[:rows]
         energies = item[rows:].reshape(-1)[:rows]
-        weighted = jnp.einsum(
-            "rb,pba->rpa", block[:, :quarter], pieces[0], precision=PREC, preferred_element_type=jnp.float32
-        ) + jnp.einsum(
-            "rb,pba->rpa", block[:, quarter:], rest, precision=PREC, preferred_element_type=jnp.float32
-        )
+        weighted = None
+        for k in range(nv):
+            term = jnp.einsum(
+                "rb,pba->rpa", block[:, k * quarter:(k + 1) * quarter], pieces[k], precision=PREC,
+                preferred_element_type=jnp.float32,
+            )
+            weighted = term if weighted is None else weighted + term
         denom = (energies[:, None] + own_virtual[None, :])[:, None, :] - pair_energy[None, :, None]
         scaled = weighted / denom
         scaled_blocks.append((block, scaled))

time: 155 us -> 173 us (1.12)
  matrix products: 35.5 us -> 51 us
  local copies, waits for them, and re-layouts: 16.2 us -> 20.4 us
  waiting for transfers between devices: 79.4 us -> 77.4 us
    dot_general x12 -> x24, matrix products: 18.7 us -> 29.7 us  [local(): jnp.einsum('rb,pba->rpa', block[:, k * quarter:(k + 1) * quarter], pieces...]
    ppermute x3, waiting for transfers between devices: 36.5 us -> 28 us  [local(): lax.ppermute(send, 'vb', [(i, (i + k) % nv) for i in range(nv)])]
    ppermute x6, waiting for transfers between devices: 1.93 us -> 9.96 us  [perm(): return lax.ppermute(x, 'blk', [(s % nb, t % nb) for s, t in pairs])]
    unnamed x35, local copies, waits for them, and re-layouts: 6.03 us -> 9.56 us
    dot_general x6, matrix products: 11.8 us -> 14.1 us  [local(): jnp.einsum('rc,rpa->pca', block[:, quarter:], scaled, precision=PREC, pre...]
    dot_general x6, matrix products: 4.98 us -> 7.2 us  [local(): jnp.einsum('rc,rpa->pca', block[:, :quarter], scaled, precision=PREC, pre...]
  transfers between devices with their start and end apart: 12 -> 12, of which waited for: 4 -> 3; matrix products, arithmetic and copies ran while one was open for 14% -> 21% of each run, Pallas kernels for 0% -> 0%
where the time goes in v8:
time: 173 us; the launch traced here: 172 us
  waiting for transfers between devices  77.4 us (45%)
  matrix products  51 us (29%)
  starting transfers between devices  20.9 us (12%)
  local copies, waits for them, and re-layouts  20.4 us (12%)
    ppermute x3, waiting for transfers between devices, local(): lax.ppermute(chunk, 'vb', [(i, (i - k) % nv) for i in range(nv)])  39.5 us
    dot_general x24, matrix products, local(): jnp.einsum('rb,pba->rpa', block[:, k * quarter:(k + 1) * quarter], pieces...  29.7 us
    ppermute x3, waiting for transfers between devices, local(): lax.ppermute(send, 'vb', [(i, (i + k) % nv) for i in range(nv)])  28 us
    dot_general x6, matrix products, local(): jnp.einsum('rc,rpa->pca', block[:, quarter:], scaled, precision=PREC, pre...  14.1 us
    ppermute x6, starting transfers between devices, perm(): return lax.ppermute(x, 'blk', [(s % nb, t % nb) for s, t in pairs])  11.9 us
    ppermute x6, waiting for transfers between devices, perm(): return lax.ppermute(x, 'blk', [(s % nb, t % nb) for s, t in pairs])  9.96 us
    unnamed x35, local copies, waits for them, and re-layouts  9.56 us
    dot_general x6, matrix products, local(): jnp.einsum('rc,rpa->pca', block[:, :quarter], scaled, precision=PREC, pre...  7.2 us
  transfers between devices with their start and end apart: 12, of which 3 were waited for; matrix products, arithmetic and copies ran while one was open for 21% of the time, Pallas kernels for 0%

profile of v8, /device:TPU:0, one launch (start us, length us, event | category | flops | bytes accessed | tf_op | source)
XLA Modules:
  0.0 171.9 jit_solution(917574596962833689)
XLA Ops:
  0.0 3.7 %constant_dynamic-slice_fusion.2 = (f32[4,256,256]{2,1,0:T(8,128)}, f32[4,256,256]{2,1,0:T(8,128)}, f32[4,256,256]{2,1,0:T(8,128)}) fusion(f32[4,256,1024]{2,1,0:T(8,128)} %param.8, s32[]{:T(128)S(6)} %select_n.85, s32[]{:T(128)S(6)} %select_n.89, s32[]{:T(128)S(6)} %select_n.87), kind=kLoop, calls=%fused_computation.142 | loop fusion | bytes 6291468 | tf_op jit(solution)/shard_map/dynamic_slice | solution.py:54
  3.7 3.0 %collective-permute-start = (f32[4,256,256]{2,1,0:T(8,128)}, f32[4,256,256]{2,1,0:T(8,128)S(1)}, u32[]{:S(2)}, u32[]{:S(2)}) collective-permute-start(f32[4,256,256]{2,1,0:T(8,128)} %get-tuple-element.6), channel_id=1, source_target_pairs={{0,1},{1,2},{2,3},{3,0},{4,5},{5,6},{6,7},{7,4},{8,9},{9,10},{10,1... | collective-permute-start | bytes 3145736 | tf_op jit(solution)/shard_map/ppermute | solution.py:55
  6.7 1.0 collective-permute-start.2
  7.7 0.7 slice_dynamic-update-slice_fusion.6
  8.4 0.7 slice_dynamic-update-slice_fusion.4
  9.1 0.7 slice_dynamic-update-slice_fusion.2
  9.9 0.7 slice_dynamic-update-slice_fusion
  10.6 0.7 slice_dynamic-update-slice_fusion.7
  11.3 0.7 slice_dynamic-update-slice_fusion.5
  12.0 0.7 slice_dynamic-update-slice_fusion.3
  12.7 0.7 slice_dynamic-update-slice_fusion.1
  13.5 1.4 gather_fusion
  14.9 1.6 constant_dynamic-slice_fusion.3
  16.5 1.1 pad_maximum_fusion
  17.6 2.1 %collective-permute-start.5 = (f32[264,1024]{1,0:T(8,128)}, f32[264,1024]{1,0:T(8,128)S(1)}, u32[]{:S(2)}, u32[]{:S(2)}) collective-permute-start(f32[264,1024]{1,0:T(8,128)} %pad_maximum_fusion), channel_id=1, source_target_pairs={{24,0},{0,8},{8,16},{16,24},{12,4},{20,12},{28,20},{4,28},{25,1},{... | collective-permute-start | bytes 3244040 | tf_op jit(solution)/shard_map/ppermute | solution.py:23
  19.7 1.1 collective-permute-start.4
  21.4 0.6 gather_fusion.2
  22.0 0.6 gather_fusion.1
  22.7 3.0 %fusion.32 = f32[256,4,256]{2,0,1:T(8,128)} fusion(f32[4,256,1024]{2,1,0:T(8,128)} %param.8, s32[]{:T(128)S(6)} %select_n.83, f32[256,2048]{1,0:T(8,128)} %slice_dynamic-update-slice_fusion.1, s32[]{:T(128)S(6)} %select_n.82), kind=kOutput, calls=%fused_computation.53 | convolution fusion | flops 402653184 | bytes 2359304 | tf_op jit(solution)/shard_map/rb,pba->rpa/dot_general | solution.py:74
  25.8 28.0 %collective-permute-done.2 = f32[4,256,256]{2,1,0:T(8,128)S(1)} collective-permute-done((f32[4,256,256]{2,1,0:T(8,128)}, f32[4,256,256]{2,1,0:T(8,128)S(1)}, u32[]{:S(2)}, u32[]{:S(2)}) %collective-permute-start.2) | collective-permute-done | bytes 1048608 | tf_op jit(solution)/shard_map/ppermute | solution.py:55
  54.1 1.7 fusion.49
  55.8 1.7 convolution_add_fusion.9
  57.5 9.9 %collective-permute-done.4 = f32[264,1024]{1,0:T(8,128)} collective-permute-done((f32[264,1024]{1,0:T(8,128)}, f32[264,1024]{1,0:T(8,128)}, u32[]{:S(2)}, u32[]{:S(2)}) %collective-permute-start.4) | collective-permute-done | bytes 1081376 | tf_op jit(solution)/shard_map/ppermute | solution.py:23
  67.4 0.8 slice_bitcast_fusion.60
  68.2 0.8 slice_bitcast_fusion.61
  69.0 1.3 collective-permute-start.7
  70.3 0.9 collective-permute-start.8
  71.2 6.0 %collective-permute-start.6 = (f32[264,1024]{1,0:T(8,128)}, f32[264,1024]{1,0:T(8,128)S(1)}, u32[]{:S(2)}, u32[]{:S(2)}) collective-permute-start(f32[264,1024]{1,0:T(8,128)} %collective-permute-done.4), channel_id=1, source_target_pairs={{0,4},{8,12},{16,20},{24,28},{4,0},{12,8},{20,16},{28,24},{1,5},{9... | collective-permute-start | bytes 3244040 | tf_op jit(solution)/shard_map/ppermute | solution.py:23
  77.2 0.7 fusion.42
  77.9 1.6 fusion.45
  79.5 1.6 fusion.48
  81.1 0.7 fusion.40
  81.8 1.6 fusion.43
  83.4 1.6 fusion.46
  85.6 1.6 fusion.44
  87.2 1.6 fusion.47
  89.3 1.8 %fusion.20 = f32[256,4,256]{2,0,1:T(8,128)S(1)} fusion(f32[256,4,256]{2,0,1:T(8,128)S(1)} %fusion.49, f32[256,4,256]{2,0,1:T(8,128)S(1)} %convolution_add_fusion.9, f32[4,256,256]{2,1,0:T(8,128)S(1)} %collective-permute-done.1, f32[4]{0:T(128)S(1)} %fusion.64, f32[256,256]{1,0:T(8,128)S(1)} %get-tuple-element.17, ...), kind=kOutput, calls=%fused_computation.33 | convolution fusion | flops 403701760 | bytes 4718612 | tf_op jit(solution)/shard_map/rb,pba->rpa/dot_general | solution.py:74
  91.1 1.7 fusion.52
  92.8 2.9 %fusion.26 = f32[4,256,768]{1,2,0:T(8,128)S(1)} fusion(f32[256,4,256]{2,0,1:T(8,128)S(1)} %fusion.20, f32[256,2048]{1,0:T(8,128)} %slice_dynamic-update-slice_fusion.1, s32[]{:T(128)S(6)} %add.326), kind=kOutput, calls=%fused_computation.47 | convolution fusion | flops 1207959552 | bytes 4980740 | tf_op jit(solution)/shard_map/rc,rpa->pca/dot_general | solution.py:82
  95.7 0.7 fusion.36
  96.4 0.7 fusion.34
  97.7 0.9 copy-done.3
  98.6 0.9 fusion.2
  99.5 0.9 fusion.51
  100.3 0.7 fusion.39
  101.0 0.7 fusion.37
  102.3 0.8 fusion.11
  103.1 1.5 fusion.23
  104.7 1.8 %fusion.15 = f32[256,4,256]{2,0,1:T(8,128)S(1)} fusion(f32[256,4,256]{2,0,1:T(8,128)S(1)} %fusion.43, f32[256,4,256]{2,0,1:T(8,128)S(1)} %fusion.44, f32[256,4,256]{2,0,1:T(8,128)S(1)} %fusion.45, f32[4,256,1024]{2,1,0:T(8,128)S(1)} %copy-done.3, s32[]{:T(128)S(6)} %select_n.83, f32[256,256]{1,0:T(8,128)S(1)} %get-tuple-element.14, f32[4]{0:T(128)S(1)} %fusion.64, ...), kind=kOutput, calls=%fused_computation.25 | convolution fusion | flops 403963904 | bytes 5767684 | tf_op jit(solution)/shard_map/rb,pba->rpa/dot_general | solution.py:74
  106.4 2.6 %fusion.24 = f32[4,256,768]{1,2,0:T(8,128)S(1)} fusion(f32[256,4,256]{2,0,1:T(8,128)S(1)} %fusion.15, f32[264,1024]{1,0:T(8,128)} %collective-permute-done.4), kind=kOutput, calls=%fused_computation.43 | convolution fusion | flops 1207959552 | bytes 4980736 | tf_op jit(solution)/shard_map/rc,rpa->pca/dot_general | solution.py:82
  109.1 1.8 %fusion.18 = f32[256,4,256]{2,0,1:T(8,128)S(1)} fusion(f32[256,4,256]{2,0,1:T(8,128)S(1)} %fusion.46, f32[256,4,256]{2,0,1:T(8,128)S(1)} %fusion.47, f32[256,4,256]{2,0,1:T(8,128)S(1)} %fusion.48, f32[4,256,1024]{2,1,0:T(8,128)S(1)} %copy-done.3, s32[]{:T(128)S(6)} %select_n.83, f32[256,256]{1,0:T(8,128)S(1)} %get-tuple-element.13, f32[4]{0:T(128)S(1)} %fusion.64, ...), kind=kOutput, calls=%fused_computation.30 | convolution fusion | flops 403963904 | bytes 5767684 | tf_op jit(solution)/shard_map/rb,pba->rpa/dot_general | solution.py:74
  110.9 2.6 %fusion.25 = f32[4,256,768]{1,2,0:T(8,128)S(1)} fusion(f32[256,4,256]{2,0,1:T(8,128)S(1)} %fusion.18, f32[264,1024]{1,0:T(8,128)} %collective-permute-done.3), kind=kOutput, calls=%fused_computation.45 | convolution fusion | flops 1207959552 | bytes 4980736 | tf_op jit(solution)/shard_map/rc,rpa->pca/dot_general | solution.py:82
  113.6 0.9 fusion.8
  114.5 1.5 fusion.22
  116.0 2.9 %add_bitcast_fusion = f32[4,768,256]{2,1,0:T(8,128)S(1)} fusion(f32[4,256,768]{1,2,0:T(8,128)S(1)} %fusion.22, f32[4,256,768]{1,2,0:T(8,128)S(1)} %fusion.23, f32[4,256,768]{1,2,0:T(8,128)S(1)} %fusion.24, f32[4,256,768]{1,2,0:T(8,128)S(1)} %fusion.26, f32[4,256,768]{1,2,0:T(8,128)S(1)} %fusion.25, f32[256,4,256]{2,0,1:T(8,128)S(1)} %fusion.2, ...), kind=kOutput, calls=%fused_computation.3 | convolution fusion | flops 1211891712 | bytes 20709376 | tf_op jit(solution)/shard_map/rc,rpa->pca/dot_general | solution.py:82
  119.1 0.9 collective-permute-start.11
  120.0 1.5 collective-permute-start.10
  121.5 2.3 %collective-permute-start.9 = (f32[4,256,256]{2,1,0:T(8,128)S(1)}, f32[4,256,256]{2,1,0:T(8,128)S(1)}, u32[]{:S(2)}, u32[]{:S(2)}) collective-permute-start(f32[4,256,256]{2,1,0:T(8,128)S(1)} %get-tuple-element.11), channel_id=1, source_target_pairs={{0,3},{1,0},{2,1},{3,2},{4,7},{5,4},{6,5},{7,6},{8,11},{9,8},{10,9... | collective-permute-start | bytes 3145736 | tf_op jit(solution)/shard_map/ppermute | solution.py:91
  123.9 1.6 convolution_add_fusion.6
  126.1 1.7 fusion.12
  128.3 0.7 fusion.5
  129.0 39.5 %collective-permute-done.9 = f32[4,256,256]{2,1,0:T(8,128)S(1)} collective-permute-done((f32[4,256,256]{2,1,0:T(8,128)S(1)}, f32[4,256,256]{2,1,0:T(8,128)S(1)}, u32[]{:S(2)}, u32[]{:S(2)}) %collective-permute-start.9) | collective-permute-done | bytes 1048608 | tf_op jit(solution)/shard_map/ppermute | solution.py:91
  168.9 2.0 %copy-done.5 = f32[4,256,1024]{2,1,0:T(8,128)} copy-done((f32[4,256,1024]{2,1,0:T(8,128)}, f32[4,256,1024]{2,1,0:T(8,128)S(1)}, u32[]{:S(2)}) %copy-start.5) | copy-done | bytes 4194328
  170.9 1.0 constant_dynamic-update-slice_fusion
  (59 shorter events, 5.1 us)
Async XLA Ops:
  0.0 21.4 %copy-start = (f32[256]{0:T(256)S(1)}, f32[256]{0:T(256)}, u32[]{:S(2)}) copy-start(f32[256]{0:T(256)} %param.12) | copy-start | bytes 3076
  0.0 7.7 %copy-start.7 = (s32[256]{0:T(256)S(1)}, s32[256]{0:T(256)}, u32[]{:S(2)}) copy-start(s32[256]{0:T(256)} %param.10) | copy-start | bytes 3076
  0.0 7.7 %copy-start.4 = (f32[256,1024]{1,0:T(8,128)S(1)}, f32[256,1024]{1,0:T(8,128)}, u32[]{:S(2)}) copy-start(f32[256,1024]{1,0:T(8,128)} %param.9) | copy-start | bytes 3145732
  3.7 52.0 %collective-permute-start = (f32[4,256,256]{2,1,0:T(8,128)}, f32[4,256,256]{2,1,0:T(8,128)S(1)}, u32[]{:S(2)}, u32[]{:S(2)}) collective-permute-start(f32[4,256,256]{2,1,0:T(8,128)} %get-tuple-element.6), channel_id=1, source_target_pairs={{0,1},{1,2},{2,3},{3,0},{4,5},{5,6},{6,7},{7,4},{8,9},{9,10},{10,1... | collective-permute-start | bytes 3145736 | tf_op jit(solution)/shard_map/ppermute | solution.py:55
  6.7 47.0 %collective-permute-start.2 = (f32[4,256,256]{2,1,0:T(8,128)}, f32[4,256,256]{2,1,0:T(8,128)S(1)}, u32[]{:S(2)}, u32[]{:S(2)}) collective-permute-start(f32[4,256,256]{2,1,0:T(8,128)} %get-tuple-element.7), channel_id=1, source_target_pairs={{0,3},{1,0},{2,1},{3,2},{4,7},{5,4},{6,5},{7,6},{8,11},{9,8},{10,9... | collective-permute-start | bytes 3145736 | tf_op jit(solution)/shard_map/ppermute | solution.py:55
  7.7 5.8 %copy-start.2 = (f32[1024]{0:T(1024)S(1)}, f32[1024]{0:T(1024)}, u32[]{:S(2)}) copy-start(f32[1024]{0:T(1024)} %param.13) | copy-start | bytes 12292
  14.9 6.5 %copy-start.8 = (s32[4,2]{0,1:T(2,128)S(1)}, s32[4,2]{0,1:T(2,128)}, u32[]{:S(2)}) copy-start(s32[4,2]{0,1:T(2,128)} %param.11) | copy-start | bytes 100
  17.6 39.8 %collective-permute-start.5 = (f32[264,1024]{1,0:T(8,128)}, f32[264,1024]{1,0:T(8,128)S(1)}, u32[]{:S(2)}, u32[]{:S(2)}) collective-permute-start(f32[264,1024]{1,0:T(8,128)} %pad_maximum_fusion), channel_id=1, source_target_pairs={{24,0},{0,8},{8,16},{16,24},{12,4},{20,12},{28,20},{4,28},{25,1},{... | collective-permute-start | bytes 3244040 | tf_op jit(solution)/shard_map/ppermute | solution.py:23
  19.7 47.8 %collective-permute-start.4 = (f32[264,1024]{1,0:T(8,128)}, f32[264,1024]{1,0:T(8,128)}, u32[]{:S(2)}, u32[]{:S(2)}) collective-permute-start(f32[264,1024]{1,0:T(8,128)} %pad_maximum_fusion), channel_id=1, source_target_pairs={{28,0},{4,8},{12,16},{20,24},{8,4},{16,12},{24,20},{0,28},{29,1},{... | collective-permute-start | bytes 3244040 | tf_op jit(solution)/shard_map/ppermute | solution.py:23
  20.7 47.5 %collective-permute-start.3 = (f32[264,1024]{1,0:T(8,128)}, f32[264,1024]{1,0:T(8,128)}, u32[]{:S(2)}, u32[]{:S(2)}) collective-permute-start(f32[264,1024]{1,0:T(8,128)} %pad_maximum_fusion), channel_id=1, source_target_pairs={{0,4},{8,12},{16,20},{24,28},{4,0},{12,8},{20,16},{28,24},{1,5},{9... | collective-permute-start | bytes 3244040 | tf_op jit(solution)/shard_map/ppermute | solution.py:23
  25.8 30.0 %copy-start.6 = (f32[256,4,256]{2,0,1:T(8,128)S(1)}, f32[256,4,256]{2,0,1:T(8,128)}, u32[]{:S(2)}) copy-start(f32[256,4,256]{2,0,1:T(8,128)} %fusion.32) | copy-start | bytes 3145732
  53.7 31.3 %collective-permute-start.1 = (f32[4,256,256]{2,1,0:T(8,128)}, f32[4,256,256]{2,1,0:T(8,128)S(1)}, u32[]{:S(2)}, u32[]{:S(2)}) collective-permute-start(f32[4,256,256]{2,1,0:T(8,128)} %get-tuple-element.8), channel_id=1, source_target_pairs={{0,2},{1,3},{2,0},{3,1},{4,6},{5,7},{6,4},{7,5},{8,10},{9,11},{10,... | collective-permute-start | bytes 3145736 | tf_op jit(solution)/shard_map/ppermute | solution.py:55
  69.0 19.7 %collective-permute-start.7 = (f32[264,1024]{1,0:T(8,128)S(1)}, f32[264,1024]{1,0:T(8,128)S(1)}, u32[]{:S(2)}, u32[]{:S(2)}) collective-permute-start(f32[264,1024]{1,0:T(8,128)S(1)} %collective-permute-done.5), channel_id=1, source_target_pairs={{4,0},{12,8},{20,16},{28,24},{5,1},{13,9},{21,17},{29,25},{6,2},{1... | collective-permute-start | bytes 3244040 | tf_op jit(solution)/shard_map/ppermute | solution.py:23
  70.3 18.4 %collective-permute-start.8 = (f32[264,1024]{1,0:T(8,128)}, f32[264,1024]{1,0:T(8,128)S(1)}, u32[]{:S(2)}, u32[]{:S(2)}) collective-permute-start(f32[264,1024]{1,0:T(8,128)} %collective-permute-done.4), channel_id=1, source_target_pairs={{12,4},{20,12},{28,20},{4,28},{13,5},{21,13},{29,21},{5,29},{14,6}... | collective-permute-start | bytes 3244040 | tf_op jit(solution)/shard_map/ppermute | solution.py:23
  71.2 17.7 %collective-permute-start.6 = (f32[264,1024]{1,0:T(8,128)}, f32[264,1024]{1,0:T(8,128)S(1)}, u32[]{:S(2)}, u32[]{:S(2)}) collective-permute-start(f32[264,1024]{1,0:T(8,128)} %collective-permute-done.4), channel_id=1, source_target_pairs={{0,4},{8,12},{16,20},{24,28},{4,0},{12,8},{20,16},{28,24},{1,5},{9... | collective-permute-start | bytes 3244040 | tf_op jit(solution)/shard_map/ppermute | solution.py:23
  96.4 2.2 %copy-start.3 = (f32[4,256,1024]{2,1,0:T(8,128)S(1)}, f32[4,256,1024]{2,1,0:T(8,128)}, u32[]{:S(2)}) copy-start(f32[4,256,1024]{2,1,0:T(8,128)} %param.8) | copy-start | bytes 12582916
  119.1 49.7 %collective-permute-start.11 = (f32[4,256,256]{2,1,0:T(8,128)S(1)}, f32[4,256,256]{2,1,0:T(8,128)S(1)}, u32[]{:S(2)}, u32[]{:S(2)}) collective-permute-start(f32[4,256,256]{2,1,0:T(8,128)S(1)} %get-tuple-element.9), channel_id=1, source_target_pairs={{0,1},{1,2},{2,3},{3,0},{4,5},{5,6},{6,7},{7,4},{8,9},{9,10},{10,1... | collective-permute-start | bytes 3145736 | tf_op jit(solution)/shard_map/ppermute | solution.py:91
  120.0 48.7 %collective-permute-start.10 = (f32[4,256,256]{2,1,0:T(8,128)S(1)}, f32[4,256,256]{2,1,0:T(8,128)S(1)}, u32[]{:S(2)}, u32[]{:S(2)}) collective-permute-start(f32[4,256,256]{2,1,0:T(8,128)S(1)} %get-tuple-element.10), channel_id=1, source_target_pairs={{0,2},{1,3},{2,0},{3,1},{4,6},{5,7},{6,4},{7,5},{8,10},{9,11},{10,... | collective-permute-start | bytes 3145736 | tf_op jit(solution)/shard_map/ppermute | solution.py:91
  121.5 47.0 %collective-permute-start.9 = (f32[4,256,256]{2,1,0:T(8,128)S(1)}, f32[4,256,256]{2,1,0:T(8,128)S(1)}, u32[]{:S(2)}, u32[]{:S(2)}) collective-permute-start(f32[4,256,256]{2,1,0:T(8,128)S(1)} %get-tuple-element.11), channel_id=1, source_target_pairs={{0,3},{1,0},{2,1},{3,2},{4,7},{5,4},{6,5},{7,6},{8,11},{9,8},{10,9... | collective-permute-start | bytes 3145736 | tf_op jit(solution)/shard_map/ppermute | solution.py:91
  168.5 3.4 %copy-start.1 = (f32[256]{0:T(256)S(1)}, f32[256]{0:T(256)}, u32[]{:S(2)}) copy-start(f32[256]{0:T(256)} %param.12) | copy-start | bytes 3076
  168.8 2.0 %copy-start.5 = (f32[4,256,1024]{2,1,0:T(8,128)}, f32[4,256,1024]{2,1,0:T(8,128)S(1)}, u32[]{:S(2)}) copy-start(f32[4,256,1024]{2,1,0:T(8,128)S(1)} %constant_dynamic-update-slice_fusion.1) | copy-start | bytes 12582916
